TPU v7x, 128 devices: a whole 4x4x4 slice. The times are simulated.
128 devices in a mesh: req: 16 (over y, z), mlp: 8 (over x, core).
Axes of the slice: x: 4, y: 4, z: 4, core: 2. Of those that a mesh axis runs over, the one named last changes fastest.
Arguments:
- resid: bfloat16 [2176, 5120], P('req', 'mlp'), may hold values from -180 to 180
- queries: bfloat16 [2176, 5120], P('req', 'mlp'), may hold values from -200 to 200
- new_keys: bfloat16 [2176, 1024], P('req', 'mlp'), may hold values from -6 to 6
- new_values: bfloat16 [2176, 1024], P('req', 'mlp'), may hold values from -6 to 6
- cache_keys: bfloat16 [48, 4096, 1024], P('req', None, 'mlp'), may hold values from -6 to 6
- cache_values: bfloat16 [48, 4096, 1024], P('req', None, 'mlp'), may hold values from -6 to 6
- context_keys: bfloat16 [5, 1024, 1024], P(None, 'req', 'mlp'), may hold values from -6 to 6
- context_values: bfloat16 [5, 1024, 1024], P(None, 'req', 'mlp'), may hold values from -6 to 6
- cache_lengths: int32 [48], P('req'), may hold values from 1 to 4096, 49152 in all
- group_ids: int32 [48], P('req'), may hold values from 0 to 3
- prefix_lengths: int32 [4], replicated, may hold values from 1 to 1024, 2048 in all
- prompt_start: int32 [1], replicated, may hold values from 1 to 1023
- out_weight: bfloat16 [5120, 5120], P('mlp'), may hold values from -1.25 to 1.25
- norm_gain: float32 [5120], P('mlp'), may hold values from 0.5 to 1.5
- gate_weight: bfloat16 [5120, 27648], P(None, ('req', 'mlp')), may hold values from -0.078125 to 0.078125
- up_weight: bfloat16 [5120, 27648], P(None, ('req', 'mlp')), may hold values from -0.078125 to 0.078125
- down_weight: bfloat16 [27648, 5120], P('req', 'mlp'), may hold values from -0.109375 to 0.109375
Outputs:
- out: bfloat16 [2176, 5120], P('req', 'mlp')
Inputs may be any that keep to these rules, and one draw needn't show every extreme that they name: `cache_lengths`: one decode request has 4096 valid positions. `prefix_lengths`: one group's prompt has 1024 positions.
All inputs are finite; a program needn't handle non-finite values. No bound on the sum of `cache_lengths` on one device may be relied on, other than what follows from the above.
Results may differ from a plain program's by a relative error of at most 0.019.
Values may be sent and summed in bfloat16 or wider, within the bound.
No kernel may reach another device: no remote copies, remote signals or barrier semaphores. Data moves between devices by JAX's collectives and lax.ppermute only.
A program may use at most 128 MiB of HBM per device.

v0:
```python
import math

import jax
import jax.numpy as jnp
from jax import lax
from jax.sharding import PartitionSpec as P

D = 5120
HQ = 40
KV = 8
HD = 128


NEGATIVE = -1e30


def absorb(carried, scores, allowed, values, pattern):
    running, totals, summed = carried
    scores = jnp.where(allowed, scores, -jnp.inf)
    highest = jnp.maximum(running, jnp.max(scores, axis=-1))
    exponent = jnp.where(allowed, jnp.exp(scores - highest[..., None]), 0.0)
    fading = jnp.exp(running - highest)
    weights = exponent.astype(jnp.bfloat16)
    summed = summed * fading[..., None] + jnp.einsum(
        pattern, weights, values, preferred_element_type=jnp.float32
    )
    totals = totals * fading + jnp.sum(exponent, axis=-1)
    return (highest, totals, summed)


def per_device(
    resid,
    queries,
    new_keys,
    new_values,
    cache_keys,
    cache_values,
    context_keys,
    context_values,
    cache_lengths,
    group_ids,
    prefix_lengths,
    prompt_start,
    out_weight,
    norm_gain,
    gate_weight,
    up_weight,
    down_weight,
):
    rows_here = queries.shape[0]
    decode_count = cache_keys.shape[0]
    prompt_count = rows_here - decode_count
    heads_kv = new_keys.shape[1] // HD
    group_size = HQ // KV
    scaling = 1.0 / math.sqrt(HD)
    cache_span = cache_keys.shape[1]
    context_count = context_keys.shape[0]
    query_rows = queries.reshape(rows_here, heads_kv, group_size, HD)
    query_decode = query_rows[:decode_count]
    query_prompt = query_rows[decode_count:]
    key_rows = new_keys.reshape(rows_here, heads_kv, HD)
    value_rows = new_values.reshape(rows_here, heads_kv, HD)

    def fresh_state(row_count):
        return (
            jnp.full((row_count, heads_kv, group_size), NEGATIVE, jnp.float32),
            jnp.zeros((row_count, heads_kv, group_size), jnp.float32),
            jnp.zeros((row_count, heads_kv, group_size, HD), jnp.float32),
        )

    past_keys = cache_keys.reshape(decode_count, cache_span, heads_kv, HD)
    past_values = cache_values.reshape(decode_count, cache_span, heads_kv, HD)
    scores = (
        jnp.einsum("ikgd,ickd->ikgc", query_decode, past_keys, preferred_element_type=jnp.float32)
        * scaling
    )
    usable = (jnp.arange(cache_span)[None, :] < cache_lengths[:, None])[:, None, None, :]
    decode_state = absorb(fresh_state(decode_count), scores, usable, past_values, "ikgc,ickd->ikgd")
    own_scores = (
        jnp.einsum(
            "ikgd,ikd->ikg",
            query_decode,
            key_rows[:decode_count],
            preferred_element_type=jnp.float32,
        )[..., None]
        * scaling
    )
    decode_state = absorb(
        decode_state,
        own_scores,
        jnp.ones(own_scores.shape, dtype=bool),
        value_rows[:decode_count][:, None],
        "ikgc,ickd->ikgd",
    )
    prompt_length = prompt_start[0]
    prefix_here = prefix_lengths[group_ids]
    state_decode = decode_state
    state_prompt = fresh_state(prompt_count)
    key_block = lax.all_gather(context_keys, "req", axis=1, tiled=True)
    value_block = lax.all_gather(context_values, "req", axis=1, tiled=True)
    extent = key_block.shape[1]
    positions = jnp.arange(extent)
    key_split = key_block.reshape(context_count, extent, heads_kv, HD)
    value_split = value_block.reshape(context_count, extent, heads_kv, HD)
    chosen_keys = key_split[group_ids]
    chosen_values = value_split[group_ids]
    block_scores = (
        jnp.einsum("ikgd,ickd->ikgc", query_decode, chosen_keys, preferred_element_type=jnp.float32)
        * scaling
    )
    block_usable = (positions[None, :] < prefix_here[:, None])[:, None, None, :]
    state_decode = absorb(
        state_decode, block_scores, block_usable, chosen_values, "ikgc,ickd->ikgd"
    )
    block_scores = (
        jnp.einsum(
            "jkgd,ckd->jkgc",
            query_prompt,
            key_split[context_count - 1],
            preferred_element_type=jnp.float32,
        )
        * scaling
    )
    block_usable = (positions < prompt_length)[None, None, None, :]
    state_prompt = absorb(
        state_prompt, block_scores, block_usable, value_split[context_count - 1], "jkgc,ckd->jkgd"
    )
    prompt_state = state_prompt
    own_positions = lax.axis_index("req") * prompt_count + jnp.arange(prompt_count, dtype=jnp.int32)
    key_block = lax.all_gather(new_keys[decode_count:], "req", axis=0, tiled=True)
    value_block = lax.all_gather(new_values[decode_count:], "req", axis=0, tiled=True)
    extent = key_block.shape[0]
    positions = jnp.arange(extent, dtype=jnp.int32)
    block_scores = (
        jnp.einsum(
            "jkgd,ckd->jkgc",
            query_prompt,
            key_block.reshape(extent, heads_kv, HD),
            preferred_element_type=jnp.float32,
        )
        * scaling
    )
    block_usable = (positions[None, :] <= own_positions[:, None])[:, None, None, :]
    prompt_state = absorb(
        prompt_state,
        block_scores,
        block_usable,
        value_block.reshape(extent, heads_kv, HD),
        "jkgc,ckd->jkgd",
    )

    def finish(carried):
        return (carried[2] / carried[1][..., None]).astype(jnp.bfloat16)

    attended = jnp.concatenate([finish(state_decode), finish(prompt_state)], 0).reshape(
        rows_here, heads_kv * group_size * HD
    )
    head_partial = jnp.dot(attended, out_weight, preferred_element_type=jnp.float32)
    projected = lax.psum_scatter(
        head_partial.astype(jnp.bfloat16), "mlp", scatter_dimension=1, tiled=True
    ).astype(jnp.float32)
    mixed = (resid.astype(jnp.float32) + projected).astype(jnp.bfloat16)
    mixed_wide = mixed.astype(jnp.float32)
    square_total = lax.psum(jnp.sum(mixed_wide * mixed_wide, axis=1), "mlp")
    normed = (
        mixed_wide * lax.rsqrt(square_total / D + 1e-06)[:, None] * norm_gain[None, :]
    ).astype(jnp.bfloat16)
    all_features = lax.all_gather(normed, "mlp", axis=1, tiled=True)
    block_rows = lax.all_gather(all_features, "req", axis=0, tiled=True)
    gate_proj = jnp.dot(block_rows, gate_weight, preferred_element_type=jnp.float32)
    up_proj = jnp.dot(block_rows, up_weight, preferred_element_type=jnp.float32)
    hidden = (jax.nn.silu(gate_proj) * up_proj).astype(jnp.bfloat16)
    hidden_block = lax.all_gather(hidden, "mlp", axis=1, tiled=True)
    feed = lax.psum_scatter(
        jnp.dot(hidden_block, down_weight, preferred_element_type=jnp.float32).astype(jnp.bfloat16),
        "req",
        scatter_dimension=0,
        tiled=True,
    ).astype(jnp.float32)
    return (mixed_wide + feed).astype(jnp.bfloat16)


def solution(mesh):
    return jax.shard_map(
        per_device,
        mesh=mesh,
        in_specs=(
            P("req", "mlp"),
            P("req", "mlp"),
            P("req", "mlp"),
            P("req", "mlp"),
            P("req", None, "mlp"),
            P("req", None, "mlp"),
            P(None, "req", "mlp"),
            P(None, "req", "mlp"),
            P("req"),
            P("req"),
            P(),
            P(),
            P("mlp", None),
            P("mlp"),
            P(None, ("req", "mlp")),
            P(None, ("req", "mlp")),
            P("req", "mlp"),
        ),
        out_specs=P("req", "mlp"),
        check_vma=False,
    )
```

profile of v0, /device:TPU:0, one launch (start us, length us, event | category | flops | bytes accessed | tf_op | source)
XLA Modules:
  0.0 504.8 jit_solution(4887309320521932131)
XLA Ops:
  9.5 1.2 slice_convert_fusion
  14.8 28.0 %all-gather.1 = bf16[16,133,128]{2,1,0:T(8,128)(2,1)} all-gather(bf16[1,133,128]{2,1,0:T(8,128)(2,1)S(1)} %slice_bitcast_fusion.4), channel_id=1, replica_groups=mesh['req'=16,'mlp'=8] {'req'}, dimensions={0}, use_global_device_ids=true | all-gather | bytes 578816 | tf_op jit(solution)/shard_map/all_gather | solution.py:131
  42.8 25.3 %all-gather = bf16[16,133,128]{2,1,0:T(8,128)(2,1)} all-gather(bf16[1,133,128]{2,1,0:T(8,128)(2,1)S(1)} %slice_bitcast_fusion.5), channel_id=1, replica_groups=mesh['req'=16,'mlp'=8] {'req'}, dimensions={0}, use_global_device_ids=true | all-gather | bytes 578816 | tf_op jit(solution)/shard_map/all_gather | solution.py:130
  69.4 1.0 slice.34
  70.4 0.9 reshape.360
  71.3 2.1 reshape.408
  73.4 2.0 reshape.407
  77.5 2.2 fusion.88
  79.7 0.9 iota_compare_fusion
  80.7 4.7 fusion.87
  85.3 2.1 gather_fusion.1
  88.1 12.7 %all-gather.10.cloned.1.call-done = bf16[5,1024,128]{2,1,0:T(8,128)(2,1)} async-done(((bf16[5,64,128]{2,1,0:T(8,128)(2,1)}), bf16[5,1024,128]{2,1,0:T(8,128)(2,1)}) %all-gather.10.cloned.1.call-update) | async-done | bytes 1310736 | tf_op jit(solution)/shard_map/all_gather | solution.py:100
  100.8 2.1 gather_fusion.2
  103.5 2.6 fusion.42
  106.2 1.6 bitcast_reduce_fusion
  107.8 1.4 fusion
  109.3 0.8 fusion.12
  110.2 2.0 fusion.31
  112.2 1.5 fusion.49
  114.0 1.3 convolution_convert_fusion
  115.2 2.6 copy.26
  117.9 34.2 %reduce-scatter.7.cloned.1.call-done = bf16[640,136]{1,0:T(8,128)(2,1)} async-done(((bf16[5120,136]{1,0:T(8,128)(2,1)}), bf16[640,136]{1,0:T(8,128)(2,1)}) %reduce-scatter.7.cloned.1.call-update) | async-done | bytes 174096
  152.2 1.1 copy.27
  153.4 12.8 %psum.7 = f32[136]{0:T(256)S(1)} all-reduce(f32[136]{0:T(256)S(1)} %fusion.52), channel_id=1, replica_groups=mesh['req'=16,'mlp'=8] {'mlp'}, use_global_device_ids=true, to_apply=%region_10.11 | all-reduce | flops 136 | bytes 1088 | tf_op jit(solution)/shard_map/psum | solution.py:164
  167.1 23.1 %all-gather.12.cloned.1.call-done = bf16[136,5120]{1,0:T(8,128)(2,1)} async-done(((bf16[136,640]{1,0:T(8,128)(2,1)}), bf16[136,5120]{1,0:T(8,128)(2,1)}) %all-gather.12.cloned.1.call-update) | async-done | bytes 1392656 | tf_op jit(solution)/shard_map/all_gather | solution.py:168
  190.4 141.3 %all-gather.14.cloned.1.call-done = bf16[2176,5120]{1,0:T(8,128)(2,1)} async-done(((bf16[136,5120]{1,0:T(8,128)(2,1)}), bf16[2176,5120]{1,0:T(8,128)(2,1)}) %all-gather.14.cloned.1.call-update) | async-done | bytes 22282256 | tf_op jit(solution)/shard_map/all_gather | solution.py:169
  331.8 13.1 %fusion.90 = f32[2176,216]{0,1:T(8,128)S(1)} fusion(bf16[2176,5120]{1,0:T(8,128)(2,1)} %all-gather.14.cloned.1.call-done, bf16[5120,216]{0,1:T(8,128)(2,1)} %param.31), kind=kOutput, calls=%fused_computation.120 | convolution fusion | flops 4812963840 | bytes 26374144 | tf_op jit(solution)/shard_map/dot_general | solution.py:170
  344.9 12.7 %fusion.3 = bf16[2176,216]{0,1:T(8,128)(2,1)} fusion(bf16[2176,5120]{1,0:T(8,128)(2,1)} %all-gather.14.cloned.1.call-done, bf16[5120,216]{0,1:T(8,128)(2,1)S(1)} %copy-done.16, f32[2176,216]{0,1:T(8,128)S(1)} %fusion.90), kind=kOutput, calls=%fused_computation.12 | convolution fusion | flops 4815783936 | bytes 27314176 | tf_op jit(solution)/shard_map/dot_general | solution.py:171
  357.6 45.6 %all-gather.16.cloned.1.call-done = bf16[2176,1728]{0,1:T(8,128)(2,1)} async-done(((bf16[2176,216]{0,1:T(8,128)(2,1)}), bf16[2176,1728]{0,1:T(8,128)(2,1)}) %all-gather.16.cloned.1.call-update) | async-done | bytes 7520272 | tf_op jit(solution)/shard_map/all_gather | solution.py:173
  403.3 10.9 %convolution_convert_fusion.1 = bf16[2176,640]{1,0:T(8,128)(2,1)} fusion(bf16[2176,1728]{0,1:T(8,128)(2,1)} %all-gather.16.cloned.1.call-done, bf16[1728,640]{1,0:T(8,128)(2,1)} %param.33), kind=kOutput, calls=%fused_computation.8 | convolution fusion | flops 4814356480 | bytes 12517376 | tf_op jit(solution)/shard_map/dot_general | solution.py:175
  414.2 82.0 %reduce-scatter.9.cloned.1.call-done = bf16[136,640]{1,0:T(8,128)(2,1)} async-done(((bf16[2176,640]{1,0:T(8,128)(2,1)}), bf16[136,640]{1,0:T(8,128)(2,1)}) %reduce-scatter.9.cloned.1.call-update) | async-done | bytes 174096
  496.2 1.7 fusion.55
  (83 shorter events, 12.4 us)
Async XLA Ops:
  6.5 70.9 %copy-start = (bf16[3,4096,128]{2,1,0:T(8,128)(2,1)S(1)}, bf16[3,4096,128]{2,1,0:T(8,128)(2,1)}, u32[]{:S(2)}) copy-start(bf16[3,4096,128]{2,1,0:T(8,128)(2,1)} %param.21) | copy-start | bytes 9437188
  6.5 68.9 %copy-start.2 = (s32[4]{0:T(128)S(1)}, s32[4]{0:T(128)}, u32[]{:S(2)}) copy-start(s32[4]{0:T(128)} %param.27) | copy-start | bytes 52
  6.5 78.8 %all-gather.8.cloned.1.call-start = ((), (), s32[]{:S(2)}) async-start(), calls=%async_computation.2 | async-start | bytes 1392640 | tf_op jit(solution)/shard_map/all_gather | solution.py:99
  7.3 93.5 %all-gather.10.cloned.1.call-start = ((), (), s32[]{:S(2)}) async-start(), calls=%async_computation.3 | async-start | bytes 1392640 | tf_op jit(solution)/shard_map/all_gather | solution.py:100
  8.0 144.2 %reduce-scatter.7.cloned.1.call-start = ((), (), s32[]{:S(2)}) async-start(), calls=%async_computation.7 | async-start | bytes 2949120
  70.4 6.4 %copy-start.9 = (bf16[3,5,128]{2,1,0:T(8,128)(2,1)}, bf16[3,5,128]{2,1,0:T(8,128)(2,1)S(1)}, u32[]{:S(2)}) copy-start(bf16[3,5,128]{2,1,0:T(8,128)(2,1)S(1)} %reshape.354) | copy-start | bytes 11524
  76.1 4.5 copy-start.4
  80.6 6.9 %copy-start.8 = (pred[3,1024]{1,0:T(4,128)(4,1)S(1)}, pred[3,1024]{1,0:T(4,128)(4,1)}, u32[]{:S(2)}) copy-start(pred[3,1024]{1,0:T(4,128)(4,1)} %iota_compare_fusion.2) | copy-start | bytes 9220
  80.6 6.9 %copy-start.10 = (bf16[3,5,128]{2,1,0:T(8,128)(2,1)S(1)}, bf16[3,5,128]{2,1,0:T(8,128)(2,1)}, u32[]{:S(2)}) copy-start(bf16[3,5,128]{2,1,0:T(8,128)(2,1)} %copy-done.9) | copy-start | bytes 11524
  80.6 7.3 %copy-start.11 = (f32[3,5]{1,0:T(4,128)S(1)}, f32[3,5]{1,0:T(4,128)}, u32[]{:S(2)}) copy-start(f32[3,5]{1,0:T(4,128)} %get-tuple-element.22) | copy-start | bytes 184
  80.6 7.3 %copy-start.14 = (f32[3,1,5]{2,1,0:T(1,128)S(1)}, f32[3,1,5]{2,1,0:T(1,128)}, u32[]{:S(2)}) copy-start(f32[3,1,5]{2,1,0:T(1,128)} %fusion.76) | copy-start | bytes 184
  85.3 18.2 %copy-start.13 = (f32[3,128]{1,0:T(4,128)S(1)}, f32[3,128]{1,0:T(4,128)}, u32[]{:S(2)}) copy-start(f32[3,128]{1,0:T(4,128)} %slice_convert_fusion) | copy-start | bytes 4612
  102.9 3.2 copy-start.5
  102.9 3.2 copy-start.12
  103.5 4.3 copy-start.3
  110.1 2.1 copy-start.7
  110.1 3.7 slice-start
  112.2 1.8 slice-start.1
  115.2 38.1 %copy-start.6 = (bf16[136,640]{1,0:T(8,128)(2,1)S(1)}, bf16[136,640]{1,0:T(8,128)(2,1)}, u32[]{:S(2)}) copy-start(bf16[136,640]{1,0:T(8,128)(2,1)} %param.17) | copy-start | bytes 522244
  115.2 51.0 %copy-start.15 = (f32[640]{0:T(1024)S(1)}, f32[640]{0:T(1024)}, u32[]{:S(2)}) copy-start(f32[640]{0:T(1024)} %param.30) | copy-start | bytes 7684
  117.9 72.3 %all-gather.12.cloned.1.call-start = ((), (), s32[]{:S(2)}) async-start(), calls=%async_computation.4 | async-start | bytes 1566720 | tf_op jit(solution)/shard_map/all_gather | solution.py:168
  167.1 164.7 %all-gather.14.cloned.1.call-start = ((), (), s32[]{:S(2)}) async-start(), calls=%async_computation.5 | async-start | bytes 23674880 | tf_op jit(solution)/shard_map/all_gather | solution.py:169
  190.2 154.7 %copy-start.16 = (bf16[5120,216]{0,1:T(8,128)(2,1)S(1)}, bf16[5120,216]{0,1:T(8,128)(2,1)}, u32[]{:S(2)}) copy-start(bf16[5120,216]{0,1:T(8,128)(2,1)} %param.32) | copy-start | bytes 6635524
  190.2 213.1 %all-gather.16.cloned.1.call-start = ((), (), s32[]{:S(2)}) async-start(), calls=%async_computation.6 | async-start | bytes 8460288 | tf_op jit(solution)/shard_map/all_gather | solution.py:173
  357.6 138.7 %reduce-scatter.9.cloned.1.call-start = ((), (), s32[]{:S(2)}) async-start(), calls=%async_computation.8 | async-start | bytes 2959360
  403.3 94.6 %copy-start.1 = (bf16[3,4096,128]{2,1,0:T(8,128)(2,1)S(1)}, bf16[3,4096,128]{2,1,0:T(8,128)(2,1)}, u32[]{:S(2)}) copy-start(bf16[3,4096,128]{2,1,0:T(8,128)(2,1)} %param.21) | copy-start | bytes 9437188
Sparse Core Ops, SparseCore 0:
  9.5 46.3 all-gather.7
  58.1 42.6 all-gather.9
  118.0 34.1 reduce-scatter.6
  167.2 22.9 all-gather.11
  192.2 139.5 all-gather.13
  357.7 45.5 all-gather.15
  414.3 81.8 reduce-scatter.8
where the time goes:
time: 506 us; the launch traced here: 505 us
  waiting for transfers between devices  341 us (67%)
  blocking collectives  66.1 us (13%)
  matrix products  54 us (11%)
  local copies, waits for them, and re-layouts  17.9 us (4%)
  between operations  14.5 us (3%)
  other arithmetic  11.3 us (2%)
    all_gather x1, waiting for transfers between devices, per_device(): block_rows = lax.all_gather(all_features, 'req', axis=0, tiled=True)  141 us
    unnamed x9, waiting for transfers between devices  118 us
    all_gather x1, waiting for transfers between devices, per_device(): hidden_block = lax.all_gather(hidden, 'mlp', axis=1, tiled=True)  45.6 us
    all_gather x1, blocking collectives, per_device(): lax.all_gather(new_values[decode_count:], 'req', axis=0, tiled=True)  28 us
    all_gather x1, blocking collectives, per_device(): lax.all_gather(new_keys[decode_count:], 'req', axis=0, tiled=True)  25.3 us
    all_gather x1, waiting for transfers between devices, per_device(): all_features = lax.all_gather(normed, 'mlp', axis=1, tiled=True)  23.1 us
    dot_general x1, matrix products, per_device(): jnp.dot(block_rows, gate_weight, preferred_element_type=jnp.float32)  13.1 us
    psum x1, blocking collectives, per_device(): square_total = lax.psum(jnp.sum(mixed_wide * mixed_wide, axis=1), 'mlp')  12.8 us
  transfers between devices with their start and end apart: 7, of which 6 were waited for; matrix products, arithmetic and copies ran while one was open for 5% of the time, Pallas kernels for 0%

commit v1 on v0

--- a/solution.py
+++ b/solution.py
@@ -96,8 +96,33 @@
     prefix_here = prefix_lengths[group_ids]
     state_decode = decode_state
     state_prompt = fresh_state(prompt_count)
-    key_block = lax.all_gather(context_keys, "req", axis=1, tiled=True)
-    value_block = lax.all_gather(context_values, "req", axis=1, tiled=True)
+    req_count = lax.axis_size("req")
+    context_rows = context_keys.shape[1]
+    packed = jnp.concatenate(
+        [
+            context_keys.reshape(context_count * context_rows, heads_kv * HD),
+            context_values.reshape(context_count * context_rows, heads_kv * HD),
+            new_keys,
+            new_values,
+        ],
+        0,
+    )
+    gathered = lax.all_gather(packed, "req", axis=0, tiled=False)
+    context_span = context_count * context_rows
+
+    def context_of(offset):
+        piece = gathered[:, offset : offset + context_span]
+        piece = piece.reshape(req_count, context_count, context_rows, heads_kv * HD)
+        return jnp.transpose(piece, (1, 0, 2, 3)).reshape(
+            context_count, req_count * context_rows, heads_kv * HD
+        )
+
+    def prompt_of(offset):
+        piece = gathered[:, offset : offset + rows_here][:, decode_count:]
+        return piece.reshape(req_count * prompt_count, heads_kv * HD)
+
+    key_block = context_of(0)
+    value_block = context_of(context_span)
     extent = key_block.shape[1]
     positions = jnp.arange(extent)
     key_split = key_block.reshape(context_count, extent, heads_kv, HD)
@@ -127,8 +152,8 @@
     )
     prompt_state = state_prompt
     own_positions = lax.axis_index("req") * prompt_count + jnp.arange(prompt_count, dtype=jnp.int32)
-    key_block = lax.all_gather(new_keys[decode_count:], "req", axis=0, tiled=True)
-    value_block = lax.all_gather(new_values[decode_count:], "req", axis=0, tiled=True)
+    key_block = prompt_of(2 * context_span)
+    value_block = prompt_of(2 * context_span + rows_here)
     extent = key_block.shape[0]
     positions = jnp.arange(extent, dtype=jnp.int32)
     block_scores = (
@@ -155,28 +180,45 @@
     attended = jnp.concatenate([finish(state_decode), finish(prompt_state)], 0).reshape(
         rows_here, heads_kv * group_size * HD
     )
+    mlp_count = lax.axis_size("mlp")
     head_partial = jnp.dot(attended, out_weight, preferred_element_type=jnp.float32)
-    projected = lax.psum_scatter(
-        head_partial.astype(jnp.bfloat16), "mlp", scatter_dimension=1, tiled=True
-    ).astype(jnp.float32)
+    pieces = lax.all_to_all(
+        head_partial.astype(jnp.bfloat16), "mlp", 1, 0, tiled=True
+    )
+    projected = jnp.sum(
+        pieces.reshape(mlp_count, rows_here, -1).astype(jnp.float32), axis=0
+    )
     mixed = (resid.astype(jnp.float32) + projected).astype(jnp.bfloat16)
     mixed_wide = mixed.astype(jnp.float32)
-    square_total = lax.psum(jnp.sum(mixed_wide * mixed_wide, axis=1), "mlp")
+    mixed_rows = lax.all_gather(mixed, "mlp", axis=1, tiled=True).astype(jnp.float32)
+    square_total = jnp.sum(mixed_rows * mixed_rows, axis=1)
+    half = D // 2
+    side = lax.axis_index("mlp") % 2
+    own_half = lax.dynamic_slice_in_dim(mixed_rows, side * half, half, axis=1)
+    own_gain = lax.dynamic_slice_in_dim(norm_gain, side * half, half, axis=0)
     normed = (
-        mixed_wide * lax.rsqrt(square_total / D + 1e-06)[:, None] * norm_gain[None, :]
+        own_half * lax.rsqrt(square_total / D + 1e-06)[:, None] * own_gain[None, :]
     ).astype(jnp.bfloat16)
-    all_features = lax.all_gather(normed, "mlp", axis=1, tiled=True)
-    block_rows = lax.all_gather(all_features, "req", axis=0, tiled=True)
-    gate_proj = jnp.dot(block_rows, gate_weight, preferred_element_type=jnp.float32)
-    up_proj = jnp.dot(block_rows, up_weight, preferred_element_type=jnp.float32)
+    near_rows = lax.all_gather(normed, "req", axis=0, tiled=True)
+    pairs = [(i, i ^ 1) for i in range(mlp_count)]
+    far_rows = lax.ppermute(near_rows, "mlp", pairs)
+
+    def project(weight):
+        near_weight = lax.dynamic_slice_in_dim(weight, side * half, half, axis=0)
+        far_weight = lax.dynamic_slice_in_dim(weight, (1 - side) * half, half, axis=0)
+        return jnp.dot(near_rows, near_weight, preferred_element_type=jnp.float32) + jnp.dot(
+            far_rows, far_weight, preferred_element_type=jnp.float32
+        )
+
+    gate_proj = project(gate_weight)
+    up_proj = project(up_weight)
     hidden = (jax.nn.silu(gate_proj) * up_proj).astype(jnp.bfloat16)
     hidden_block = lax.all_gather(hidden, "mlp", axis=1, tiled=True)
-    feed = lax.psum_scatter(
-        jnp.dot(hidden_block, down_weight, preferred_element_type=jnp.float32).astype(jnp.bfloat16),
-        "req",
-        scatter_dimension=0,
-        tiled=True,
-    ).astype(jnp.float32)
+    down_partial = jnp.dot(hidden_block, down_weight, preferred_element_type=jnp.float32)
+    req_pieces = lax.all_to_all(down_partial.astype(jnp.bfloat16), "req", 0, 0, tiled=True)
+    feed = jnp.sum(
+        req_pieces.reshape(req_count, rows_here, -1).astype(jnp.float32), axis=0
+    )
     return (mixed_wide + feed).astype(jnp.bfloat16)
 
 
@@ -198,7 +240,7 @@
             P(),
             P(),
             P("mlp", None),
-            P("mlp"),
+            P(),
             P(None, ("req", "mlp")),
             P(None, ("req", "mlp")),
             P("req", "mlp"),

time: 506 us -> 364 us (0.72)
  waiting for transfers between devices: 341 us -> 184 us
  blocking collectives: 66.1 us -> 79.6 us
    unnamed x9 -> x4, waiting for transfers between devices: 118 us -> 0.07 us
    all_to_all x0 -> x2, blocking collectives: none -> 66.8 us  [the longest x1 43 us: per_device(): lax.all_to_all(down_partial.astype(jnp.bfloat16), 'req', 0, 0, tiled=True)]
    all_gather x2 -> x0, blocking collectives: 53.3 us -> none  [the longest x1 28 us: per_device(): lax.all_gather(new_values[decode_count:], 'req', axis=0, tiled=True)]
    all_gather x4 -> x3, waiting for transfers between devices: 177 us -> 133 us  [the longest x1 83.5 us: per_device(): near_rows = lax.all_gather(normed, 'req', axis=0, tiled=True)]
    psum x1 -> x0, blocking collectives: 12.8 us -> none  [per_device(): square_total = lax.psum(jnp.sum(mixed_wide * mixed_wide, axis=1), 'mlp')]
    unnamed x0 -> x1, blocking collectives: none -> 12.7 us
    unnamed x47 -> x56, local copies, waits for them, and re-layouts: 9.66 us -> 1.94 us
    slice x0 -> x4, local copies, waits for them, and re-layouts: none -> 5.92 us  [the longest x1 2.58 us: prompt_of(): piece = gathered[:, offset:offset + rows_here][:, decode_count:]]
  transfers between devices with their start and end apart: 7 -> 5, of which waited for: 6 -> 5; matrix products, arithmetic and copies ran while one was open for 5% -> 7% of each run, Pallas kernels for 0% -> 0%
where the time goes in v1:
time: 364 us
  waiting for transfers between devices  184 us (51%)
  blocking collectives  79.6 us (22%)
  matrix products  50.3 us (14%)
  local copies, waits for them, and re-layouts  20 us (5%)
  other arithmetic  15.7 us (4%)
  between operations  14.2 us (4%)
    all_gather x1, waiting for transfers between devices, per_device(): near_rows = lax.all_gather(normed, 'req', axis=0, tiled=True)  83.5 us
    all_gather x1, waiting for transfers between devices, per_device(): hidden_block = lax.all_gather(hidden, 'mlp', axis=1, tiled=True)  45.7 us
    all_to_all x1, blocking collectives, per_device(): lax.all_to_all(down_partial.astype(jnp.bfloat16), 'req', 0, 0, tiled=True)  43 us
    all_gather x1, waiting for transfers between devices, per_device(): gathered = lax.all_gather(packed, 'req', axis=0, tiled=False)  40.7 us
    all_to_all x1, blocking collectives, per_device(): lax.all_to_all(head_partial.astype(jnp.bfloat16), 'mlp', 1, 0, tiled=True)  23.8 us
    dot_general x2, matrix products, project(): jnp.dot(far_rows, far_weight, preferred_element_type=jnp.float32)  16.7 us
    unnamed x1, blocking collectives  12.7 us
    dot_general x2, matrix products, project(): jnp.dot(near_rows, near_weight, preferred_element_type=jnp.float32)  11.7 us
  transfers between devices with their start and end apart: 5, of which 5 were waited for; matrix products, arithmetic and copies ran while one was open for 7% of the time, Pallas kernels for 0%

profile of v1, /device:TPU:0, one launch (start us, length us, event | category | flops | bytes accessed | tf_op | source)
XLA Modules:
  0.0 363.8 jit_solution(15924429722874897913)
XLA Ops:
  6.5 1.8 pad_maximum_fusion
  13.0 1.3 gather_fusion
  15.5 1.2 slice_convert_fusion
  18.8 2.3 fusion.97
  21.4 40.7 %all-gather.14.cloned.1.call-done = bf16[14592,128]{1,0:T(8,128)(2,1)} async-done(((bf16[912,128]{1,0:T(8,128)(2,1)}), bf16[14592,128]{1,0:T(8,128)(2,1)}) %all-gather.14.cloned.1.call-update) | async-done | bytes 3735568 | tf_op jit(solution)/shard_map/all_gather | solution.py:110
  62.0 1.9 fusion.95
  63.9 2.6 fusion.94
  66.5 1.2 copy.26
  68.4 1.2 copy.27
  70.4 1.7 gather_fusion.1
  72.1 2.1 gather_fusion.2
  74.2 1.6 fusion.98
  76.6 2.5 fusion.43
  80.3 1.3 fusion.96
  82.4 1.4 fusion
  85.8 1.4 fusion.56
  88.1 1.3 convolution_convert_fusion
  89.5 23.8 %all_to_all.22 = bf16[136,8,640]{2,0,1:T(8,128)(2,1)S(1)} all-to-all(bf16[136,8,640]{2,0,1:T(8,128)(2,1)S(1)} %bitcast.174), channel_id=1, replica_groups=mesh['req'=16,'mlp'=8] {'mlp'}, dimensions={1} | all-to-all | bytes 2785280 | tf_op jit(solution)/shard_map/all_to_all | solution.py:185
  114.4 12.7 %all-gather.2 = f32[8,1,640]{2,1,0:T(1,128)S(1)} all-gather(f32[1,1,640]{2,1,0:T(1,128)S(1)} %reshape.425), channel_id=2, replica_groups=mesh['req'=16,'mlp'=8] {'mlp'}, dimensions={0}, use_global_device_ids=true | all-gather | bytes 23040 | tf_op args[13]
  127.2 8.5 %all-gather.8.cloned.1.call-done = bf16[136,5120]{1,0:T(8,128)(2,1)} async-done(((bf16[136,640]{1,0:T(8,128)(2,1)}), bf16[136,5120]{1,0:T(8,128)(2,1)}) %all-gather.8.cloned.1.call-update) | async-done | bytes 1392656 | tf_op jit(solution)/shard_map/all_gather | solution.py:193
  135.7 1.7 multiply_reduce_fusion
  137.5 1.6 convert_element_type.68
  139.1 1.0 multiply_convert_fusion
  140.2 83.5 %all-gather.10.cloned.1.call-done = bf16[2176,2560]{1,0:T(8,128)(2,1)} async-done(((bf16[136,2560]{1,0:T(8,128)(2,1)}), bf16[2176,2560]{1,0:T(8,128)(2,1)}) %all-gather.10.cloned.1.call-update) | async-done | bytes 11141136 | tf_op jit(solution)/shard_map/all_gather | solution.py:202
  223.7 8.1 %fusion.48 = f32[2176,216]{0,1:T(8,128)S(1)} fusion(bf16[2176,2560]{1,0:T(8,128)(2,1)} %all-gather.10.cloned.1.call-done, bf16[5120,216]{0,1:T(8,128)(2,1)} %param.31, s32[]{:T(128)S(6)} %select_n.78), kind=kOutput, calls=%fused_computation.57 | convolution fusion | flops 2406481920 | bytes 14127108 | tf_op jit(solution)/shard_map/dot_general | solution.py:209
  232.0 3.6 fusion.45
  235.6 5.5 %collective-permute-done = bf16[2176,2560]{1,0:T(8,128)(2,1)} collective-permute-done((bf16[2176,2560]{1,0:T(8,128)(2,1)}, bf16[2176,2560]{1,0:T(8,128)(2,1)}, u32[]{:S(2)}, u32[]{:S(2)}) %collective-permute-start) | collective-permute-done | bytes 11141152 | tf_op jit(solution)/shard_map/ppermute | solution.py:204
  241.1 7.7 %convolution_add_fusion.1 = f32[2176,216]{0,1:T(8,128)S(1)} fusion(f32[2176,216]{0,1:T(8,128)S(1)} %fusion.48, bf16[2176,2560]{1,0:T(8,128)(2,1)} %collective-permute-done, bf16[5120,216]{0,1:T(8,128)(2,1)S(1)} %copy-done.21, s32[]{:T(128)S(6)} %select_n.79), kind=kOutput, calls=%fused_computation.15 | convolution fusion | flops 2406951936 | bytes 16007172 | tf_op jit(solution)/shard_map/dot_general | solution.py:209
  248.9 9.0 %fusion.4 = bf16[2176,216]{0,1:T(8,128)(2,1)} fusion(f32[2176,216]{0,1:T(8,128)S(1)} %fusion.45, bf16[2176,2560]{1,0:T(8,128)(2,1)} %collective-permute-done, f32[2176,216]{0,1:T(8,128)S(1)} %convolution_add_fusion.1, bf16[5120,216]{0,1:T(8,128)(2,1)S(1)} %copy-done.22, s32[]{:T(128)S(6)} %select_n.79), kind=kOutput, calls=%fused_computation.14 | convolution fusion | flops 2409772032 | bytes 16947204 | tf_op jit(solution)/shard_map/dot_general | solution.py:209
  257.9 45.7 %all-gather.12.cloned.1.call-done = bf16[2176,1728]{0,1:T(8,128)(2,1)} async-done(((bf16[2176,216]{0,1:T(8,128)(2,1)}), bf16[2176,1728]{0,1:T(8,128)(2,1)}) %all-gather.12.cloned.1.call-update) | async-done | bytes 7520272 | tf_op jit(solution)/shard_map/all_gather | solution.py:216
  303.6 9.0 %convolution_convert_fusion.1 = bf16[2176,640]{1,0:T(8,128)(2,1)S(1)} fusion(bf16[2176,1728]{0,1:T(8,128)(2,1)} %all-gather.12.cloned.1.call-done, bf16[1728,640]{1,0:T(8,128)(2,1)S(1)} %copy-done.23), kind=kOutput, calls=%fused_computation.9 | convolution fusion | flops 4814356480 | bytes 12517376 | tf_op jit(solution)/shard_map/dot_general | solution.py:217
  312.6 43.0 %all_to_all.23 = bf16[16,136,640]{2,1,0:T(8,128)(2,1)S(1)} all-to-all(bf16[16,136,640]{2,1,0:T(8,128)(2,1)S(1)} %bitcast.180), channel_id=1, replica_groups=mesh['req'=16,'mlp'=8] {'req'}, dimensions={0} | all-to-all | bytes 5570560 | tf_op jit(solution)/shard_map/all_to_all | solution.py:218
  (101 shorter events, 17.5 us)
Async XLA Ops:
  6.5 12.3 %copy-start = (bf16[3,4096,128]{2,1,0:T(8,128)(2,1)S(1)}, bf16[3,4096,128]{2,1,0:T(8,128)(2,1)}, u32[]{:S(2)}) copy-start(bf16[3,4096,128]{2,1,0:T(8,128)(2,1)} %param.21) | copy-start | bytes 9437188
  6.5 55.5 %all-gather.14.cloned.1.call-start = ((), (), s32[]{:S(2)}) async-start(), calls=%async_computation.5 | async-start | bytes 3969024 | tf_op jit(solution)/shard_map/all_gather | solution.py:110
  8.4 127.4 %all-gather.8.cloned.1.call-start = ((), (), s32[]{:S(2)}) async-start(), calls=%async_computation.2 | async-start | bytes 1566720 | tf_op jit(solution)/shard_map/all_gather | solution.py:193
  10.1 8.0 %copy-start.13 = (bf16[3,5,128]{2,1,0:T(8,128)(2,1)}, bf16[3,5,128]{2,1,0:T(8,128)(2,1)S(1)}, u32[]{:S(2)}) copy-start(bf16[3,5,128]{2,1,0:T(8,128)(2,1)S(1)} %reshape.375) | copy-start | bytes 11524
  68.4 2.0 copy-start.2
  68.4 5.8 %copy-start.12 = (pred[3,1024]{1,0:T(4,128)(4,1)S(1)}, pred[3,1024]{1,0:T(4,128)(4,1)}, u32[]{:S(2)}) copy-start(pred[3,1024]{1,0:T(4,128)(4,1)} %iota_compare_fusion.2) | copy-start | bytes 9220
  68.4 5.8 %copy-start.14 = (bf16[3,5,128]{2,1,0:T(8,128)(2,1)S(1)}, bf16[3,5,128]{2,1,0:T(8,128)(2,1)}, u32[]{:S(2)}) copy-start(bf16[3,5,128]{2,1,0:T(8,128)(2,1)} %copy-done.13) | copy-start | bytes 11524
  69.6 6.2 %copy-start.15 = (f32[3,5]{1,0:T(4,128)S(1)}, f32[3,5]{1,0:T(4,128)}, u32[]{:S(2)}) copy-start(f32[3,5]{1,0:T(4,128)} %get-tuple-element.26) | copy-start | bytes 184
  69.6 6.2 %copy-start.18 = (f32[3,1,5]{2,1,0:T(1,128)S(1)}, f32[3,1,5]{2,1,0:T(1,128)}, u32[]{:S(2)}) copy-start(f32[3,1,5]{2,1,0:T(1,128)} %fusion.79) | copy-start | bytes 184
  70.4 6.2 %copy-start.17 = (f32[3,128]{1,0:T(4,128)S(1)}, f32[3,128]{1,0:T(4,128)}, u32[]{:S(2)}) copy-start(f32[3,128]{1,0:T(4,128)} %slice_convert_fusion) | copy-start | bytes 4612
  74.2 4.9 %copy-start.4 = (bf16[16,133,128]{2,1,0:T(8,128)(2,1)S(1)}, bf16[16,133,128]{2,1,0:T(8,128)(2,1)}, u32[]{:S(2)}) copy-start(bf16[16,133,128]{2,1,0:T(8,128)(2,1)} %get-tuple-element.8) | copy-start | bytes 1634308
  76.3 3.0 copy-start.3
  76.6 3.7 %copy-start.5 = (bf16[133,5,128]{2,1,0:T(8,128)(2,1)S(1)}, bf16[133,5,128]{2,1,0:T(8,128)(2,1)}, u32[]{:S(2)}) copy-start(bf16[133,5,128]{2,1,0:T(8,128)(2,1)} %reshape.383) | copy-start | bytes 510724
  80.3 1.4 copy-start.6
  80.3 1.4 copy-start.8
  80.3 1.4 copy-start.16
  83.8 1.0 copy-start.10
  84.8 1.0 copy-start.9
  84.8 2.6 slice-start
  85.8 2.3 slice-start.1
  89.5 24.1 %copy-start.11 = (bf16[136,640]{1,0:T(8,128)(2,1)S(1)}, bf16[136,640]{1,0:T(8,128)(2,1)}, u32[]{:S(2)}) copy-start(bf16[136,640]{1,0:T(8,128)(2,1)} %param.17) | copy-start | bytes 522244
  89.5 24.8 %copy-start.19 = (f32[640]{0:T(1024)S(1)}, f32[640]{0:T(1024)}, u32[]{:S(2)}) copy-start(f32[640]{0:T(1024)} %param.30) | copy-start | bytes 7684
  114.3 109.4 %all-gather.10.cloned.1.call-start = ((), (), s32[]{:S(2)}) async-start(), calls=%async_computation.3 | async-start | bytes 11837440 | tf_op jit(solution)/shard_map/all_gather | solution.py:202
  140.1 163.5 %all-gather.12.cloned.1.call-start = ((), (), s32[]{:S(2)}) async-start(), calls=%async_computation.4 | async-start | bytes 8460288 | tf_op jit(solution)/shard_map/all_gather | solution.py:216
  223.7 17.4 %collective-permute-start = (bf16[2176,2560]{1,0:T(8,128)(2,1)}, bf16[2176,2560]{1,0:T(8,128)(2,1)}, u32[]{:S(2)}, u32[]{:S(2)}) collective-permute-start(bf16[2176,2560]{1,0:T(8,128)(2,1)} %all-gather.10.cloned.1.call-done), channel_id=1, source_target_pairs={{0,1},{1,0},{2,3},{3,2},{4,5},{5,4},{6,7},{7,6},{8,9},{9,8},{10,11... | collective-permute-start | bytes 33423368 | tf_op jit(solution)/shard_map/ppermute | solution.py:204
  223.7 8.1 %copy-start.20 = (bf16[2176,2560]{1,0:T(8,128)(2,1)S(1)}, bf16[2176,2560]{1,0:T(8,128)(2,1)}, u32[]{:S(2)}) copy-start(bf16[2176,2560]{1,0:T(8,128)(2,1)} %all-gather.10.cloned.1.call-done) | copy-start | bytes 33423364
  223.7 8.3 %copy-start.22 = (bf16[5120,216]{0,1:T(8,128)(2,1)S(1)}, bf16[5120,216]{0,1:T(8,128)(2,1)}, u32[]{:S(2)}) copy-start(bf16[5120,216]{0,1:T(8,128)(2,1)} %param.32) | copy-start | bytes 6635524
  232.0 9.2 %copy-start.21 = (bf16[5120,216]{0,1:T(8,128)(2,1)S(1)}, bf16[5120,216]{0,1:T(8,128)(2,1)}, u32[]{:S(2)}) copy-start(bf16[5120,216]{0,1:T(8,128)(2,1)} %param.31) | copy-start | bytes 6635524
  248.8 54.8 %copy-start.23 = (bf16[1728,640]{1,0:T(8,128)(2,1)S(1)}, bf16[1728,640]{1,0:T(8,128)(2,1)}, u32[]{:S(2)}) copy-start(bf16[1728,640]{1,0:T(8,128)(2,1)} %param.33) | copy-start | bytes 6635524
  312.6 44.6 %copy-start.1 = (bf16[3,4096,128]{2,1,0:T(8,128)(2,1)S(1)}, bf16[3,4096,128]{2,1,0:T(8,128)(2,1)}, u32[]{:S(2)}) copy-start(bf16[3,4096,128]{2,1,0:T(8,128)(2,1)} %param.21) | copy-start | bytes 9437188
  355.6 0.9 copy-start.7
Sparse Core Ops, SparseCore 0:
  9.5 52.4 all-gather.13
  114.4 21.2 all-gather.7
  140.3 83.3 all-gather.9
  258.0 45.5 all-gather.11

commit v2 on v1

--- a/solution.py
+++ b/solution.py
@@ -190,35 +190,55 @@
     )
     mixed = (resid.astype(jnp.float32) + projected).astype(jnp.bfloat16)
     mixed_wide = mixed.astype(jnp.float32)
-    mixed_rows = lax.all_gather(mixed, "mlp", axis=1, tiled=True).astype(jnp.float32)
+    gain_pieces = []
+    remainder = norm_gain
+    for _ in range(3):
+        piece = remainder.astype(jnp.bfloat16)
+        gain_pieces.append(piece)
+        remainder = remainder - piece.astype(jnp.float32)
+    with_gain = jnp.concatenate([mixed, jnp.stack(gain_pieces, 0)], 0)
+    gathered_rows = lax.all_gather(with_gain, "mlp", axis=1, tiled=True).astype(jnp.float32)
+    mixed_rows = gathered_rows[:rows_here]
+    full_gain = (gathered_rows[rows_here] + gathered_rows[rows_here + 1]) + gathered_rows[rows_here + 2]
     square_total = jnp.sum(mixed_rows * mixed_rows, axis=1)
     half = D // 2
     side = lax.axis_index("mlp") % 2
     own_half = lax.dynamic_slice_in_dim(mixed_rows, side * half, half, axis=1)
-    own_gain = lax.dynamic_slice_in_dim(norm_gain, side * half, half, axis=0)
+    own_gain = lax.dynamic_slice_in_dim(full_gain, side * half, half, axis=0)
     normed = (
         own_half * lax.rsqrt(square_total / D + 1e-06)[:, None] * own_gain[None, :]
     ).astype(jnp.bfloat16)
-    near_rows = lax.all_gather(normed, "req", axis=0, tiled=True)
     pairs = [(i, i ^ 1) for i in range(mlp_count)]
-    far_rows = lax.ppermute(near_rows, "mlp", pairs)
-
-    def project(weight):
-        near_weight = lax.dynamic_slice_in_dim(weight, side * half, half, axis=0)
-        far_weight = lax.dynamic_slice_in_dim(weight, (1 - side) * half, half, axis=0)
-        return jnp.dot(near_rows, near_weight, preferred_element_type=jnp.float32) + jnp.dot(
-            far_rows, far_weight, preferred_element_type=jnp.float32
-        )
-
-    gate_proj = project(gate_weight)
-    up_proj = project(up_weight)
-    hidden = (jax.nn.silu(gate_proj) * up_proj).astype(jnp.bfloat16)
-    hidden_block = lax.all_gather(hidden, "mlp", axis=1, tiled=True)
-    down_partial = jnp.dot(hidden_block, down_weight, preferred_element_type=jnp.float32)
-    req_pieces = lax.all_to_all(down_partial.astype(jnp.bfloat16), "req", 0, 0, tiled=True)
-    feed = jnp.sum(
-        req_pieces.reshape(req_count, rows_here, -1).astype(jnp.float32), axis=0
-    )
+
+    def halves(weight):
+        return (
+            lax.dynamic_slice_in_dim(weight, side * half, half, axis=0),
+            lax.dynamic_slice_in_dim(weight, (1 - side) * half, half, axis=0),
+        )
+
+    gate_near, gate_far = halves(gate_weight)
+    up_near, up_far = halves(up_weight)
+    chunk_count = 2
+    chunk_rows = rows_here // chunk_count
+    feeds = []
+    for chunk in range(chunk_count):
+        rows = normed[chunk * chunk_rows : (chunk + 1) * chunk_rows]
+        near_rows = lax.all_gather(rows, "req", axis=0, tiled=True)
+        far_rows = lax.ppermute(near_rows, "mlp", pairs)
+        gate_proj = jnp.dot(near_rows, gate_near, preferred_element_type=jnp.float32) + jnp.dot(
+            far_rows, gate_far, preferred_element_type=jnp.float32
+        )
+        up_proj = jnp.dot(near_rows, up_near, preferred_element_type=jnp.float32) + jnp.dot(
+            far_rows, up_far, preferred_element_type=jnp.float32
+        )
+        hidden = (jax.nn.silu(gate_proj) * up_proj).astype(jnp.bfloat16)
+        hidden_block = lax.all_gather(hidden, "mlp", axis=1, tiled=True)
+        down_partial = jnp.dot(hidden_block, down_weight, preferred_element_type=jnp.float32)
+        req_pieces = lax.all_to_all(down_partial.astype(jnp.bfloat16), "req", 0, 0, tiled=True)
+        feeds.append(
+            jnp.sum(req_pieces.reshape(req_count, chunk_rows, -1).astype(jnp.float32), axis=0)
+        )
+    feed = jnp.concatenate(feeds, 0)
     return (mixed_wide + feed).astype(jnp.bfloat16)
 
 
@@ -240,7 +260,7 @@
             P(),
             P(),
             P("mlp", None),
-            P(),
+            P("mlp"),
             P(None, ("req", "mlp")),
             P(None, ("req", "mlp")),
             P("req", "mlp"),

time: 364 us -> 401 us (1.10)
  blocking collectives: 79.6 us -> 0 us
  waiting for transfers between devices: 184 us -> 245 us
  local copies, waits for them, and re-layouts: 20 us -> 42.2 us
  starting transfers between devices: 0.13 us -> 19.2 us
  matrix products: 50.3 us -> 62.1 us
    all_to_all x2 -> x0, blocking collectives: 66.8 us -> none  [the longest x1 43 us: per_device(): lax.all_to_all(down_partial.astype(jnp.bfloat16), 'req', 0, 0, tiled=True)]
    all_gather x2 -> x3, waiting for transfers between devices: 92 us -> 134 us  [the longest x2 112 us: per_device(): near_rows = lax.all_gather(rows, 'req', axis=0, tiled=True)]
    all_to_all x0 -> x3, waiting for transfers between devices: none -> 41.1 us  [the longest x2 21.8 us: per_device(): lax.all_to_all(down_partial.astype(jnp.bfloat16), 'req', 0, 0, tiled=True)]
    all_to_all x0 -> x3, starting transfers between devices: none -> 18.6 us  [the longest x2 14.2 us: per_device(): lax.all_to_all(down_partial.astype(jnp.bfloat16), 'req', 0, 0, tiled=True)]
    all_gather x1 -> x2, waiting for transfers between devices: 45.7 us -> 29 us  [per_device(): hidden_block = lax.all_gather(hidden, 'mlp', axis=1, tiled=True)]
    unnamed x56 -> x60, local copies, waits for them, and re-layouts: 1.94 us -> 18.1 us
    unnamed x1 -> x0, blocking collectives: 12.7 us -> none
    dot_general x4 -> x8, matrix products: 28.4 us -> 36.6 us  [the longest x2 11 us: per_device(): jnp.dot(far_rows, up_far, preferred_element_type=jnp.float32)]
  transfers between devices with their start and end apart: 5 -> 11, of which waited for: 5 -> 8; matrix products, arithmetic and copies ran while one was open for 7% -> 20% of each run, Pallas kernels for 0% -> 0%
where the time goes in v2:
time: 401 us; the launch traced here: 400 us
  waiting for transfers between devices  245 us (61%)
  matrix products  62.1 us (15%)
  local copies, waits for them, and re-layouts  42.2 us (11%)
  starting transfers between devices  19.2 us (5%)
  other arithmetic  16.5 us (4%)
  between operations  14.6 us (4%)
    all_gather x2, waiting for transfers between devices, per_device(): near_rows = lax.all_gather(rows, 'req', axis=0, tiled=True)  112 us
    all_gather x1, waiting for transfers between devices, per_device(): gathered = lax.all_gather(packed, 'req', axis=0, tiled=False)  40.6 us
    all_gather x2, waiting for transfers between devices, per_device(): hidden_block = lax.all_gather(hidden, 'mlp', axis=1, tiled=True)  29 us
    all_to_all x2, waiting for transfers between devices, per_device(): lax.all_to_all(down_partial.astype(jnp.bfloat16), 'req', 0, 0, tiled=True)  21.8 us
    all_gather x1, waiting for transfers between devices, per_device(): lax.all_gather(with_gain, 'mlp', axis=1, tiled=True).astype(jnp.float32)  21.5 us
    all_to_all x1, waiting for transfers between devices, per_device(): lax.all_to_all(head_partial.astype(jnp.bfloat16), 'mlp', 1, 0, tiled=True)  19.3 us
    unnamed x60, local copies, waits for them, and re-layouts  18.1 us
    all_to_all x2, starting transfers between devices, per_device(): lax.all_to_all(down_partial.astype(jnp.bfloat16), 'req', 0, 0, tiled=True)  14.2 us
  transfers between devices with their start and end apart: 11, of which 8 were waited for; matrix products, arithmetic and copies ran while one was open for 20% of the time, Pallas kernels for 0%

profile of v2, /device:TPU:0, one launch (start us, length us, event | category | flops | bytes accessed | tf_op | source)
XLA Modules:
  0.0 399.9 jit_solution(140865241295268066)
XLA Ops:
  6.5 1.8 pad_maximum_fusion
  18.9 2.3 fusion.114
  21.4 40.6 %all-gather.16.cloned.1.call-done = bf16[14592,128]{1,0:T(8,128)(2,1)} async-done(((bf16[912,128]{1,0:T(8,128)(2,1)}), bf16[14592,128]{1,0:T(8,128)(2,1)}) %all-gather.16.cloned.1.call-update) | async-done | bytes 3735568 | tf_op jit(solution)/shard_map/all_gather | solution.py:110
  62.0 1.9 fusion.110
  63.9 2.6 fusion.109
  70.4 1.7 gather_fusion.1
  72.0 2.1 gather_fusion.2
  76.6 2.5 fusion.45
  90.6 4.4 %all-to-all-start = ((bf16[136,8,640]{2,0,1:T(8,128)(2,1)}), bf16[136,8,640]{2,0,1:T(8,128)(2,1)S(1)}, u32[]{:S(2)}, u32[]{:S(2)}) async-start(bf16[136,8,640]{2,0,1:T(8,128)(2,1)} %bitcast.172), calls=%async_computation | async-start | bytes 2785280 | tf_op jit(solution)/shard_map/all_to_all | solution.py:185
  95.3 19.3 %all-to-all-done = bf16[136,8,640]{2,0,1:T(8,128)(2,1)S(1)} async-done(((bf16[136,8,640]{2,0,1:T(8,128)(2,1)}), bf16[136,8,640]{2,0,1:T(8,128)(2,1)S(1)}, u32[]{:S(2)}, u32[]{:S(2)}) %all-to-all-start) | async-done | bytes 1392672 | tf_op jit(solution)/shard_map/all_to_all | solution.py:185
  115.6 21.5 %all-gather.10.cloned.1.call-done = bf16[139,5120]{1,0:T(8,128)(2,1)} async-done(((bf16[139,640]{1,0:T(8,128)(2,1)}), bf16[139,5120]{1,0:T(8,128)(2,1)}) %all-gather.10.cloned.1.call-update) | async-done | bytes 1423376 | tf_op jit(solution)/shard_map/all_gather | solution.py:200
  137.2 1.8 convert_element_type.97
  141.4 59.1 %all-gather.18.cloned.1.call-done = bf16[16,68,2560]{2,1,0:T(8,128)(2,1)} async-done(((bf16[1,68,2560]{2,1,0:T(8,128)(2,1)}), bf16[16,68,2560]{2,1,0:T(8,128)(2,1)}) %all-gather.18.cloned.1.call-update) | async-done | bytes 5570576 | tf_op jit(solution)/shard_map/all_gather | solution.py:226
  200.5 7.9 %reshape.433 = bf16[1088,2560]{1,0:T(8,128)(2,1)} reshape(bf16[16,68,2560]{2,1,0:T(8,128)(2,1)} %all-gather.18.cloned.1.call-done) | data formatting | bytes 11141120
  208.4 53.3 %all-gather.20.cloned.1.call-done = bf16[16,68,2560]{2,1,0:T(8,128)(2,1)} async-done(((bf16[1,68,2560]{2,1,0:T(8,128)(2,1)}), bf16[16,68,2560]{2,1,0:T(8,128)(2,1)}) %all-gather.20.cloned.1.call-update) | async-done | bytes 5570576 | tf_op jit(solution)/shard_map/all_gather | solution.py:226
  261.7 7.9 %reshape.435 = bf16[1088,2560]{1,0:T(8,128)(2,1)} reshape(bf16[16,68,2560]{2,1,0:T(8,128)(2,1)} %all-gather.20.cloned.1.call-done) | data formatting | bytes 11141120
  269.6 4.7 %fusion.65 = f32[1088,216]{0,1:T(8,128)S(1)} fusion(bf16[1088,2560]{1,0:T(8,128)(2,1)} %reshape.433, bf16[5120,216]{0,1:T(8,128)(2,1)S(1)} %copy-done.21, s32[]{:T(128)S(6)} %select_n.78), kind=kOutput, calls=%fused_computation.72 | convolution fusion | flops 1203240960 | bytes 7616516 | tf_op jit(solution)/shard_map/dot_general | solution.py:228
  274.5 2.0 fusion.59
  276.5 4.6 %convolution_add_fusion.3 = f32[1088,216]{0,1:T(8,128)S(1)} fusion(f32[1088,216]{0,1:T(8,128)S(1)} %fusion.65, bf16[1088,2560]{1,0:T(8,128)(2,1)} %collective-permute-done, bf16[5120,216]{0,1:T(8,128)(2,1)S(1)} %copy-done.21, s32[]{:T(128)S(6)} %select_n.79), kind=kOutput, calls=%fused_computation.31 | convolution fusion | flops 1203475968 | bytes 8611844 | tf_op jit(solution)/shard_map/dot_general | solution.py:228
  281.1 5.5 %fusion.13 = bf16[1088,216]{0,1:T(8,128)(2,1)} fusion(f32[1088,216]{0,1:T(8,128)S(1)} %fusion.59, bf16[1088,2560]{1,0:T(8,128)(2,1)} %collective-permute-done, f32[1088,216]{0,1:T(8,128)S(1)} %convolution_add_fusion.3, bf16[5120,216]{0,1:T(8,128)(2,1)S(1)} %copy-done.22, s32[]{:T(128)S(6)} %select_n.79), kind=kOutput, calls=%fused_computation.32 | convolution fusion | flops 1204886016 | bytes 9137156 | tf_op jit(solution)/shard_map/dot_general | solution.py:231
  286.9 4.7 %fusion.63 = f32[1088,216]{0,1:T(8,128)S(1)} fusion(bf16[1088,2560]{1,0:T(8,128)(2,1)} %reshape.435, bf16[5120,216]{0,1:T(8,128)(2,1)S(1)} %copy-done.21, s32[]{:T(128)S(6)} %select_n.78), kind=kOutput, calls=%fused_computation.70 | convolution fusion | flops 1203240960 | bytes 7616516 | tf_op jit(solution)/shard_map/dot_general | solution.py:228
  291.6 4.6 %fusion.57 = f32[1088,216]{0,1:T(8,128)S(1)} fusion(bf16[1088,2560]{1,0:T(8,128)(2,1)} %reshape.435, bf16[5120,216]{0,1:T(8,128)(2,1)S(1)} %copy-done.23, s32[]{:T(128)S(6)} %select_n.78), kind=kOutput, calls=%fused_computation.64 | convolution fusion | flops 1203240960 | bytes 7616516 | tf_op jit(solution)/shard_map/dot_general | solution.py:231
  296.2 4.9 %convolution_add_fusion.1 = f32[1088,216]{0,1:T(8,128)S(1)} fusion(f32[1088,216]{0,1:T(8,128)S(1)} %fusion.63, bf16[1088,2560]{1,0:T(8,128)(2,1)} %collective-permute-done.1, bf16[5120,216]{0,1:T(8,128)(2,1)S(1)} %copy-done.21, s32[]{:T(128)S(6)} %select_n.79), kind=kOutput, calls=%fused_computation.28 | convolution fusion | flops 1203475968 | bytes 8611844 | tf_op jit(solution)/shard_map/dot_general | solution.py:228
  301.2 5.5 %fusion.14 = bf16[1088,216]{0,1:T(8,128)(2,1)} fusion(f32[1088,216]{0,1:T(8,128)S(1)} %fusion.57, bf16[1088,2560]{1,0:T(8,128)(2,1)} %collective-permute-done.1, f32[1088,216]{0,1:T(8,128)S(1)} %convolution_add_fusion.1, bf16[5120,216]{0,1:T(8,128)(2,1)S(1)} %copy-done.23, s32[]{:T(128)S(6)} %select_n.79), kind=kOutput, calls=%fused_computation.33 | convolution fusion | flops 1204886016 | bytes 9137156 | tf_op jit(solution)/shard_map/dot_general | solution.py:231
  306.7 10.9 %all-gather.12.cloned.1.call-done = bf16[1088,1728]{0,1:T(8,128)(2,1)} async-done(((bf16[1088,216]{0,1:T(8,128)(2,1)}), bf16[1088,1728]{0,1:T(8,128)(2,1)}) %all-gather.12.cloned.1.call-update) | async-done | bytes 3760144 | tf_op jit(solution)/shard_map/all_gather | solution.py:235
  317.6 6.1 %convolution_convert_fusion.2 = bf16[1088,640]{1,0:T(8,128)(2,1)S(1)} fusion(bf16[1088,1728]{0,1:T(8,128)(2,1)} %all-gather.12.cloned.1.call-done, bf16[1728,640]{1,0:T(8,128)(2,1)} %param.33), kind=kOutput, calls=%fused_computation.11 | convolution fusion | flops 2407178240 | bytes 7364608 | tf_op jit(solution)/shard_map/dot_general | solution.py:236
  325.0 7.2 %all-to-all-start.1 = ((bf16[16,68,640]{2,1,0:T(8,128)(2,1)}), bf16[16,68,640]{2,1,0:T(8,128)(2,1)}, u32[]{:S(2)}, u32[]{:S(2)}) async-start(bf16[16,68,640]{2,1,0:T(8,128)(2,1)} %all_to_all.24), calls=%async_computation.1 | async-start | bytes 2949120 | tf_op jit(solution)/shard_map/all_to_all | solution.py:237
  332.2 18.1 %all-gather.14.cloned.1.call-done = bf16[1088,1728]{0,1:T(8,128)(2,1)} async-done(((bf16[1088,216]{0,1:T(8,128)(2,1)}), bf16[1088,1728]{0,1:T(8,128)(2,1)}) %all-gather.14.cloned.1.call-update) | async-done | bytes 3760144 | tf_op jit(solution)/shard_map/all_gather | solution.py:235
  350.3 6.6 %convolution_convert_fusion.1 = bf16[1088,640]{1,0:T(8,128)(2,1)} fusion(bf16[1088,1728]{0,1:T(8,128)(2,1)} %all-gather.14.cloned.1.call-done, bf16[1728,640]{1,0:T(8,128)(2,1)S(1)} %copy-done.24), kind=kOutput, calls=%fused_computation.10 | convolution fusion | flops 2407178240 | bytes 7364608 | tf_op jit(solution)/shard_map/dot_general | solution.py:236
  356.9 3.4 all_to_all.26
  360.3 7.0 %all-to-all-start.2 = ((bf16[16,68,640]{2,1,0:T(8,128)(2,1)}), bf16[16,68,640]{2,1,0:T(8,128)(2,1)}, u32[]{:S(2)}, u32[]{:S(2)}) async-start(bf16[16,68,640]{2,1,0:T(8,128)(2,1)} %all_to_all.26), calls=%async_computation.2 | async-start | bytes 2949120 | tf_op jit(solution)/shard_map/all_to_all | solution.py:237
  368.9 21.8 %all-to-all-done.2 = bf16[16,68,640]{2,1,0:T(8,128)(2,1)} async-done(((bf16[16,68,640]{2,1,0:T(8,128)(2,1)}), bf16[16,68,640]{2,1,0:T(8,128)(2,1)}, u32[]{:S(2)}, u32[]{:S(2)}) %all-to-all-start.2) | async-done | bytes 1392672 | tf_op jit(solution)/shard_map/all_to_all | solution.py:237
  (131 shorter events, 36.9 us)
Async XLA Ops:
  6.5 12.3 %copy-start = (bf16[3,4096,128]{2,1,0:T(8,128)(2,1)S(1)}, bf16[3,4096,128]{2,1,0:T(8,128)(2,1)}, u32[]{:S(2)}) copy-start(bf16[3,4096,128]{2,1,0:T(8,128)(2,1)} %param.21) | copy-start | bytes 9437188
  6.5 55.5 %all-gather.16.cloned.1.call-start = ((), (), s32[]{:S(2)}) async-start(), calls=%async_computation.6 | async-start | bytes 3969024 | tf_op jit(solution)/shard_map/all_gather | solution.py:110
  10.1 8.0 %copy-start.14 = (bf16[3,5,128]{2,1,0:T(8,128)(2,1)}, bf16[3,5,128]{2,1,0:T(8,128)(2,1)S(1)}, u32[]{:S(2)}) copy-start(bf16[3,5,128]{2,1,0:T(8,128)(2,1)S(1)} %reshape.382) | copy-start | bytes 11524
  68.4 5.7 %copy-start.13 = (pred[3,1024]{1,0:T(4,128)(4,1)S(1)}, pred[3,1024]{1,0:T(4,128)(4,1)}, u32[]{:S(2)}) copy-start(pred[3,1024]{1,0:T(4,128)(4,1)} %iota_compare_fusion.2) | copy-start | bytes 9220
  68.4 5.8 %copy-start.15 = (bf16[3,5,128]{2,1,0:T(8,128)(2,1)S(1)}, bf16[3,5,128]{2,1,0:T(8,128)(2,1)}, u32[]{:S(2)}) copy-start(bf16[3,5,128]{2,1,0:T(8,128)(2,1)} %copy-done.14) | copy-start | bytes 11524
  69.6 6.2 %copy-start.16 = (f32[3,5]{1,0:T(4,128)S(1)}, f32[3,5]{1,0:T(4,128)}, u32[]{:S(2)}) copy-start(f32[3,5]{1,0:T(4,128)} %get-tuple-element.34) | copy-start | bytes 184
  69.6 6.2 %copy-start.19 = (f32[3,1,5]{2,1,0:T(1,128)S(1)}, f32[3,1,5]{2,1,0:T(1,128)}, u32[]{:S(2)}) copy-start(f32[3,1,5]{2,1,0:T(1,128)} %fusion.98) | copy-start | bytes 184
  70.4 6.2 %copy-start.18 = (f32[3,128]{1,0:T(4,128)S(1)}, f32[3,128]{1,0:T(4,128)}, u32[]{:S(2)}) copy-start(f32[3,128]{1,0:T(4,128)} %slice_convert_fusion) | copy-start | bytes 4612
  74.2 4.9 %copy-start.6 = (bf16[16,133,128]{2,1,0:T(8,128)(2,1)S(1)}, bf16[16,133,128]{2,1,0:T(8,128)(2,1)}, u32[]{:S(2)}) copy-start(bf16[16,133,128]{2,1,0:T(8,128)(2,1)} %get-tuple-element.8) | copy-start | bytes 1634308
  76.3 3.0 copy-start.5
  76.6 3.7 copy-start.7
  84.8 2.6 slice-start
  85.8 2.3 slice-start.1
  89.3 5.9 %copy-start.20 = (f32[640]{0:T(1024)S(1)}, f32[640]{0:T(1024)}, u32[]{:S(2)}) copy-start(f32[640]{0:T(1024)} %param.30) | copy-start | bytes 7684
  90.6 24.2 %copy-start.12 = (bf16[136,640]{1,0:T(8,128)(2,1)S(1)}, bf16[136,640]{1,0:T(8,128)(2,1)}, u32[]{:S(2)}) copy-start(bf16[136,640]{1,0:T(8,128)(2,1)} %param.17) | copy-start | bytes 522244
  90.6 24.0 %all-to-all-start = ((bf16[136,8,640]{2,0,1:T(8,128)(2,1)}), bf16[136,8,640]{2,0,1:T(8,128)(2,1)S(1)}, u32[]{:S(2)}, u32[]{:S(2)}) async-start(bf16[136,8,640]{2,0,1:T(8,128)(2,1)} %bitcast.172), calls=%async_computation | async-start | bytes 2785280 | tf_op jit(solution)/shard_map/all_to_all | solution.py:185
  95.0 42.2 %all-gather.10.cloned.1.call-start = ((), (), s32[]{:S(2)}) async-start(), calls=%async_computation.3 | async-start | bytes 1658880 | tf_op jit(solution)/shard_map/all_gather | solution.py:200
  115.6 84.9 %all-gather.18.cloned.1.call-start = ((), (), s32[]{:S(2)}) async-start(), calls=%async_computation.7 | async-start | bytes 6266880 | tf_op jit(solution)/shard_map/all_gather | solution.py:226
  137.1 2.1 copy-start.2
  140.8 120.9 %all-gather.20.cloned.1.call-start = ((), (), s32[]{:S(2)}) async-start(), calls=%async_computation.8 | async-start | bytes 6266880 | tf_op jit(solution)/shard_map/all_gather | solution.py:226
  141.3 176.3 %all-gather.12.cloned.1.call-start = ((), (), s32[]{:S(2)}) async-start(), calls=%async_computation.4 | async-start | bytes 4478976 | tf_op jit(solution)/shard_map/all_gather | solution.py:235
  208.4 68.1 %collective-permute-start = (bf16[1088,2560]{1,0:T(8,128)(2,1)}, bf16[1088,2560]{1,0:T(8,128)(2,1)}, u32[]{:S(2)}, u32[]{:S(2)}) collective-permute-start(bf16[1088,2560]{1,0:T(8,128)(2,1)} %reshape.433), channel_id=1, source_target_pairs={{0,1},{1,0},{2,3},{3,2},{4,5},{5,4},{6,7},{7,6},{8,9},{9,8},{10,11... | collective-permute-start | bytes 16711688 | tf_op jit(solution)/shard_map/ppermute | solution.py:227
  208.4 61.2 %copy-start.21 = (bf16[5120,216]{0,1:T(8,128)(2,1)S(1)}, bf16[5120,216]{0,1:T(8,128)(2,1)}, u32[]{:S(2)}) copy-start(bf16[5120,216]{0,1:T(8,128)(2,1)} %param.31) | copy-start | bytes 6635524
  269.5 4.8 %copy-start.3 = (bf16[1088,2560]{1,0:T(8,128)(2,1)S(1)}, bf16[1088,2560]{1,0:T(8,128)(2,1)}, u32[]{:S(2)}) copy-start(bf16[1088,2560]{1,0:T(8,128)(2,1)} %reshape.433) | copy-start | bytes 16711684
  269.5 4.9 %copy-start.22 = (bf16[5120,216]{0,1:T(8,128)(2,1)S(1)}, bf16[5120,216]{0,1:T(8,128)(2,1)}, u32[]{:S(2)}) copy-start(bf16[5120,216]{0,1:T(8,128)(2,1)} %param.32) | copy-start | bytes 6635524
  269.6 26.7 %collective-permute-start.1 = (bf16[1088,2560]{1,0:T(8,128)(2,1)}, bf16[1088,2560]{1,0:T(8,128)(2,1)}, u32[]{:S(2)}, u32[]{:S(2)}) collective-permute-start(bf16[1088,2560]{1,0:T(8,128)(2,1)} %reshape.435), channel_id=1, source_target_pairs={{0,1},{1,0},{2,3},{3,2},{4,5},{5,4},{6,7},{7,6},{8,9},{9,8},{10,11... | collective-permute-start | bytes 16711688 | tf_op jit(solution)/shard_map/ppermute | solution.py:227
  286.6 63.7 %all-gather.14.cloned.1.call-start = ((), (), s32[]{:S(2)}) async-start(), calls=%async_computation.5 | async-start | bytes 4478976 | tf_op jit(solution)/shard_map/all_gather | solution.py:235
  286.9 4.7 %copy-start.23 = (bf16[5120,216]{0,1:T(8,128)(2,1)S(1)}, bf16[5120,216]{0,1:T(8,128)(2,1)}, u32[]{:S(2)}) copy-start(bf16[5120,216]{0,1:T(8,128)(2,1)} %param.32) | copy-start | bytes 6635524
  325.0 25.3 %copy-start.24 = (bf16[1728,640]{1,0:T(8,128)(2,1)S(1)}, bf16[1728,640]{1,0:T(8,128)(2,1)}, u32[]{:S(2)}) copy-start(bf16[1728,640]{1,0:T(8,128)(2,1)} %param.33) | copy-start | bytes 6635524
  325.0 35.2 %all-to-all-start.1 = ((bf16[16,68,640]{2,1,0:T(8,128)(2,1)}), bf16[16,68,640]{2,1,0:T(8,128)(2,1)}, u32[]{:S(2)}, u32[]{:S(2)}) async-start(bf16[16,68,640]{2,1,0:T(8,128)(2,1)} %all_to_all.24), calls=%async_computation.1 | async-start | bytes 2949120 | tf_op jit(solution)/shard_map/all_to_all | solution.py:237
  356.9 36.1 %copy-start.1 = (bf16[3,4096,128]{2,1,0:T(8,128)(2,1)S(1)}, bf16[3,4096,128]{2,1,0:T(8,128)(2,1)}, u32[]{:S(2)}) copy-start(bf16[3,4096,128]{2,1,0:T(8,128)(2,1)} %param.21) | copy-start | bytes 9437188
  360.3 30.4 %all-to-all-start.2 = ((bf16[16,68,640]{2,1,0:T(8,128)(2,1)}), bf16[16,68,640]{2,1,0:T(8,128)(2,1)}, u32[]{:S(2)}, u32[]{:S(2)}) async-start(bf16[16,68,640]{2,1,0:T(8,128)(2,1)} %all_to_all.26), calls=%async_computation.2 | async-start | bytes 2949120 | tf_op jit(solution)/shard_map/all_to_all | solution.py:237
  (6 other events, 8.0 us)
Sparse Core Ops, SparseCore 0:
  9.5 52.4 all-gather.15
  115.7 21.4 all-gather.9
  140.9 59.5 all-gather.17
  202.5 59.0 all-gather.19
  286.7 30.8 all-gather.11
  319.2 31.0 all-gather.13

commit v3 on v1

--- a/solution.py
+++ b/solution.py
@@ -190,25 +190,57 @@
     )
     mixed = (resid.astype(jnp.float32) + projected).astype(jnp.bfloat16)
     mixed_wide = mixed.astype(jnp.float32)
-    mixed_rows = lax.all_gather(mixed, "mlp", axis=1, tiled=True).astype(jnp.float32)
+    gain_pieces = []
+    remainder = norm_gain
+    for _ in range(3):
+        piece = remainder.astype(jnp.bfloat16)
+        gain_pieces.append(piece)
+        remainder = remainder - piece.astype(jnp.float32)
+    with_gain = jnp.concatenate([mixed, jnp.stack(gain_pieces, 0)], 0)
+    gathered_rows = lax.all_gather(with_gain, "mlp", axis=1, tiled=True).astype(jnp.float32)
+    mixed_rows = gathered_rows[:rows_here]
+    full_gain = (gathered_rows[rows_here] + gathered_rows[rows_here + 1]) + gathered_rows[rows_here + 2]
     square_total = jnp.sum(mixed_rows * mixed_rows, axis=1)
     half = D // 2
     side = lax.axis_index("mlp") % 2
     own_half = lax.dynamic_slice_in_dim(mixed_rows, side * half, half, axis=1)
-    own_gain = lax.dynamic_slice_in_dim(norm_gain, side * half, half, axis=0)
+    own_gain = lax.dynamic_slice_in_dim(full_gain, side * half, half, axis=0)
     normed = (
         own_half * lax.rsqrt(square_total / D + 1e-06)[:, None] * own_gain[None, :]
     ).astype(jnp.bfloat16)
-    near_rows = lax.all_gather(normed, "req", axis=0, tiled=True)
     pairs = [(i, i ^ 1) for i in range(mlp_count)]
-    far_rows = lax.ppermute(near_rows, "mlp", pairs)
+
+    def halves(weight):
+        return (
+            lax.dynamic_slice_in_dim(weight, side * half, half, axis=0),
+            lax.dynamic_slice_in_dim(weight, (1 - side) * half, half, axis=0),
+        )
+
+    req_split = (half * 7 // 10) // 128 * 128
+
+    def gathered(block):
+        spread = block.shape[1] - req_split
+        copies = jnp.broadcast_to(block[:, req_split:][None], (req_count, rows_here, spread))
+        return (
+            lax.all_gather(block[:, :req_split], "req", axis=0, tiled=True),
+            lax.all_to_all(
+                copies.reshape(req_count * rows_here, spread), "req", 0, 0, tiled=True
+            ),
+        )
+
+    near_rows = gathered(normed)
+    far_rows = tuple(lax.ppermute(part, "mlp", pairs) for part in near_rows)
 
     def project(weight):
-        near_weight = lax.dynamic_slice_in_dim(weight, side * half, half, axis=0)
-        far_weight = lax.dynamic_slice_in_dim(weight, (1 - side) * half, half, axis=0)
-        return jnp.dot(near_rows, near_weight, preferred_element_type=jnp.float32) + jnp.dot(
-            far_rows, far_weight, preferred_element_type=jnp.float32
-        )
+        near_weight, far_weight = halves(weight)
+        total = None
+        for rows, part_weight in ((near_rows, near_weight), (far_rows, far_weight)):
+            for index, lower, upper in ((0, 0, req_split), (1, req_split, half)):
+                term = jnp.dot(
+                    rows[index], part_weight[lower:upper], preferred_element_type=jnp.float32
+                )
+                total = term if total is None else total + term
+        return total
 
     gate_proj = project(gate_weight)
     up_proj = project(up_weight)
@@ -240,7 +272,7 @@
             P(),
             P(),
             P("mlp", None),
-            P(),
+            P("mlp"),
             P(None, ("req", "mlp")),
             P(None, ("req", "mlp")),
             P("req", "mlp"),

time: 364 us -> 392 us (1.077)
  waiting for transfers between devices: 184 us -> 238 us
  blocking collectives: 79.6 us -> 43 us
  starting transfers between devices: 0.13 us -> 12.2 us
    all_to_all x1 -> x0, blocking collectives: 23.8 us -> none  [per_device(): lax.all_to_all(head_partial.astype(jnp.bfloat16), 'mlp', 1, 0, tiled=True)]
    all_gather x2, waiting for transfers between devices: 92 us -> 116 us  [the longest x1 94.1 us: gathered(): lax.all_gather(block[:, :req_split], 'req', axis=0, tiled=True)]
    all_to_all x0 -> x2, waiting for transfers between devices: none -> 19.3 us  [the longest x1 19.3 us: per_device(): lax.all_to_all(head_partial.astype(jnp.bfloat16), 'mlp', 1, 0, tiled=True)]
    unnamed x1 -> x0, blocking collectives: 12.7 us -> none
    ppermute x1 -> x2, waiting for transfers between devices: 5.54 us -> 16.9 us  [per_device(): far_rows = tuple((lax.ppermute(part, 'mlp', pairs) for part in near_rows))]
    all_to_all x0 -> x2, starting transfers between devices: none -> 11.4 us  [the longest x1 6.98 us: gathered(): lax.all_to_all(copies.reshape(req_count * rows_here, spread), 'req', 0, 0...]
    dot_general x4 -> x8, matrix products: 28.4 us -> 27.2 us  [project(): jnp.dot(rows[index], part_weight[lower:upper], preferred_element_type=jnp...]
  transfers between devices with their start and end apart: 5 -> 8, of which waited for: 5 -> 6; matrix products, arithmetic and copies ran while one was open for 7% -> 7% of each run, Pallas kernels for 0% -> 0%
where the time goes in v3:
time: 392 us
  waiting for transfers between devices  238 us (61%)
  matrix products  48.9 us (12%)
  blocking collectives  43 us (11%)
  local copies, waits for them, and re-layouts  21.2 us (5%)
  between operations  14.3 us (4%)
  other arithmetic  13.6 us (3%)
  starting transfers between devices  12.2 us (3%)
    all_gather x1, waiting for transfers between devices, gathered(): lax.all_gather(block[:, :req_split], 'req', axis=0, tiled=True)  94.1 us
    all_gather x1, waiting for transfers between devices, per_device(): hidden_block = lax.all_gather(hidden, 'mlp', axis=1, tiled=True)  45.7 us
    all_to_all x1, blocking collectives, per_device(): lax.all_to_all(down_partial.astype(jnp.bfloat16), 'req', 0, 0, tiled=True)  43 us
    all_gather x1, waiting for transfers between devices, per_device(): gathered = lax.all_gather(packed, 'req', axis=0, tiled=False)  40.7 us
    dot_general x8, matrix products, project(): jnp.dot(rows[index], part_weight[lower:upper], preferred_element_type=jnp...  27.2 us
    all_gather x1, waiting for transfers between devices, per_device(): lax.all_gather(with_gain, 'mlp', axis=1, tiled=True).astype(jnp.float32)  21.5 us
    all_to_all x1, waiting for transfers between devices, per_device(): lax.all_to_all(head_partial.astype(jnp.bfloat16), 'mlp', 1, 0, tiled=True)  19.3 us
    ppermute x2, waiting for transfers between devices, per_device(): far_rows = tuple((lax.ppermute(part, 'mlp', pairs) for part in near_rows))  16.9 us
  transfers between devices with their start and end apart: 8, of which 6 were waited for; matrix products, arithmetic and copies ran while one was open for 7% of the time, Pallas kernels for 0%

profile of v3, /device:TPU:0, one launch (start us, length us, event | category | flops | bytes accessed | tf_op | source)
XLA Modules:
  0.0 391.6 jit_solution(15192644658047380030)
XLA Ops:
  6.5 1.8 pad_maximum_fusion
  12.9 1.3 gather_fusion
  15.5 1.3 slice_convert_fusion
  18.8 2.3 fusion.113
  21.4 40.7 %all-gather.12.cloned.1.call-done = bf16[14592,128]{1,0:T(8,128)(2,1)} async-done(((bf16[912,128]{1,0:T(8,128)(2,1)}), bf16[14592,128]{1,0:T(8,128)(2,1)}) %all-gather.12.cloned.1.call-update) | async-done | bytes 3735568 | tf_op jit(solution)/shard_map/all_gather | solution.py:110
  62.0 2.6 fusion.108
  64.6 1.9 fusion.109
  68.2 2.0 reshape.438
  70.3 1.8 gather_fusion.2
  73.5 1.4 fusion.81
  75.2 2.5 fusion.43
  78.6 1.3 fusion.112
  80.0 1.4 fusion
  83.4 1.4 fusion.50
  85.7 1.3 convolution_convert_fusion
  88.2 4.4 %all-to-all-start = ((bf16[136,8,640]{2,0,1:T(8,128)(2,1)}), bf16[136,8,640]{2,0,1:T(8,128)(2,1)S(1)}, u32[]{:S(2)}, u32[]{:S(2)}) async-start(bf16[136,8,640]{2,0,1:T(8,128)(2,1)} %bitcast.168), calls=%async_computation | async-start | bytes 2785280 | tf_op jit(solution)/shard_map/all_to_all | solution.py:185
  92.9 19.3 %all-to-all-done = bf16[136,8,640]{2,0,1:T(8,128)(2,1)S(1)} async-done(((bf16[136,8,640]{2,0,1:T(8,128)(2,1)}), bf16[136,8,640]{2,0,1:T(8,128)(2,1)S(1)}, u32[]{:S(2)}, u32[]{:S(2)}) %all-to-all-start) | async-done | bytes 1392672 | tf_op jit(solution)/shard_map/all_to_all | solution.py:185
  113.2 21.5 %all-gather.6.cloned.1.call-done = bf16[139,5120]{1,0:T(8,128)(2,1)} async-done(((bf16[139,640]{1,0:T(8,128)(2,1)}), bf16[139,5120]{1,0:T(8,128)(2,1)}) %all-gather.6.cloned.1.call-update) | async-done | bytes 1423376 | tf_op jit(solution)/shard_map/all_gather | solution.py:200
  134.7 1.8 convert_element_type.88
  138.3 1.9 broadcast_in_dim.147
  140.2 7.0 %all-to-all-start.1 = ((bf16[16,136,768]{2,1,0:T(8,128)(2,1)}), bf16[16,136,768]{2,1,0:T(8,128)(2,1)S(1)}, u32[]{:S(2)}, u32[]{:S(2)}) async-start(bf16[16,136,768]{2,1,0:T(8,128)(2,1)} %broadcast_in_dim.147), calls=%async_computation.1 | async-start | bytes 6684672 | tf_op jit(solution)/shard_map/all_to_all | solution.py:226
  147.3 94.1 %all-gather.8.cloned.1.call-done = bf16[2176,1792]{1,0:T(8,128)(2,1)} async-done(((bf16[136,1792]{1,0:T(8,128)(2,1)}), bf16[2176,1792]{1,0:T(8,128)(2,1)}) %all-gather.8.cloned.1.call-update) | async-done | bytes 7798800 | tf_op jit(solution)/shard_map/all_gather | solution.py:225
  241.9 16.9 %collective-permute-done.1 = bf16[2176,768]{1,0:T(8,128)(2,1)} collective-permute-done((bf16[2176,768]{1,0:T(8,128)(2,1)S(1)}, bf16[2176,768]{1,0:T(8,128)(2,1)}, u32[]{:S(2)}, u32[]{:S(2)}) %collective-permute-start.1) | collective-permute-done | bytes 3342368 | tf_op jit(solution)/shard_map/ppermute | solution.py:232
  258.8 3.3 fusion.61
  262.2 3.3 fusion.64
  265.5 2.5 fusion.56
  269.3 2.5 fusion.59
  273.1 5.9 %fusion.4 = f32[2176,216]{0,1:T(8,128)S(1)} fusion(f32[2176,216]{0,1:T(8,128)S(1)} %fusion.64, f32[2176,216]{0,1:T(8,128)S(1)} %convolution_add_fusion.1, bf16[2176,1792]{1,0:T(8,128)(2,1)} %collective-permute-done, bf16[5120,216]{0,1:T(8,128)(2,1)S(1)} %copy-done.6, s32[]{:T(128)S(6)} %select_n.79), kind=kOutput, calls=%fused_computation.17 | convolution fusion | flops 1685477376 | bytes 14213124 | tf_op jit(solution)/shard_map/dot_general | solution.py:239
  279.0 7.2 %multiply_convert_fusion = bf16[2176,216]{0,1:T(8,128)(2,1)} fusion(f32[2176,216]{0,1:T(8,128)S(1)} %fusion.4, f32[2176,216]{0,1:T(8,128)S(1)} %fusion.61, f32[2176,216]{0,1:T(8,128)S(1)} %convolution_add_fusion, bf16[2176,1792]{1,0:T(8,128)(2,1)} %collective-permute-done, bf16[5120,216]{0,1:T(8,128)(2,1)S(1)} %copy-done.9, s32[]{:T(128)S(6)} %select_n.79), kind=kOutput, calls=%fused_computation.32 | convolution fusion | flops 1688297472 | bytes 15153156 | tf_op jit(solution)/shard_map/dot_general | solution.py:239
  286.2 45.7 %all-gather.10.cloned.1.call-done = bf16[2176,1728]{0,1:T(8,128)(2,1)} async-done(((bf16[2176,216]{0,1:T(8,128)(2,1)}), bf16[2176,1728]{0,1:T(8,128)(2,1)}) %all-gather.10.cloned.1.call-update) | async-done | bytes 7520272 | tf_op jit(solution)/shard_map/all_gather | solution.py:248
  331.9 9.0 %convolution_convert_fusion.1 = bf16[2176,640]{1,0:T(8,128)(2,1)S(1)} fusion(bf16[2176,1728]{0,1:T(8,128)(2,1)} %all-gather.10.cloned.1.call-done, bf16[1728,640]{1,0:T(8,128)(2,1)S(1)} %copy-done.20), kind=kOutput, calls=%fused_computation.9 | convolution fusion | flops 4814356480 | bytes 12517376 | tf_op jit(solution)/shard_map/dot_general | solution.py:249
  340.9 43.0 %all_to_all.31 = bf16[16,136,640]{2,1,0:T(8,128)(2,1)S(1)} all-to-all(bf16[16,136,640]{2,1,0:T(8,128)(2,1)S(1)} %bitcast.186), channel_id=1, replica_groups=mesh['req'=16,'mlp'=8] {'req'}, dimensions={0} | all-to-all | bytes 5570560 | tf_op jit(solution)/shard_map/all_to_all | solution.py:250
  (112 shorter events, 22.9 us)
Async XLA Ops:
  6.5 12.3 %copy-start = (bf16[3,4096,128]{2,1,0:T(8,128)(2,1)S(1)}, bf16[3,4096,128]{2,1,0:T(8,128)(2,1)}, u32[]{:S(2)}) copy-start(bf16[3,4096,128]{2,1,0:T(8,128)(2,1)} %param.21) | copy-start | bytes 9437188
  6.5 55.5 %all-gather.12.cloned.1.call-start = ((), (), s32[]{:S(2)}) async-start(), calls=%async_computation.6 | async-start | bytes 3969024 | tf_op jit(solution)/shard_map/all_gather | solution.py:110
  10.7 7.4 %copy-start.12 = (bf16[3,5,128]{2,1,0:T(8,128)(2,1)}, bf16[3,5,128]{2,1,0:T(8,128)(2,1)S(1)}, u32[]{:S(2)}) copy-start(bf16[3,5,128]{2,1,0:T(8,128)(2,1)S(1)} %reshape.383) | copy-start | bytes 11524
  68.1 4.8 %copy-start.11 = (pred[3,1024]{1,0:T(4,128)(4,1)S(1)}, pred[3,1024]{1,0:T(4,128)(4,1)}, u32[]{:S(2)}) copy-start(pred[3,1024]{1,0:T(4,128)(4,1)} %iota_compare_fusion.2) | copy-start | bytes 9220
  68.1 4.8 %copy-start.13 = (bf16[3,5,128]{2,1,0:T(8,128)(2,1)S(1)}, bf16[3,5,128]{2,1,0:T(8,128)(2,1)}, u32[]{:S(2)}) copy-start(bf16[3,5,128]{2,1,0:T(8,128)(2,1)} %copy-done.12) | copy-start | bytes 11524
  68.2 5.1 %copy-start.14 = (f32[3,5]{1,0:T(4,128)S(1)}, f32[3,5]{1,0:T(4,128)}, u32[]{:S(2)}) copy-start(f32[3,5]{1,0:T(4,128)} %get-tuple-element.32) | copy-start | bytes 184
  68.2 5.1 %copy-start.17 = (f32[3,1,5]{2,1,0:T(1,128)S(1)}, f32[3,1,5]{2,1,0:T(1,128)}, u32[]{:S(2)}) copy-start(f32[3,1,5]{2,1,0:T(1,128)} %fusion.97) | copy-start | bytes 184
  70.3 5.0 %copy-start.16 = (f32[3,128]{1,0:T(4,128)S(1)}, f32[3,128]{1,0:T(4,128)}, u32[]{:S(2)}) copy-start(f32[3,128]{1,0:T(4,128)} %slice_convert_fusion) | copy-start | bytes 4612
  72.9 4.8 %copy-start.3 = (bf16[16,133,128]{2,1,0:T(8,128)(2,1)S(1)}, bf16[16,133,128]{2,1,0:T(8,128)(2,1)}, u32[]{:S(2)}) copy-start(bf16[16,133,128]{2,1,0:T(8,128)(2,1)} %get-tuple-element.8) | copy-start | bytes 1634308
  74.9 3.0 copy-start.4
  74.9 3.0 copy-start.5
  74.9 3.0 copy-start.15
  81.4 1.0 copy-start.8
  82.4 1.0 copy-start.7
  82.4 2.6 slice-start
  83.4 2.3 slice-start.1
  87.0 5.8 %copy-start.18 = (f32[640]{0:T(1024)S(1)}, f32[640]{0:T(1024)}, u32[]{:S(2)}) copy-start(f32[640]{0:T(1024)} %param.30) | copy-start | bytes 7684
  88.2 24.2 %copy-start.10 = (bf16[136,640]{1,0:T(8,128)(2,1)S(1)}, bf16[136,640]{1,0:T(8,128)(2,1)}, u32[]{:S(2)}) copy-start(bf16[136,640]{1,0:T(8,128)(2,1)} %param.17) | copy-start | bytes 522244
  88.2 24.0 %all-to-all-start = ((bf16[136,8,640]{2,0,1:T(8,128)(2,1)}), bf16[136,8,640]{2,0,1:T(8,128)(2,1)S(1)}, u32[]{:S(2)}, u32[]{:S(2)}) async-start(bf16[136,8,640]{2,0,1:T(8,128)(2,1)} %bitcast.168), calls=%async_computation | async-start | bytes 2785280 | tf_op jit(solution)/shard_map/all_to_all | solution.py:185
  92.6 42.2 %all-gather.6.cloned.1.call-start = ((), (), s32[]{:S(2)}) async-start(), calls=%async_computation.3 | async-start | bytes 1658880 | tf_op jit(solution)/shard_map/all_gather | solution.py:200
  113.2 128.2 %all-gather.8.cloned.1.call-start = ((), (), s32[]{:S(2)}) async-start(), calls=%async_computation.4 | async-start | bytes 8286208 | tf_op jit(solution)/shard_map/all_gather | solution.py:225
  134.7 2.1 copy-start.2
  140.2 101.2 %all-to-all-start.1 = ((bf16[16,136,768]{2,1,0:T(8,128)(2,1)}), bf16[16,136,768]{2,1,0:T(8,128)(2,1)S(1)}, u32[]{:S(2)}, u32[]{:S(2)}) async-start(bf16[16,136,768]{2,1,0:T(8,128)(2,1)} %broadcast_in_dim.147), calls=%async_computation.1 | async-start | bytes 6684672 | tf_op jit(solution)/shard_map/all_to_all | solution.py:226
  147.2 184.7 %all-gather.10.cloned.1.call-start = ((), (), s32[]{:S(2)}) async-start(), calls=%async_computation.5 | async-start | bytes 8460288 | tf_op jit(solution)/shard_map/all_gather | solution.py:248
  241.4 31.7 %collective-permute-start = (bf16[2176,1792]{1,0:T(8,128)(2,1)}, bf16[2176,1792]{1,0:T(8,128)(2,1)}, u32[]{:S(2)}, u32[]{:S(2)}) collective-permute-start(bf16[2176,1792]{1,0:T(8,128)(2,1)} %all-gather.8.cloned.1.call-done), channel_id=1, source_target_pairs={{0,1},{1,0},{2,3},{3,2},{4,5},{5,4},{6,7},{7,6},{8,9},{9,8},{10,11... | collective-permute-start | bytes 23396360 | tf_op jit(solution)/shard_map/ppermute | solution.py:232
  241.4 17.4 %collective-permute-start.1 = (bf16[2176,768]{1,0:T(8,128)(2,1)S(1)}, bf16[2176,768]{1,0:T(8,128)(2,1)}, u32[]{:S(2)}, u32[]{:S(2)}) collective-permute-start(bf16[2176,768]{1,0:T(8,128)(2,1)S(1)} %bitcast.172), channel_id=1, source_target_pairs={{0,1},{1,0},{2,3},{3,2},{4,5},{5,4},{6,7},{7,6},{8,9},{9,8},{10,11... | collective-permute-start | bytes 10027016 | tf_op jit(solution)/shard_map/ppermute | solution.py:232
  241.9 20.2 %copy-start.6 = (bf16[5120,216]{0,1:T(8,128)(2,1)S(1)}, bf16[5120,216]{0,1:T(8,128)(2,1)}, u32[]{:S(2)}) copy-start(bf16[5120,216]{0,1:T(8,128)(2,1)} %param.31) | copy-start | bytes 6635524
  258.8 6.7 %copy-start.19 = (bf16[2176,1792]{1,0:T(8,128)(2,1)S(1)}, bf16[2176,1792]{1,0:T(8,128)(2,1)}, u32[]{:S(2)}) copy-start(bf16[2176,1792]{1,0:T(8,128)(2,1)} %all-gather.8.cloned.1.call-done) | copy-start | bytes 23396356
  262.2 3.3 copy-start.9
  279.0 52.9 %copy-start.20 = (bf16[1728,640]{1,0:T(8,128)(2,1)S(1)}, bf16[1728,640]{1,0:T(8,128)(2,1)}, u32[]{:S(2)}) copy-start(bf16[1728,640]{1,0:T(8,128)(2,1)} %param.33) | copy-start | bytes 6635524
  340.9 44.1 %copy-start.1 = (bf16[3,4096,128]{2,1,0:T(8,128)(2,1)S(1)}, bf16[3,4096,128]{2,1,0:T(8,128)(2,1)}, u32[]{:S(2)}) copy-start(bf16[3,4096,128]{2,1,0:T(8,128)(2,1)} %param.21) | copy-start | bytes 9437188
Sparse Core Ops, SparseCore 0:
  9.5 52.4 all-gather.11
  113.3 21.4 all-gather.5
  138.4 102.9 all-gather.7
  286.3 45.5 all-gather.9

commit v4 on v2

--- a/solution.py
+++ b/solution.py
@@ -4,6 +4,7 @@
 import jax.numpy as jnp
 from jax import lax
 from jax.sharding import PartitionSpec as P
+
 
 D = 5120
 HQ = 40
@@ -68,6 +69,9 @@
             jnp.zeros((row_count, heads_kv, group_size, HD), jnp.float32),
         )
 
+    swap_with = [(i, i ^ 2) for i in range(lax.axis_size("mlp"))]
+    gate_other = lax.ppermute(gate_weight, "mlp", swap_with)
+    up_other = lax.ppermute(up_weight, "mlp", swap_with)
     past_keys = cache_keys.reshape(decode_count, cache_span, heads_kv, HD)
     past_values = cache_values.reshape(decode_count, cache_span, heads_kv, HD)
     scores = (
@@ -209,6 +213,9 @@
         own_half * lax.rsqrt(square_total / D + 1e-06)[:, None] * own_gain[None, :]
     ).astype(jnp.bfloat16)
     pairs = [(i, i ^ 1) for i in range(mlp_count)]
+    parity = (lax.axis_index("mlp") // 2) % 2
+    gate_pair = jnp.concatenate([gate_weight, gate_other], 1)
+    up_pair = jnp.concatenate([up_weight, up_other], 1)
 
     def halves(weight):
         return (
@@ -216,29 +223,40 @@
             lax.dynamic_slice_in_dim(weight, (1 - side) * half, half, axis=0),
         )
 
-    gate_near, gate_far = halves(gate_weight)
-    up_near, up_far = halves(up_weight)
-    chunk_count = 2
-    chunk_rows = rows_here // chunk_count
-    feeds = []
-    for chunk in range(chunk_count):
-        rows = normed[chunk * chunk_rows : (chunk + 1) * chunk_rows]
-        near_rows = lax.all_gather(rows, "req", axis=0, tiled=True)
-        far_rows = lax.ppermute(near_rows, "mlp", pairs)
-        gate_proj = jnp.dot(near_rows, gate_near, preferred_element_type=jnp.float32) + jnp.dot(
-            far_rows, gate_far, preferred_element_type=jnp.float32
-        )
-        up_proj = jnp.dot(near_rows, up_near, preferred_element_type=jnp.float32) + jnp.dot(
-            far_rows, up_far, preferred_element_type=jnp.float32
-        )
-        hidden = (jax.nn.silu(gate_proj) * up_proj).astype(jnp.bfloat16)
-        hidden_block = lax.all_gather(hidden, "mlp", axis=1, tiled=True)
-        down_partial = jnp.dot(hidden_block, down_weight, preferred_element_type=jnp.float32)
-        req_pieces = lax.all_to_all(down_partial.astype(jnp.bfloat16), "req", 0, 0, tiled=True)
-        feeds.append(
-            jnp.sum(req_pieces.reshape(req_count, chunk_rows, -1).astype(jnp.float32), axis=0)
-        )
-    feed = jnp.concatenate(feeds, 0)
+    row_half = rows_here // 2
+    my_rows = lax.dynamic_slice_in_dim(normed, parity * row_half, row_half, axis=0)
+    near_rows = lax.all_gather(my_rows, "req", axis=0, tiled=True)
+    far_rows = lax.ppermute(near_rows, "mlp", pairs)
+
+    def project(weight):
+        near_weight, far_weight = halves(weight)
+        return jnp.dot(near_rows, near_weight, preferred_element_type=jnp.float32) + jnp.dot(
+            far_rows, far_weight, preferred_element_type=jnp.float32
+        )
+
+    gate_proj = project(gate_pair)
+    up_proj = project(up_pair)
+    hidden = (jax.nn.silu(gate_proj) * up_proj).astype(jnp.bfloat16)
+    hidden_all = lax.all_gather(hidden, "mlp", axis=0, tiled=False)
+    unit = down_weight.shape[0] // mlp_count
+    down_units = down_weight.reshape(mlp_count, unit, -1)
+    partials = []
+    for which in range(2):
+        owners = [2 * which, 2 * which + 1, 2 * which + 4, 2 * which + 5]
+        pieces_in = jnp.concatenate(
+            [hidden_all[2 * which : 2 * which + 2], hidden_all[2 * which + 4 : 2 * which + 6]], 0
+        )
+        order = [unit_index for owner in owners for unit_index in (owner, owner ^ 2)]
+        weight_in = down_units[jnp.array(order)].reshape(len(owners), 2 * unit, -1)
+        partial = jnp.einsum(
+            "dik,dkn->in", pieces_in, weight_in, preferred_element_type=jnp.float32
+        )
+        partials.append(partial.astype(jnp.bfloat16).reshape(req_count, row_half, -1))
+    down_partial = jnp.concatenate(partials, 1).reshape(req_count * rows_here, -1)
+    req_pieces = lax.all_to_all(down_partial, "req", 0, 0, tiled=True)
+    feed = jnp.sum(
+        req_pieces.reshape(req_count, rows_here, -1).astype(jnp.float32), axis=0
+    )
     return (mixed_wide + feed).astype(jnp.bfloat16)
 
 

time: 401 us -> 448 us (1.12)
  blocking collectives: 0 us -> 43 us
  waiting for transfers between devices: 245 us -> 277 us
  matrix products: 62.1 us -> 43.1 us
  starting transfers between devices: 19.2 us -> 6.72 us
  local copies, waits for them, and re-layouts: 42.2 us -> 48 us
    ppermute x0 -> x2, waiting for transfers between devices: none -> 92.4 us  [the longest x1 47.2 us: per_device(): gate_other = lax.ppermute(gate_weight, 'mlp', swap_with)]
    all_to_all x0 -> x1, blocking collectives: none -> 43 us  [per_device(): req_pieces = lax.all_to_all(down_partial, 'req', 0, 0, tiled=True)]
    all_gather x4 -> x2, waiting for transfers between devices: 141 us -> 103 us  [the longest x1 59.7 us: per_device(): near_rows = lax.all_gather(my_rows, 'req', axis=0, tiled=True)]
    all_to_all x2 -> x0, waiting for transfers between devices: 21.8 us -> none  [per_device(): lax.all_to_all(down_partial.astype(jnp.bfloat16), 'req', 0, 0, tiled=True)]
    dot_general x10 -> x6, matrix products: 49.3 us -> 30.3 us  [the longest x2 11.6 us: per_device(): jnp.einsum('dik,dkn->in', pieces_in, weight_in, preferred_element_type=jn...]
    all_to_all x2 -> x0, starting transfers between devices: 14.2 us -> none  [per_device(): lax.all_to_all(down_partial.astype(jnp.bfloat16), 'req', 0, 0, tiled=True)]
    unnamed x60 -> x66, local copies, waits for them, and re-layouts: 18.1 us -> 11 us
    slice x0 -> x1, local copies, waits for them, and re-layouts: none -> 4.87 us  [per_device(): hidden_all[2 * which:2 * which + 2]]
  transfers between devices with their start and end apart: 11 -> 8, of which waited for: 8 -> 7; matrix products, arithmetic and copies ran while one was open for 20% -> 5% of each run, Pallas kernels for 0% -> 0%
where the time goes in v4:
time: 448 us; the launch traced here: 447 us
  waiting for transfers between devices  277 us (62%)
  local copies, waits for them, and re-layouts  48 us (11%)
  matrix products  43.1 us (10%)
  blocking collectives  43 us (10%)
  other arithmetic  15.1 us (3%)
  between operations  14.4 us (3%)
  starting transfers between devices  6.72 us (2%)
    all_gather x1, waiting for transfers between devices, per_device(): near_rows = lax.all_gather(my_rows, 'req', axis=0, tiled=True)  59.7 us
    ppermute x1, waiting for transfers between devices, per_device(): gate_other = lax.ppermute(gate_weight, 'mlp', swap_with)  47.2 us
    ppermute x1, waiting for transfers between devices, per_device(): up_other = lax.ppermute(up_weight, 'mlp', swap_with)  45.2 us
    all_gather x1, waiting for transfers between devices, per_device(): hidden_all = lax.all_gather(hidden, 'mlp', axis=0, tiled=False)  43 us
    all_to_all x1, blocking collectives, per_device(): req_pieces = lax.all_to_all(down_partial, 'req', 0, 0, tiled=True)  43 us
    all_gather x1, waiting for transfers between devices, per_device(): gathered = lax.all_gather(packed, 'req', axis=0, tiled=False)  40.6 us
    all_gather x1, waiting for transfers between devices, per_device(): lax.all_gather(with_gain, 'mlp', axis=1, tiled=True).astype(jnp.float32)  21.5 us
    all_to_all x1, waiting for transfers between devices, per_device(): lax.all_to_all(head_partial.astype(jnp.bfloat16), 'mlp', 1, 0, tiled=True)  19.3 us
  transfers between devices with their start and end apart: 8, of which 7 were waited for; matrix products, arithmetic and copies ran while one was open for 5% of the time, Pallas kernels for 0%

profile of v4, /device:TPU:0, one launch (start us, length us, event | category | flops | bytes accessed | tf_op | source)
XLA Modules:
  0.0 446.9 jit_solution(2891539405170704771)
XLA Ops:
  6.5 1.8 pad_maximum_fusion.1
  18.9 2.3 fusion.128
  21.4 40.6 %all-gather.11.cloned.1.call-done = bf16[14592,128]{1,0:T(8,128)(2,1)} async-done(((bf16[912,128]{1,0:T(8,128)(2,1)}), bf16[14592,128]{1,0:T(8,128)(2,1)}) %all-gather.11.cloned.1.call-update) | async-done | bytes 3735568 | tf_op jit(solution)/shard_map/all_gather | solution.py:114
  62.0 1.9 fusion.124
  63.9 2.6 fusion.123
  70.4 1.7 gather_fusion.1
  72.0 2.1 gather_fusion.2
  74.2 1.6 fusion.129
  76.6 2.5 fusion.67
  90.6 4.4 all-to-all-start
  95.3 19.3 %all-to-all-done = bf16[136,8,640]{2,0,1:T(8,128)(2,1)S(1)} async-done(((bf16[136,8,640]{2,0,1:T(8,128)(2,1)}), bf16[136,8,640]{2,0,1:T(8,128)(2,1)S(1)}, u32[]{:S(2)}, u32[]{:S(2)}) %all-to-all-start) | async-done | bytes 1392672 | tf_op jit(solution)/shard_map/all_to_all | solution.py:189
  115.7 21.5 %all-gather.9.cloned.1.call-done = bf16[139,5120]{1,0:T(8,128)(2,1)} async-done(((bf16[139,640]{1,0:T(8,128)(2,1)}), bf16[139,5120]{1,0:T(8,128)(2,1)}) %all-gather.9.cloned.1.call-update) | async-done | bytes 1423376 | tf_op jit(solution)/shard_map/all_gather | solution.py:204
  137.2 1.8 convert_element_type.91
  140.8 59.7 %all-gather.13.cloned.1.call-done = bf16[16,68,2560]{2,1,0:T(8,128)(2,1)} async-done(((bf16[1,68,2560]{2,1,0:T(8,128)(2,1)}), bf16[16,68,2560]{2,1,0:T(8,128)(2,1)}) %all-gather.13.cloned.1.call-update) | async-done | bytes 5570576 | tf_op jit(solution)/shard_map/all_gather | solution.py:228
  200.5 7.9 %reshape.472 = bf16[1088,2560]{1,0:T(8,128)(2,1)} reshape(bf16[16,68,2560]{2,1,0:T(8,128)(2,1)} %all-gather.13.cloned.1.call-done) | data formatting | bytes 11141120
  212.2 47.2 %collective-permute-done = bf16[5120,216]{0,1:T(8,128)(2,1)} collective-permute-done((bf16[5120,216]{0,1:T(8,128)(2,1)S(1)}, bf16[5120,216]{0,1:T(8,128)(2,1)}, u32[]{:S(2)}, u32[]{:S(2)}) %collective-permute-start) | collective-permute-done | bytes 2211872 | tf_op jit(solution)/shard_map/ppermute | solution.py:73
  259.4 1.8 constant_dynamic-update-slice_fusion
  261.2 45.2 %collective-permute-done.2 = bf16[5120,216]{0,1:T(8,128)(2,1)} collective-permute-done((bf16[5120,216]{0,1:T(8,128)(2,1)}, bf16[5120,216]{0,1:T(8,128)(2,1)}, u32[]{:S(2)}, u32[]{:S(2)}) %collective-permute-start.2) | collective-permute-done | bytes 2211872 | tf_op jit(solution)/shard_map/ppermute | solution.py:74
  306.4 1.9 constant_dynamic-update-slice_fusion.2
  308.3 5.7 %fusion.34 = f32[1088,432]{0,1:T(8,128)S(1)} fusion(bf16[1088,2560]{1,0:T(8,128)(2,1)} %collective-permute-done.1, bf16[5120,432]{0,1:T(8,128)(2,1)S(1)} %constant_dynamic-update-slice_fusion, s32[]{:T(128)S(6)} %select_n.99), kind=kOutput, calls=%fused_computation.43 | convolution fusion | flops 2406481920 | bytes 9662468 | tf_op jit(solution)/shard_map/dot_general | solution.py:233
  314.1 3.1 convolution_add_fusion.1
  317.2 5.6 %fusion.31 = f32[1088,432]{0,1:T(8,128)S(1)} fusion(bf16[1088,2560]{1,0:T(8,128)(2,1)} %collective-permute-done.1, bf16[5120,432]{0,1:T(8,128)(2,1)S(1)} %constant_dynamic-update-slice_fusion.2, s32[]{:T(128)S(6)} %select_n.99), kind=kOutput, calls=%fused_computation.40 | convolution fusion | flops 2406481920 | bytes 9662468 | tf_op jit(solution)/shard_map/dot_general | solution.py:233
  322.9 4.2 fusion.77
  327.2 2.2 gather_fusion.3
  329.4 2.2 gather_fusion.4
  331.7 43.0 %all-gather.15.cloned.1.call-done = bf16[8,1088,432]{1,2,0:T(8,128)(2,1)} async-done(((bf16[1,1088,432]{1,2,0:T(8,128)(2,1)}), bf16[8,1088,432]{1,2,0:T(8,128)(2,1)}) %all-gather.15.cloned.1.call-update) | async-done | bytes 7520272 | tf_op jit(solution)/shard_map/all_gather | solution.py:240
  374.7 4.9 %fusion.122 = (bf16[2,1088,432]{1,2,0:T(8,128)(2,1)S(1)}, bf16[2,1088,432]{1,2,0:T(8,128)(2,1)}, bf16[2,1088,432]{1,2,0:T(8,128)(2,1)S(1)}, bf16[2,1088,432]{1,2,0:T(8,128)(2,1)}) fusion(bf16[8,1088,432]{1,2,0:T(8,128)(2,1)} %all-gather.15.cloned.1.call-done), kind=kLoop, calls=%fused_computation.157 | loop fusion | bytes 15040512 | tf_op jit(solution)/shard_map/slice | solution.py:247
  379.6 4.4 fusion.17
  384.0 2.2 reshape.411
  386.2 7.2 %fusion.20 = bf16[1088,640]{1,0:T(8,128)(2,1)} fusion(bf16[4,432,640]{2,1,0:T(8,128)(2,1)} %bitcast.196, bf16[2,1088,432]{1,2,0:T(8,128)(2,1)} %get-tuple-element.10, bf16[2,1088,432]{1,2,0:T(8,128)(2,1)} %get-tuple-element.8), kind=kOutput, calls=%fused_computation.24 | convolution fusion | flops 2409058304 | bytes 7364608 | tf_op jit(solution)/shard_map/dik,dkn->in/dot_general | solution.py:251
  393.4 2.2 reshape.413
  396.2 43.0 %all_to_all.19 = bf16[16,136,640]{2,1,0:T(8,128)(2,1)S(1)} all-to-all(bf16[16,136,640]{2,1,0:T(8,128)(2,1)S(1)} %pad_maximum_fusion), channel_id=1, replica_groups=mesh['req'=16,'mlp'=8] {'req'}, dimensions={0} | all-to-all | bytes 5570560 | tf_op jit(solution)/shard_map/all_to_all | solution.py:256
  (134 shorter events, 34.7 us)
Async XLA Ops:
  6.5 12.3 %copy-start = (bf16[3,4096,128]{2,1,0:T(8,128)(2,1)S(1)}, bf16[3,4096,128]{2,1,0:T(8,128)(2,1)}, u32[]{:S(2)}) copy-start(bf16[3,4096,128]{2,1,0:T(8,128)(2,1)} %param.23) | copy-start | bytes 9437188
  6.5 55.5 %all-gather.11.cloned.1.call-start = ((), (), s32[]{:S(2)}) async-start(), calls=%async_computation.3 | async-start | bytes 3969024 | tf_op jit(solution)/shard_map/all_gather | solution.py:114
  10.1 8.1 %copy-start.17 = (bf16[3,5,128]{2,1,0:T(8,128)(2,1)}, bf16[3,5,128]{2,1,0:T(8,128)(2,1)S(1)}, u32[]{:S(2)}) copy-start(bf16[3,5,128]{2,1,0:T(8,128)(2,1)S(1)} %reshape.395) | copy-start | bytes 11524
  68.4 2.0 copy-start.4
  68.4 5.8 %copy-start.16 = (pred[3,1024]{1,0:T(4,128)(4,1)S(1)}, pred[3,1024]{1,0:T(4,128)(4,1)}, u32[]{:S(2)}) copy-start(pred[3,1024]{1,0:T(4,128)(4,1)} %iota_compare_fusion.2) | copy-start | bytes 9220
  68.4 5.8 %copy-start.18 = (bf16[3,5,128]{2,1,0:T(8,128)(2,1)S(1)}, bf16[3,5,128]{2,1,0:T(8,128)(2,1)}, u32[]{:S(2)}) copy-start(bf16[3,5,128]{2,1,0:T(8,128)(2,1)} %copy-done.17) | copy-start | bytes 11524
  69.6 6.2 %copy-start.19 = (f32[3,5]{1,0:T(4,128)S(1)}, f32[3,5]{1,0:T(4,128)}, u32[]{:S(2)}) copy-start(f32[3,5]{1,0:T(4,128)} %get-tuple-element.36) | copy-start | bytes 184
  69.6 6.2 %copy-start.22 = (f32[3,1,5]{2,1,0:T(1,128)S(1)}, f32[3,1,5]{2,1,0:T(1,128)}, u32[]{:S(2)}) copy-start(f32[3,1,5]{2,1,0:T(1,128)} %fusion.109) | copy-start | bytes 184
  70.4 6.2 %copy-start.21 = (f32[3,128]{1,0:T(4,128)S(1)}, f32[3,128]{1,0:T(4,128)}, u32[]{:S(2)}) copy-start(f32[3,128]{1,0:T(4,128)} %slice_convert_fusion) | copy-start | bytes 4612
  74.2 4.9 %copy-start.6 = (bf16[16,133,128]{2,1,0:T(8,128)(2,1)S(1)}, bf16[16,133,128]{2,1,0:T(8,128)(2,1)}, u32[]{:S(2)}) copy-start(bf16[16,133,128]{2,1,0:T(8,128)(2,1)} %get-tuple-element.12) | copy-start | bytes 1634308
  76.3 3.0 copy-start.5
  76.6 3.7 copy-start.10
  84.8 2.6 slice-start
  85.8 2.3 slice-start.1
  89.4 5.9 %copy-start.23 = (f32[640]{0:T(1024)S(1)}, f32[640]{0:T(1024)}, u32[]{:S(2)}) copy-start(f32[640]{0:T(1024)} %param.32) | copy-start | bytes 7684
  90.6 24.2 %copy-start.15 = (bf16[136,640]{1,0:T(8,128)(2,1)S(1)}, bf16[136,640]{1,0:T(8,128)(2,1)}, u32[]{:S(2)}) copy-start(bf16[136,640]{1,0:T(8,128)(2,1)} %param.19) | copy-start | bytes 522244
  90.6 24.0 %all-to-all-start = ((bf16[136,8,640]{2,0,1:T(8,128)(2,1)}), bf16[136,8,640]{2,0,1:T(8,128)(2,1)S(1)}, u32[]{:S(2)}, u32[]{:S(2)}) async-start(bf16[136,8,640]{2,0,1:T(8,128)(2,1)} %bitcast.177), calls=%async_computation | async-start | bytes 2785280 | tf_op jit(solution)/shard_map/all_to_all | solution.py:189
  95.0 42.2 %all-gather.9.cloned.1.call-start = ((), (), s32[]{:S(2)}) async-start(), calls=%async_computation.2 | async-start | bytes 1658880 | tf_op jit(solution)/shard_map/all_gather | solution.py:204
  115.6 84.9 %all-gather.13.cloned.1.call-start = ((), (), s32[]{:S(2)}) async-start(), calls=%async_computation.4 | async-start | bytes 6266880 | tf_op jit(solution)/shard_map/all_gather | solution.py:228
  137.2 2.2 copy-start.2
  140.8 67.6 %copy-start.7 = (bf16[5120,216]{0,1:T(8,128)(2,1)S(1)}, bf16[5120,216]{0,1:T(8,128)(2,1)}, u32[]{:S(2)}) copy-start(bf16[5120,216]{0,1:T(8,128)(2,1)} %param.33) | copy-start | bytes 6635524
  140.8 233.9 %all-gather.15.cloned.1.call-start = ((), (), s32[]{:S(2)}) async-start(), calls=%async_computation.5 | async-start | bytes 8957952 | tf_op jit(solution)/shard_map/all_gather | solution.py:240
  208.4 99.9 %collective-permute-start.1 = (bf16[1088,2560]{1,0:T(8,128)(2,1)}, bf16[1088,2560]{1,0:T(8,128)(2,1)}, u32[]{:S(2)}, u32[]{:S(2)}) collective-permute-start(bf16[1088,2560]{1,0:T(8,128)(2,1)} %reshape.472), channel_id=1, source_target_pairs={{0,1},{1,0},{2,3},{3,2},{4,5},{5,4},{6,7},{7,6},{8,9},{9,8},{10,11... | collective-permute-start | bytes 16711688 | tf_op jit(solution)/shard_map/ppermute | solution.py:229
  208.4 51.1 %collective-permute-start = (bf16[5120,216]{0,1:T(8,128)(2,1)S(1)}, bf16[5120,216]{0,1:T(8,128)(2,1)}, u32[]{:S(2)}, u32[]{:S(2)}) collective-permute-start(bf16[5120,216]{0,1:T(8,128)(2,1)S(1)} %copy-done.7), channel_id=1, source_target_pairs={{0,2},{1,3},{2,0},{3,1},{4,6},{5,7},{6,4},{7,5},{8,10},{9,11},{10,... | collective-permute-start | bytes 6635528 | tf_op jit(solution)/shard_map/ppermute | solution.py:73
  209.8 96.5 %collective-permute-start.2 = (bf16[5120,216]{0,1:T(8,128)(2,1)}, bf16[5120,216]{0,1:T(8,128)(2,1)}, u32[]{:S(2)}, u32[]{:S(2)}) collective-permute-start(bf16[5120,216]{0,1:T(8,128)(2,1)} %param.34), channel_id=1, source_target_pairs={{0,2},{1,3},{2,0},{3,1},{4,6},{5,7},{6,4},{7,5},{8,10},{9,11},{10,... | collective-permute-start | bytes 6635528 | tf_op jit(solution)/shard_map/ppermute | solution.py:74
  306.4 7.7 %slice-start.2 = ((s8[5570560]{0:T(1024)(128)(4,1)}), s8[4194304]{0:T(1024)(128)(4,1)S(1)}, s32[]{:S(2)}) async-start(s8[5570560]{0:T(1024)(128)(4,1)} %bitcast.189), calls=%async_computation.8 | async-start | bytes 8388608
  308.3 5.8 %slice-start.3 = ((s8[5570560]{0:T(1024)(128)(4,1)}), s8[1376256]{0:T(1024)(128)(4,1)S(1)}, s32[]{:S(2)}) async-start(s8[5570560]{0:T(1024)(128)(4,1)} %bitcast.189), calls=%async_computation.9 | async-start | bytes 2752512
  322.9 4.3 copy-start.24
  322.9 4.3 copy-start.25
  322.9 4.3 copy-start.3
  331.7 47.9 %copy-start.9 = (bf16[8,216,640]{2,1,0:T(8,128)(2,1)S(1)}, bf16[8,216,640]{2,1,0:T(8,128)(2,1)}, u32[]{:S(2)}) copy-start(bf16[8,216,640]{2,1,0:T(8,128)(2,1)} %gather_fusion.3) | copy-start | bytes 6635524
  396.2 44.1 %copy-start.1 = (bf16[3,4096,128]{2,1,0:T(8,128)(2,1)S(1)}, bf16[3,4096,128]{2,1,0:T(8,128)(2,1)}, u32[]{:S(2)}) copy-start(bf16[3,4096,128]{2,1,0:T(8,128)(2,1)} %param.23) | copy-start | bytes 9437188
  (6 other events, 7.7 us)
Sparse Core Ops, SparseCore 0:
  9.5 52.4 all-gather.10
  115.7 21.4 all-gather.8
  140.9 59.5 all-gather.12
  327.3 47.3 all-gather.14

commit v5 on v4

--- a/solution.py
+++ b/solution.py
@@ -225,35 +225,36 @@
 
     row_half = rows_here // 2
     my_rows = lax.dynamic_slice_in_dim(normed, parity * row_half, row_half, axis=0)
-    near_rows = lax.all_gather(my_rows, "req", axis=0, tiled=True)
+    near_rows = lax.all_gather(my_rows, "req", axis=0, tiled=False)
     far_rows = lax.ppermute(near_rows, "mlp", pairs)
 
     def project(weight):
         near_weight, far_weight = halves(weight)
-        return jnp.dot(near_rows, near_weight, preferred_element_type=jnp.float32) + jnp.dot(
-            far_rows, far_weight, preferred_element_type=jnp.float32
-        )
+        return jnp.einsum(
+            "rik,kn->rin", near_rows, near_weight, preferred_element_type=jnp.float32
+        ) + jnp.einsum("rik,kn->rin", far_rows, far_weight, preferred_element_type=jnp.float32)
 
     gate_proj = project(gate_pair)
     up_proj = project(up_pair)
     hidden = (jax.nn.silu(gate_proj) * up_proj).astype(jnp.bfloat16)
     hidden_all = lax.all_gather(hidden, "mlp", axis=0, tiled=False)
     unit = down_weight.shape[0] // mlp_count
-    down_units = down_weight.reshape(mlp_count, unit, -1)
-    partials = []
-    for which in range(2):
-        owners = [2 * which, 2 * which + 1, 2 * which + 4, 2 * which + 5]
-        pieces_in = jnp.concatenate(
-            [hidden_all[2 * which : 2 * which + 2], hidden_all[2 * which + 4 : 2 * which + 6]], 0
-        )
-        order = [unit_index for owner in owners for unit_index in (owner, owner ^ 2)]
-        weight_in = down_units[jnp.array(order)].reshape(len(owners), 2 * unit, -1)
-        partial = jnp.einsum(
-            "dik,dkn->in", pieces_in, weight_in, preferred_element_type=jnp.float32
-        )
-        partials.append(partial.astype(jnp.bfloat16).reshape(req_count, row_half, -1))
-    down_partial = jnp.concatenate(partials, 1).reshape(req_count * rows_here, -1)
-    req_pieces = lax.all_to_all(down_partial, "req", 0, 0, tiled=True)
+    hidden_all = hidden_all.reshape(2, 2, 2, req_count, row_half, 2 * unit)
+    down_units = down_weight.reshape(2, 2, 2, unit, -1)
+    down_units = jnp.transpose(down_units, (0, 2, 1, 3, 4))
+    down_stack = jnp.stack(
+        [
+            down_units.reshape(2, 2, 2 * unit, -1),
+            down_units[:, :, ::-1].reshape(2, 2, 2 * unit, -1),
+        ],
+        0,
+    )
+    down_partial = jnp.einsum(
+        "aqcrik,qacko->rqio", hidden_all, down_stack, preferred_element_type=jnp.float32
+    ).astype(jnp.bfloat16)
+    req_pieces = lax.all_to_all(
+        down_partial.reshape(req_count * rows_here, -1), "req", 0, 0, tiled=True
+    )
     feed = jnp.sum(
         req_pieces.reshape(req_count, rows_here, -1).astype(jnp.float32), axis=0
     )

time: 448 us -> 459 us (1.025); the launches traced: 447 us -> 450 us
  starting transfers between devices: 6.72 us -> 17.5 us
  local copies, waits for them, and re-layouts: 48 us -> 38.8 us
  matrix products: 43.1 us -> 51.2 us
  waiting for transfers between devices: 277 us -> 271 us
    all_gather x1, starting transfers between devices: 0.22 us -> 11 us  [per_device(): lax.all_gather(with_gain, 'mlp', axis=1, tiled=True).astype(jnp.float32)]
    all_to_all x1, waiting for transfers between devices: 19.3 us -> 8.51 us  [per_device(): lax.all_to_all(head_partial.astype(jnp.bfloat16), 'mlp', 1, 0, tiled=True)]
    dot_general x6 -> x5, matrix products: 30.3 us -> 38.4 us  [the longest x1 19.1 us: per_device(): jnp.einsum('aqcrik,qacko->rqio', hidden_all, down_stack, preferred_elemen...]
    unnamed x66 -> x55, local copies, waits for them, and re-layouts: 11 us -> 3.31 us
    all_gather x0 -> x1, local copies, waits for them, and re-layouts: none -> 6.81 us  [per_device(): near_rows = lax.all_gather(my_rows, 'req', axis=0, tiled=False)]
    all_gather x1, waiting for transfers between devices: 43 us -> 48.2 us  [per_device(): hidden_all = lax.all_gather(hidden, 'mlp', axis=0, tiled=False)]
    slice x1 -> x0, local copies, waits for them, and re-layouts: 4.87 us -> none  [per_device(): hidden_all[2 * which:2 * which + 2]]
where the time goes in v5:
time: 459 us; the launch traced here: 450 us
  waiting for transfers between devices  271 us (59%)
  matrix products  51.2 us (11%)
  blocking collectives  43 us (9%)
  local copies, waits for them, and re-layouts  38.8 us (8%)
  starting transfers between devices  17.5 us (4%)
  between operations  14.7 us (3%)
  other arithmetic  14.5 us (3%)
    all_gather x1, waiting for transfers between devices, per_device(): near_rows = lax.all_gather(my_rows, 'req', axis=0, tiled=False)  59.7 us
    all_gather x1, waiting for transfers between devices, per_device(): hidden_all = lax.all_gather(hidden, 'mlp', axis=0, tiled=False)  48.2 us
    ppermute x1, waiting for transfers between devices, per_device(): gate_other = lax.ppermute(gate_weight, 'mlp', swap_with)  46.9 us
    ppermute x1, waiting for transfers between devices, per_device(): up_other = lax.ppermute(up_weight, 'mlp', swap_with)  45.2 us
    all_to_all x1, blocking collectives, per_device(): lax.all_to_all(down_partial.reshape(req_count * rows_here, -1), 'req', 0,...  43 us
    all_gather x1, waiting for transfers between devices, per_device(): gathered = lax.all_gather(packed, 'req', axis=0, tiled=False)  40.7 us
    all_gather x1, waiting for transfers between devices, per_device(): lax.all_gather(with_gain, 'mlp', axis=1, tiled=True).astype(jnp.float32)  21.5 us
    dot_general x1, matrix products, per_device(): jnp.einsum('aqcrik,qacko->rqio', hidden_all, down_stack, preferred_elemen...  19.1 us
  transfers between devices with their start and end apart: 8, of which 7 were waited for; matrix products, arithmetic and copies ran while one was open for 5% of the time, Pallas kernels for 0%

profile of v5, /device:TPU:0, one launch (start us, length us, event | category | flops | bytes accessed | tf_op | source)
XLA Modules:
  0.0 450.4 jit_solution(15610069988084236145)
XLA Ops:
  6.5 1.8 pad_maximum_fusion
  18.9 2.3 fusion.121
  21.4 40.7 %all-gather.11.cloned.1.call-done = bf16[14592,128]{1,0:T(8,128)(2,1)} async-done(((bf16[912,128]{1,0:T(8,128)(2,1)}), bf16[14592,128]{1,0:T(8,128)(2,1)}) %all-gather.11.cloned.1.call-update) | async-done | bytes 3735568 | tf_op jit(solution)/shard_map/all_gather | solution.py:114
  62.1 1.9 fusion.116
  63.9 2.6 fusion.115
  70.3 1.7 gather_fusion.1
  72.0 2.1 gather_fusion.2
  74.2 1.6 fusion.122
  76.6 2.5 fusion.64
  82.3 1.4 fusion.2
  90.6 4.4 all-to-all-start
  95.0 11.0 %all-gather.9.cloned.1.call-start = ((), (), s32[]{:S(2)}) async-start(), calls=%async_computation.2 | async-start | bytes 1658880 | tf_op jit(solution)/shard_map/all_gather | solution.py:204
  106.1 8.5 %all-to-all-done = bf16[136,8,640]{2,0,1:T(8,128)(2,1)S(1)} async-done(((bf16[136,8,640]{2,0,1:T(8,128)(2,1)}), bf16[136,8,640]{2,0,1:T(8,128)(2,1)S(1)}, u32[]{:S(2)}, u32[]{:S(2)}) %all-to-all-start) | async-done | bytes 1392672 | tf_op jit(solution)/shard_map/all_to_all | solution.py:189
  115.7 21.5 %all-gather.9.cloned.1.call-done = bf16[139,5120]{1,0:T(8,128)(2,1)} async-done(((bf16[139,640]{1,0:T(8,128)(2,1)}), bf16[139,5120]{1,0:T(8,128)(2,1)}) %all-gather.9.cloned.1.call-update) | async-done | bytes 1423376 | tf_op jit(solution)/shard_map/all_gather | solution.py:204
  137.1 1.8 convert_element_type.91
  140.8 59.7 %all-gather.15.cloned.1.call-done = bf16[16,68,2560]{2,1,0:T(8,128)(2,1)} async-done(((bf16[1,68,2560]{2,1,0:T(8,128)(2,1)}), bf16[16,68,2560]{2,1,0:T(8,128)(2,1)}) %all-gather.15.cloned.1.call-update) | async-done | bytes 5570576 | tf_op jit(solution)/shard_map/all_gather | solution.py:228
  200.5 6.8 %copy.54 = bf16[16,68,2560]{2,0,1:T(8,128)(2,1)} copy(bf16[16,68,2560]{2,1,0:T(8,128)(2,1)} %all-gather.15.cloned.1.call-done) | data formatting | bytes 11141120 | tf_op jit(solution)/shard_map/all_gather | solution.py:228
  207.3 1.5 collective-permute-start
  209.5 1.9 constant_dynamic-update-slice_fusion.3
  211.4 46.9 %collective-permute-done = bf16[5120,216]{0,1:T(8,128)(2,1)} collective-permute-done((bf16[5120,216]{0,1:T(8,128)(2,1)S(1)}, bf16[5120,216]{0,1:T(8,128)(2,1)}, u32[]{:S(2)}, u32[]{:S(2)}) %collective-permute-start) | collective-permute-done | bytes 2211872 | tf_op jit(solution)/shard_map/ppermute | solution.py:73
  258.4 1.8 constant_dynamic-update-slice_fusion
  260.1 45.2 %collective-permute-done.2 = bf16[5120,216]{0,1:T(8,128)(2,1)} collective-permute-done((bf16[5120,216]{0,1:T(8,128)(2,1)}, bf16[5120,216]{0,1:T(8,128)(2,1)}, u32[]{:S(2)}, u32[]{:S(2)}) %collective-permute-start.2) | collective-permute-done | bytes 2211872 | tf_op jit(solution)/shard_map/ppermute | solution.py:74
  305.3 1.8 constant_dynamic-update-slice_fusion.2
  307.1 3.3 fusion.24
  310.4 5.1 %fusion.22 = f32[16,68,432]{2,0,1:T(8,128)S(1)} fusion(bf16[16,68,2560]{2,0,1:T(8,128)(2,1)} %collective-permute-done.1, bf16[5120,432]{0,1:T(8,128)(2,1)S(1)} %constant_dynamic-update-slice_fusion, s32[]{:T(128)S(6)} %select_n.93), kind=kOutput, calls=%fused_computation.38 | convolution fusion | flops 2406481920 | bytes 9662468 | tf_op jit(solution)/shard_map/rik,kn->rin/dot_general | solution.py:235
  315.5 5.1 %fusion.18 = f32[16,68,432]{2,0,1:T(8,128)S(1)} fusion(bf16[16,68,2560]{2,0,1:T(8,128)(2,1)} %collective-permute-done.1, bf16[5120,432]{0,1:T(8,128)(2,1)S(1)} %constant_dynamic-update-slice_fusion.2, s32[]{:T(128)S(6)} %select_n.93), kind=kOutput, calls=%fused_computation.34 | convolution fusion | flops 2406481920 | bytes 9662468 | tf_op jit(solution)/shard_map/rik,kn->rin/dot_general | solution.py:235
  320.5 5.9 %fusion.17 = bf16[16,68,432]{2,1,0:T(8,128)(2,1)S(1)} fusion(f32[16,68,432]{2,0,1:T(8,128)S(1)} %fusion.18, f32[16,68,432]{2,1,0:T(8,128)S(1)} %fusion.24, f32[16,68,432]{2,0,1:T(8,128)S(1)} %fusion.22, bf16[16,68,2560]{2,1,0:T(8,128)(2,1)S(1)} %bitcast.213, bf16[5120,432]{0,1:T(8,128)(2,1)S(1)} %constant_dynamic-update-slice_fusion.2, s32[]{:T(128)S(6)} %select_n.89), kind=kOutput, calls=%fused_computation.32 | convolution fusion | flops 2410242048 | bytes 15865860 | tf_op jit(solution)/shard_map/rik,kn->rin/dot_general | solution.py:233
  327.8 1.8 copy.123
  329.6 1.6 rev.3
  331.2 48.2 %all-gather.13.cloned.1.call-done = bf16[128,68,432]{2,0,1:T(8,128)(2,1)} async-done(((bf16[16,68,432]{2,0,1:T(8,128)(2,1)}), bf16[128,68,432]{2,0,1:T(8,128)(2,1)}) %all-gather.13.cloned.1.call-update) | async-done | bytes 7520272 | tf_op jit(solution)/shard_map/all_gather | solution.py:240
  379.3 19.1 %fusion.13 = bf16[16,2,68,640]{3,2,0,1:T(8,128)(2,1)S(1)} fusion(bf16[2,2,2,16,68,432]{5,3,2,1,0,4:T(8,128)(2,1)} %bitcast.229, bf16[1,2,2,432,640]{4,3,2,1,0:T(8,128)(2,1)} %bitcast.220, bf16[1,2,2,432,640]{4,3,2,1,0:T(8,128)(2,1)S(1)} %bitcast.207), kind=kOutput, calls=%fused_computation.22 | convolution fusion | flops 4823203840 | bytes 14729216 | tf_op jit(solution)/shard_map/aqcrik,qacko->rqio/dot_general | solution.py:252
  399.4 43.0 %all_to_all.22 = bf16[16,136,640]{2,1,0:T(8,128)(2,1)S(1)} all-to-all(bf16[16,136,640]{2,1,0:T(8,128)(2,1)S(1)} %copy.60), channel_id=1, replica_groups=mesh['req'=16,'mlp'=8] {'req'}, dimensions={0} | all-to-all | bytes 5570560 | tf_op jit(solution)/shard_map/all_to_all | solution.py:255
  (121 shorter events, 31.5 us)
Async XLA Ops:
  6.5 12.3 %copy-start = (bf16[3,4096,128]{2,1,0:T(8,128)(2,1)S(1)}, bf16[3,4096,128]{2,1,0:T(8,128)(2,1)}, u32[]{:S(2)}) copy-start(bf16[3,4096,128]{2,1,0:T(8,128)(2,1)} %param.21) | copy-start | bytes 9437188
  6.5 55.5 %all-gather.11.cloned.1.call-start = ((), (), s32[]{:S(2)}) async-start(), calls=%async_computation.3 | async-start | bytes 3969024 | tf_op jit(solution)/shard_map/all_gather | solution.py:114
  10.1 8.0 %copy-start.14 = (bf16[3,5,128]{2,1,0:T(8,128)(2,1)}, bf16[3,5,128]{2,1,0:T(8,128)(2,1)S(1)}, u32[]{:S(2)}) copy-start(bf16[3,5,128]{2,1,0:T(8,128)(2,1)S(1)} %reshape.386) | copy-start | bytes 11524
  68.4 1.9 copy-start.3
  68.4 5.8 %copy-start.13 = (pred[3,1024]{1,0:T(4,128)(4,1)S(1)}, pred[3,1024]{1,0:T(4,128)(4,1)}, u32[]{:S(2)}) copy-start(pred[3,1024]{1,0:T(4,128)(4,1)} %iota_compare_fusion.2) | copy-start | bytes 9220
  68.4 5.8 %copy-start.15 = (bf16[3,5,128]{2,1,0:T(8,128)(2,1)S(1)}, bf16[3,5,128]{2,1,0:T(8,128)(2,1)}, u32[]{:S(2)}) copy-start(bf16[3,5,128]{2,1,0:T(8,128)(2,1)} %copy-done.14) | copy-start | bytes 11524
  69.6 6.2 %copy-start.16 = (f32[3,5]{1,0:T(4,128)S(1)}, f32[3,5]{1,0:T(4,128)}, u32[]{:S(2)}) copy-start(f32[3,5]{1,0:T(4,128)} %get-tuple-element.34) | copy-start | bytes 184
  69.6 6.2 %copy-start.19 = (f32[3,1,5]{2,1,0:T(1,128)S(1)}, f32[3,1,5]{2,1,0:T(1,128)}, u32[]{:S(2)}) copy-start(f32[3,1,5]{2,1,0:T(1,128)} %fusion.103) | copy-start | bytes 184
  70.3 6.2 %copy-start.18 = (f32[3,128]{1,0:T(4,128)S(1)}, f32[3,128]{1,0:T(4,128)}, u32[]{:S(2)}) copy-start(f32[3,128]{1,0:T(4,128)} %slice_convert_fusion) | copy-start | bytes 4612
  74.2 4.9 %copy-start.5 = (bf16[16,133,128]{2,1,0:T(8,128)(2,1)S(1)}, bf16[16,133,128]{2,1,0:T(8,128)(2,1)}, u32[]{:S(2)}) copy-start(bf16[16,133,128]{2,1,0:T(8,128)(2,1)} %get-tuple-element.8) | copy-start | bytes 1634308
  76.3 3.0 copy-start.4
  76.5 3.7 copy-start.7
  80.3 1.4 copy-start.8
  80.3 1.4 copy-start.9
  80.3 1.4 copy-start.17
  84.8 1.0 copy-start.10
  84.8 2.6 slice-start
  85.8 2.3 slice-start.1
  89.3 16.7 %copy-start.20 = (f32[640]{0:T(1024)S(1)}, f32[640]{0:T(1024)}, u32[]{:S(2)}) copy-start(f32[640]{0:T(1024)} %param.30) | copy-start | bytes 7684
  90.6 24.2 %copy-start.12 = (bf16[136,640]{1,0:T(8,128)(2,1)S(1)}, bf16[136,640]{1,0:T(8,128)(2,1)}, u32[]{:S(2)}) copy-start(bf16[136,640]{1,0:T(8,128)(2,1)} %param.17) | copy-start | bytes 522244
  90.6 24.0 %all-to-all-start = ((bf16[136,8,640]{2,0,1:T(8,128)(2,1)}), bf16[136,8,640]{2,0,1:T(8,128)(2,1)S(1)}, u32[]{:S(2)}, u32[]{:S(2)}) async-start(bf16[136,8,640]{2,0,1:T(8,128)(2,1)} %bitcast.199), calls=%async_computation | async-start | bytes 2785280 | tf_op jit(solution)/shard_map/all_to_all | solution.py:189
  95.0 42.2 %all-gather.9.cloned.1.call-start = ((), (), s32[]{:S(2)}) async-start(), calls=%async_computation.2 | async-start | bytes 1658880 | tf_op jit(solution)/shard_map/all_gather | solution.py:204
  115.6 84.9 %all-gather.15.cloned.1.call-start = ((), (), s32[]{:S(2)}) async-start(), calls=%async_computation.5 | async-start | bytes 6266880 | tf_op jit(solution)/shard_map/all_gather | solution.py:228
  137.1 2.2 copy-start.2
  140.7 66.5 %copy-start.6 = (bf16[5120,216]{0,1:T(8,128)(2,1)S(1)}, bf16[5120,216]{0,1:T(8,128)(2,1)}, u32[]{:S(2)}) copy-start(bf16[5120,216]{0,1:T(8,128)(2,1)} %param.31) | copy-start | bytes 6635524
  140.8 238.6 %all-gather.13.cloned.1.call-start = ((), (), s32[]{:S(2)}) async-start(), calls=%async_computation.4 | async-start | bytes 10027008 | tf_op jit(solution)/shard_map/all_gather | solution.py:240
  207.3 103.1 %collective-permute-start.1 = (bf16[16,68,2560]{2,0,1:T(8,128)(2,1)}, bf16[16,68,2560]{2,0,1:T(8,128)(2,1)}, u32[]{:S(2)}, u32[]{:S(2)}) collective-permute-start(bf16[16,68,2560]{2,0,1:T(8,128)(2,1)} %copy.54), channel_id=1, source_target_pairs={{0,1},{1,0},{2,3},{3,2},{4,5},{5,4},{6,7},{7,6},{8,9},{9,8},{10,11... | collective-permute-start | bytes 16711688 | tf_op jit(solution)/shard_map/ppermute | solution.py:229
  207.3 51.1 %collective-permute-start = (bf16[5120,216]{0,1:T(8,128)(2,1)S(1)}, bf16[5120,216]{0,1:T(8,128)(2,1)}, u32[]{:S(2)}, u32[]{:S(2)}) collective-permute-start(bf16[5120,216]{0,1:T(8,128)(2,1)S(1)} %copy-done.6), channel_id=1, source_target_pairs={{0,2},{1,3},{2,0},{3,1},{4,6},{5,7},{6,4},{7,5},{8,10},{9,11},{10,... | collective-permute-start | bytes 6635528 | tf_op jit(solution)/shard_map/ppermute | solution.py:73
  208.8 96.5 %collective-permute-start.2 = (bf16[5120,216]{0,1:T(8,128)(2,1)}, bf16[5120,216]{0,1:T(8,128)(2,1)}, u32[]{:S(2)}, u32[]{:S(2)}) collective-permute-start(bf16[5120,216]{0,1:T(8,128)(2,1)} %param.32), channel_id=1, source_target_pairs={{0,2},{1,3},{2,0},{3,1},{4,6},{5,7},{6,4},{7,5},{8,10},{9,11},{10,... | collective-permute-start | bytes 6635528 | tf_op jit(solution)/shard_map/ppermute | solution.py:74
  209.5 97.6 %slice-start.2 = ((s8[5898240]{0:T(1024)(128)(4,1)}), s8[4194304]{0:T(1024)(128)(4,1)S(1)}, s32[]{:S(2)}) async-start(s8[5898240]{0:T(1024)(128)(4,1)} %bitcast.212), calls=%async_computation.8 | async-start | bytes 8388608
  211.4 95.7 %slice-start.3 = ((s8[5898240]{0:T(1024)(128)(4,1)}), s8[1703936]{0:T(1024)(128)(4,1)S(1)}, s32[]{:S(2)}) async-start(s8[5898240]{0:T(1024)(128)(4,1)} %bitcast.212), calls=%async_computation.9 | async-start | bytes 3407872
  399.3 44.1 %copy-start.1 = (bf16[3,4096,128]{2,1,0:T(8,128)(2,1)S(1)}, bf16[3,4096,128]{2,1,0:T(8,128)(2,1)}, u32[]{:S(2)}) copy-start(bf16[3,4096,128]{2,1,0:T(8,128)(2,1)} %param.21) | copy-start | bytes 9437188
  (1 other events, 1.0 us)
Sparse Core Ops, SparseCore 0:
  9.5 52.4 all-gather.10
  115.7 21.4 all-gather.8
  140.9 59.5 all-gather.14
  327.9 51.3 all-gather.12

commit v6 on v1

--- a/solution.py
+++ b/solution.py
@@ -98,27 +98,30 @@
     state_prompt = fresh_state(prompt_count)
     req_count = lax.axis_size("req")
     context_rows = context_keys.shape[1]
-    packed = jnp.concatenate(
+    context_pack = jnp.concatenate(
         [
             context_keys.reshape(context_count * context_rows, heads_kv * HD),
             context_values.reshape(context_count * context_rows, heads_kv * HD),
-            new_keys,
-            new_values,
         ],
         0,
     )
-    gathered = lax.all_gather(packed, "req", axis=0, tiled=False)
+    context_gathered = lax.all_gather(context_pack, "req", axis=0, tiled=False)
+    new_pack = jnp.concatenate([new_keys, new_values], 0)
+    new_copies = jnp.broadcast_to(new_pack[None], (req_count,) + new_pack.shape)
+    new_gathered = lax.all_to_all(
+        new_copies.reshape(req_count * new_pack.shape[0], -1), "req", 0, 0, tiled=True
+    ).reshape(req_count, new_pack.shape[0], -1)
     context_span = context_count * context_rows
 
     def context_of(offset):
-        piece = gathered[:, offset : offset + context_span]
+        piece = context_gathered[:, offset : offset + context_span]
         piece = piece.reshape(req_count, context_count, context_rows, heads_kv * HD)
         return jnp.transpose(piece, (1, 0, 2, 3)).reshape(
             context_count, req_count * context_rows, heads_kv * HD
         )
 
     def prompt_of(offset):
-        piece = gathered[:, offset : offset + rows_here][:, decode_count:]
+        piece = new_gathered[:, offset : offset + rows_here][:, decode_count:]
         return piece.reshape(req_count * prompt_count, heads_kv * HD)
 
     key_block = context_of(0)
@@ -152,8 +155,8 @@
     )
     prompt_state = state_prompt
     own_positions = lax.axis_index("req") * prompt_count + jnp.arange(prompt_count, dtype=jnp.int32)
-    key_block = prompt_of(2 * context_span)
-    value_block = prompt_of(2 * context_span + rows_here)
+    key_block = prompt_of(0)
+    value_block = prompt_of(rows_here)
     extent = key_block.shape[0]
     positions = jnp.arange(extent, dtype=jnp.int32)
     block_scores = (

time: 364 us -> 364 us (level)
  waiting for transfers between devices: 184 us -> 173 us
  starting transfers between devices: 0.13 us -> 8.37 us
    all_gather x1, waiting for transfers between devices: 40.7 us -> 18.6 us  [per_device(): context_gathered = lax.all_gather(context_pack, 'req', axis=0, tiled=False)]
    all_to_all x0 -> x1, waiting for transfers between devices: none -> 10.5 us  [per_device(): lax.all_to_all(new_copies.reshape(req_count * new_pack.shape[0], -1), 're...]
    all_to_all x0 -> x1, starting transfers between devices: none -> 8.2 us  [per_device(): lax.all_to_all(new_copies.reshape(req_count * new_pack.shape[0], -1), 're...]
  transfers between devices with their start and end apart: 5 -> 6, of which waited for: 5 -> 6; matrix products, arithmetic and copies ran while one was open for 7% -> 8% of each run, Pallas kernels for 0% -> 0%
where the time goes in v6:
time: 364 us; the launch traced here: 363 us
  waiting for transfers between devices  173 us (48%)
  blocking collectives  79.7 us (22%)
  matrix products  52.2 us (14%)
  local copies, waits for them, and re-layouts  19.4 us (5%)
  other arithmetic  16.7 us (5%)
  between operations  14.2 us (4%)
  starting transfers between devices  8.37 us (2%)
    all_gather x1, waiting for transfers between devices, per_device(): near_rows = lax.all_gather(normed, 'req', axis=0, tiled=True)  83.5 us
    all_gather x1, waiting for transfers between devices, per_device(): hidden_block = lax.all_gather(hidden, 'mlp', axis=1, tiled=True)  45.7 us
    all_to_all x1, blocking collectives, per_device(): lax.all_to_all(down_partial.astype(jnp.bfloat16), 'req', 0, 0, tiled=True)  43 us
    all_to_all x1, blocking collectives, per_device(): lax.all_to_all(head_partial.astype(jnp.bfloat16), 'mlp', 1, 0, tiled=True)  23.8 us
    all_gather x1, waiting for transfers between devices, per_device(): context_gathered = lax.all_gather(context_pack, 'req', axis=0, tiled=False)  18.6 us
    dot_general x2, matrix products, project(): jnp.dot(far_rows, far_weight, preferred_element_type=jnp.float32)  16.8 us
    unnamed x1, blocking collectives  12.9 us
    dot_general x2, matrix products, project(): jnp.dot(near_rows, near_weight, preferred_element_type=jnp.float32)  11.5 us
  transfers between devices with their start and end apart: 6, of which 6 were waited for; matrix products, arithmetic and copies ran while one was open for 8% of the time, Pallas kernels for 0%

profile of v6, /device:TPU:0, one launch (start us, length us, event | category | flops | bytes accessed | tf_op | source)
XLA Modules:
  0.0 363.2 jit_solution(7720320294620631062)
XLA Ops:
  6.6 1.8 pad_maximum_fusion
  10.3 8.2 %all-to-all-start = ((bf16[16,272,128]{2,1,0:T(8,128)(2,1)}), bf16[16,272,128]{2,1,0:T(8,128)(2,1)}, u32[]{:S(2)}, u32[]{:S(2)}) async-start(bf16[16,272,128]{2,1,0:T(8,128)(2,1)} %broadcast_in_dim.145), calls=%async_computation | async-start | bytes 2228224 | tf_op jit(solution)/shard_map/all_to_all | solution.py:111
  21.8 1.2 slice_convert_fusion
  26.0 2.2 fusion.97
  28.5 10.5 %all-to-all-done = bf16[16,272,128]{2,1,0:T(8,128)(2,1)} async-done(((bf16[16,272,128]{2,1,0:T(8,128)(2,1)}), bf16[16,272,128]{2,1,0:T(8,128)(2,1)}, u32[]{:S(2)}, u32[]{:S(2)}) %all-to-all-start) | async-done | bytes 1114144 | tf_op jit(solution)/shard_map/all_to_all | solution.py:111
  38.9 1.6 fusion.95
  41.7 3.7 %fusion.96 = (f32[133,5]{0,1:T(8,128)S(1)}, f32[133,1,5,2128]{3,0,2,1:T(8,128)}) fusion(bf16[2128,128,1]{1,0,2:T(8,128)(2,1)S(1)} %reshape.438, bf16[133,5,128]{2,1,0:T(8,128)(2,1)S(1)} %copy-done.3, pred[133,2128]{1,0:T(8,128)(4,1)S(1)} %iota_compare_fusion), kind=kOutput, calls=%fused_computation.128 | convolution fusion | flops 366515392 | bytes 6661172 | tf_op jit(solution)/shard_map/jkgd,ckd->jkgc/dot_general | solution.py:163
  45.4 18.6 %all-gather.14.cloned.1.call-done = bf16[10240,128]{1,0:T(8,128)(2,1)} async-done(((bf16[640,128]{1,0:T(8,128)(2,1)}), bf16[10240,128]{1,0:T(8,128)(2,1)}) %all-gather.14.cloned.1.call-update) | async-done | bytes 2621456 | tf_op jit(solution)/shard_map/all_gather | solution.py:108
  64.0 1.9 fusion.94
  65.9 1.3 copy.26
  67.9 1.2 copy.27
  69.8 3.1 gather_fusion.1
  72.9 2.1 gather_fusion.2
  75.0 1.6 fusion.98
  78.2 2.5 fusion.43
  81.5 1.4 fusion
  84.9 1.2 fusion.56
  87.2 1.3 convolution_convert_fusion
  88.7 23.8 %all_to_all.28 = bf16[136,8,640]{2,0,1:T(8,128)(2,1)S(1)} all-to-all(bf16[136,8,640]{2,0,1:T(8,128)(2,1)S(1)} %bitcast.176), channel_id=1, replica_groups=mesh['req'=16,'mlp'=8] {'mlp'}, dimensions={1} | all-to-all | bytes 2785280 | tf_op jit(solution)/shard_map/all_to_all | solution.py:188
  113.5 12.9 %all-gather.2 = f32[8,1,640]{2,1,0:T(1,128)S(1)} all-gather(f32[1,1,640]{2,1,0:T(1,128)S(1)} %reshape.432), channel_id=2, replica_groups=mesh['req'=16,'mlp'=8] {'mlp'}, dimensions={0}, use_global_device_ids=true | all-gather | bytes 23040 | tf_op args[13]
  126.5 8.4 %all-gather.8.cloned.1.call-done = bf16[136,5120]{1,0:T(8,128)(2,1)} async-done(((bf16[136,640]{1,0:T(8,128)(2,1)}), bf16[136,5120]{1,0:T(8,128)(2,1)}) %all-gather.8.cloned.1.call-update) | async-done | bytes 1392656 | tf_op jit(solution)/shard_map/all_gather | solution.py:196
  134.9 1.7 multiply_reduce_fusion
  136.7 1.8 convert_element_type.68
  139.6 83.5 %all-gather.10.cloned.1.call-done = bf16[2176,2560]{1,0:T(8,128)(2,1)} async-done(((bf16[136,2560]{1,0:T(8,128)(2,1)}), bf16[2176,2560]{1,0:T(8,128)(2,1)}) %all-gather.10.cloned.1.call-update) | async-done | bytes 11141136 | tf_op jit(solution)/shard_map/all_gather | solution.py:205
  223.1 7.9 %fusion.48 = f32[2176,216]{0,1:T(8,128)S(1)} fusion(bf16[2176,2560]{1,0:T(8,128)(2,1)} %all-gather.10.cloned.1.call-done, bf16[5120,216]{0,1:T(8,128)(2,1)S(1)} %copy-done.21, s32[]{:T(128)S(6)} %select_n.78), kind=kOutput, calls=%fused_computation.57 | convolution fusion | flops 2406481920 | bytes 14127108 | tf_op jit(solution)/shard_map/dot_general | solution.py:212
  231.0 3.6 fusion.45
  234.6 5.9 %collective-permute-done = bf16[2176,2560]{1,0:T(8,128)(2,1)} collective-permute-done((bf16[2176,2560]{1,0:T(8,128)(2,1)}, bf16[2176,2560]{1,0:T(8,128)(2,1)}, u32[]{:S(2)}, u32[]{:S(2)}) %collective-permute-start) | collective-permute-done | bytes 11141152 | tf_op jit(solution)/shard_map/ppermute | solution.py:207
  240.5 7.7 %convolution_add_fusion.1 = f32[2176,216]{0,1:T(8,128)S(1)} fusion(f32[2176,216]{0,1:T(8,128)S(1)} %fusion.48, bf16[2176,2560]{1,0:T(8,128)(2,1)} %collective-permute-done, bf16[5120,216]{0,1:T(8,128)(2,1)S(1)} %copy-done.21, s32[]{:T(128)S(6)} %select_n.79), kind=kOutput, calls=%fused_computation.15 | convolution fusion | flops 2406951936 | bytes 16007172 | tf_op jit(solution)/shard_map/dot_general | solution.py:212
  248.2 9.0 %fusion.4 = bf16[2176,216]{0,1:T(8,128)(2,1)} fusion(f32[2176,216]{0,1:T(8,128)S(1)} %fusion.45, bf16[2176,2560]{1,0:T(8,128)(2,1)} %collective-permute-done, f32[2176,216]{0,1:T(8,128)S(1)} %convolution_add_fusion.1, bf16[5120,216]{0,1:T(8,128)(2,1)S(1)} %copy-done.22, s32[]{:T(128)S(6)} %select_n.79), kind=kOutput, calls=%fused_computation.14 | convolution fusion | flops 2409772032 | bytes 16947204 | tf_op jit(solution)/shard_map/dot_general | solution.py:212
  257.3 45.7 %all-gather.12.cloned.1.call-done = bf16[2176,1728]{0,1:T(8,128)(2,1)} async-done(((bf16[2176,216]{0,1:T(8,128)(2,1)}), bf16[2176,1728]{0,1:T(8,128)(2,1)}) %all-gather.12.cloned.1.call-update) | async-done | bytes 7520272 | tf_op jit(solution)/shard_map/all_gather | solution.py:219
  303.0 9.0 %convolution_convert_fusion.1 = bf16[2176,640]{1,0:T(8,128)(2,1)S(1)} fusion(bf16[2176,1728]{0,1:T(8,128)(2,1)} %all-gather.12.cloned.1.call-done, bf16[1728,640]{1,0:T(8,128)(2,1)S(1)} %copy-done.23), kind=kOutput, calls=%fused_computation.9 | convolution fusion | flops 4814356480 | bytes 12517376 | tf_op jit(solution)/shard_map/dot_general | solution.py:220
  312.1 43.0 %all_to_all.29 = bf16[16,136,640]{2,1,0:T(8,128)(2,1)S(1)} all-to-all(bf16[16,136,640]{2,1,0:T(8,128)(2,1)S(1)} %bitcast.180), channel_id=1, replica_groups=mesh['req'=16,'mlp'=8] {'req'}, dimensions={0} | all-to-all | bytes 5570560 | tf_op jit(solution)/shard_map/all_to_all | solution.py:221
  (112 shorter events, 19.7 us)
Async XLA Ops:
  6.5 19.4 %copy-start = (bf16[3,4096,128]{2,1,0:T(8,128)(2,1)S(1)}, bf16[3,4096,128]{2,1,0:T(8,128)(2,1)}, u32[]{:S(2)}) copy-start(bf16[3,4096,128]{2,1,0:T(8,128)(2,1)} %param.21) | copy-start | bytes 9437188
  6.5 12.0 %copy-start.9 = (bf16[136,640]{1,0:T(8,128)(2,1)S(1)}, bf16[136,640]{1,0:T(8,128)(2,1)}, u32[]{:S(2)}) copy-start(bf16[136,640]{1,0:T(8,128)(2,1)} %param.18) | copy-start | bytes 522244
  6.5 12.7 %copy-start.24 = (s32[3]{0:T(128)S(1)}, s32[3]{0:T(128)}, u32[]{:S(2)}) copy-start(s32[3]{0:T(128)} %param.26) | copy-start | bytes 40
  6.5 13.3 %copy-start.2 = (s32[4]{0:T(128)S(1)}, s32[4]{0:T(128)}, u32[]{:S(2)}) copy-start(s32[4]{0:T(128)} %param.27) | copy-start | bytes 52
  6.5 17.8 %copy-start.19 = (s32[3]{0:T(128)S(1)}, s32[3]{0:T(128)}, u32[]{:S(2)}) copy-start(s32[3]{0:T(128)} %param.25) | copy-start | bytes 40
  6.5 57.4 %all-gather.14.cloned.1.call-start = ((), (), s32[]{:S(2)}) async-start(), calls=%async_computation.6 | async-start | bytes 2785280 | tf_op jit(solution)/shard_map/all_gather | solution.py:108
  10.3 28.6 %all-to-all-start = ((bf16[16,272,128]{2,1,0:T(8,128)(2,1)}), bf16[16,272,128]{2,1,0:T(8,128)(2,1)}, u32[]{:S(2)}, u32[]{:S(2)}) async-start(bf16[16,272,128]{2,1,0:T(8,128)(2,1)} %broadcast_in_dim.145), calls=%async_computation | async-start | bytes 2228224 | tf_op jit(solution)/shard_map/all_to_all | solution.py:111
  18.5 116.4 %all-gather.8.cloned.1.call-start = ((), (), s32[]{:S(2)}) async-start(), calls=%async_computation.3 | async-start | bytes 1566720 | tf_op jit(solution)/shard_map/all_gather | solution.py:196
  18.6 5.8 %copy-start.12 = (bf16[3,5,128]{2,1,0:T(8,128)(2,1)}, bf16[3,5,128]{2,1,0:T(8,128)(2,1)S(1)}, u32[]{:S(2)}) copy-start(bf16[3,5,128]{2,1,0:T(8,128)(2,1)S(1)} %reshape.382) | copy-start | bytes 11524
  26.0 2.2 copy-start.18
  28.2 13.4 %copy-start.3 = (bf16[133,5,128]{2,1,0:T(8,128)(2,1)S(1)}, bf16[133,5,128]{2,1,0:T(8,128)(2,1)}, u32[]{:S(2)}) copy-start(bf16[133,5,128]{2,1,0:T(8,128)(2,1)} %reshape.390) | copy-start | bytes 510724
  67.9 7.1 %copy-start.11 = (pred[3,1024]{1,0:T(4,128)(4,1)S(1)}, pred[3,1024]{1,0:T(4,128)(4,1)}, u32[]{:S(2)}) copy-start(pred[3,1024]{1,0:T(4,128)(4,1)} %iota_compare_fusion.2) | copy-start | bytes 9220
  67.9 7.1 %copy-start.13 = (bf16[3,5,128]{2,1,0:T(8,128)(2,1)S(1)}, bf16[3,5,128]{2,1,0:T(8,128)(2,1)}, u32[]{:S(2)}) copy-start(bf16[3,5,128]{2,1,0:T(8,128)(2,1)} %copy-done.12) | copy-start | bytes 11524
  67.9 13.6 %slice-start = ((s8[5918720]{0:T(1024)(128)(4,1)}), s8[1724416]{0:T(1024)(128)(4,1)S(1)}, s32[]{:S(2)}) async-start(s8[5918720]{0:T(1024)(128)(4,1)} %bitcast.168), calls=%async_computation.7 | async-start | bytes 3448832
  69.1 7.6 %copy-start.14 = (f32[3,5]{1,0:T(4,128)S(1)}, f32[3,5]{1,0:T(4,128)}, u32[]{:S(2)}) copy-start(f32[3,5]{1,0:T(4,128)} %get-tuple-element.26) | copy-start | bytes 184
  69.1 7.6 %copy-start.16 = (f32[3,1,5]{2,1,0:T(1,128)S(1)}, f32[3,1,5]{2,1,0:T(1,128)}, u32[]{:S(2)}) copy-start(f32[3,1,5]{2,1,0:T(1,128)} %fusion.79) | copy-start | bytes 184
  75.0 5.7 %copy-start.4 = (bf16[133,5,128]{2,1,0:T(8,128)(2,1)S(1)}, bf16[133,5,128]{2,1,0:T(8,128)(2,1)}, u32[]{:S(2)}) copy-start(bf16[133,5,128]{2,1,0:T(8,128)(2,1)} %reshape.390) | copy-start | bytes 510724
  75.0 5.7 %copy-start.6 = (bf16[1,16,64,128]{3,2,0,1:T(8,128)(2,1)S(1)}, bf16[1,16,64,128]{3,2,0,1:T(8,128)(2,1)}, u32[]{:S(2)}) copy-start(bf16[1,16,64,128]{3,2,0,1:T(8,128)(2,1)} %slice.58) | copy-start | bytes 786436
  75.0 5.7 %copy-start.15 = (pred[1024]{0:T(1024)(128)(4,1)S(1)}, pred[1024]{0:T(1024)(128)(4,1)}, u32[]{:S(2)}) copy-start(pred[1024]{0:T(1024)(128)(4,1)} %iota_compare_fusion.3) | copy-start | bytes 3076
  76.8 4.6 %slice-start.1 = ((s8[5918720]{0:T(1024)(128)(4,1)}), s8[4194304]{0:T(1024)(128)(4,1)S(1)}, s32[]{:S(2)}) async-start(s8[5918720]{0:T(1024)(128)(4,1)} %bitcast.168), calls=%async_computation.8 | async-start | bytes 8388608
  83.9 2.5 slice-start.2
  84.9 2.3 slice-start.3
  88.6 24.1 %copy-start.10 = (bf16[136,640]{1,0:T(8,128)(2,1)S(1)}, bf16[136,640]{1,0:T(8,128)(2,1)}, u32[]{:S(2)}) copy-start(bf16[136,640]{1,0:T(8,128)(2,1)} %param.17) | copy-start | bytes 522244
  88.6 24.9 %copy-start.17 = (f32[640]{0:T(1024)S(1)}, f32[640]{0:T(1024)}, u32[]{:S(2)}) copy-start(f32[640]{0:T(1024)} %param.30) | copy-start | bytes 7684
  113.4 109.6 %all-gather.10.cloned.1.call-start = ((), (), s32[]{:S(2)}) async-start(), calls=%async_computation.4 | async-start | bytes 11837440 | tf_op jit(solution)/shard_map/all_gather | solution.py:205
  136.7 86.4 %copy-start.21 = (bf16[5120,216]{0,1:T(8,128)(2,1)S(1)}, bf16[5120,216]{0,1:T(8,128)(2,1)}, u32[]{:S(2)}) copy-start(bf16[5120,216]{0,1:T(8,128)(2,1)} %param.31) | copy-start | bytes 6635524
  139.5 163.5 %all-gather.12.cloned.1.call-start = ((), (), s32[]{:S(2)}) async-start(), calls=%async_computation.5 | async-start | bytes 8460288 | tf_op jit(solution)/shard_map/all_gather | solution.py:219
  223.1 17.4 %collective-permute-start = (bf16[2176,2560]{1,0:T(8,128)(2,1)}, bf16[2176,2560]{1,0:T(8,128)(2,1)}, u32[]{:S(2)}, u32[]{:S(2)}) collective-permute-start(bf16[2176,2560]{1,0:T(8,128)(2,1)} %all-gather.10.cloned.1.call-done), channel_id=1, source_target_pairs={{0,1},{1,0},{2,3},{3,2},{4,5},{5,4},{6,7},{7,6},{8,9},{9,8},{10,11... | collective-permute-start | bytes 33423368 | tf_op jit(solution)/shard_map/ppermute | solution.py:207
  223.1 7.9 %copy-start.20 = (bf16[2176,2560]{1,0:T(8,128)(2,1)S(1)}, bf16[2176,2560]{1,0:T(8,128)(2,1)}, u32[]{:S(2)}) copy-start(bf16[2176,2560]{1,0:T(8,128)(2,1)} %all-gather.10.cloned.1.call-done) | copy-start | bytes 33423364
  223.1 8.0 %copy-start.22 = (bf16[5120,216]{0,1:T(8,128)(2,1)S(1)}, bf16[5120,216]{0,1:T(8,128)(2,1)}, u32[]{:S(2)}) copy-start(bf16[5120,216]{0,1:T(8,128)(2,1)} %param.32) | copy-start | bytes 6635524
  248.2 54.8 %copy-start.23 = (bf16[1728,640]{1,0:T(8,128)(2,1)S(1)}, bf16[1728,640]{1,0:T(8,128)(2,1)}, u32[]{:S(2)}) copy-start(bf16[1728,640]{1,0:T(8,128)(2,1)} %param.33) | copy-start | bytes 6635524
  312.1 44.6 %copy-start.1 = (bf16[3,4096,128]{2,1,0:T(8,128)(2,1)S(1)}, bf16[3,4096,128]{2,1,0:T(8,128)(2,1)}, u32[]{:S(2)}) copy-start(bf16[3,4096,128]{2,1,0:T(8,128)(2,1)} %param.21) | copy-start | bytes 9437188
  (3 other events, 2.9 us)
Sparse Core Ops, SparseCore 0:
  9.5 54.4 all-gather.13
  113.6 21.3 all-gather.7
  139.7 83.3 all-gather.9
  257.4 45.5 all-gather.11

commit v7 on v6

--- a/solution.py
+++ b/solution.py
@@ -98,23 +98,20 @@
     state_prompt = fresh_state(prompt_count)
     req_count = lax.axis_size("req")
     context_rows = context_keys.shape[1]
-    context_pack = jnp.concatenate(
-        [
-            context_keys.reshape(context_count * context_rows, heads_kv * HD),
-            context_values.reshape(context_count * context_rows, heads_kv * HD),
-        ],
-        0,
-    )
-    context_gathered = lax.all_gather(context_pack, "req", axis=0, tiled=False)
-    new_pack = jnp.concatenate([new_keys, new_values], 0)
+    context_span = context_count * context_rows
+    context_gathered = lax.all_gather(
+        context_keys.reshape(context_span, heads_kv * HD), "req", axis=0, tiled=False
+    )
+    new_pack = jnp.concatenate(
+        [context_values.reshape(context_span, heads_kv * HD), new_keys, new_values], 0
+    )
     new_copies = jnp.broadcast_to(new_pack[None], (req_count,) + new_pack.shape)
     new_gathered = lax.all_to_all(
         new_copies.reshape(req_count * new_pack.shape[0], -1), "req", 0, 0, tiled=True
     ).reshape(req_count, new_pack.shape[0], -1)
-    context_span = context_count * context_rows
-
-    def context_of(offset):
-        piece = context_gathered[:, offset : offset + context_span]
+
+    def context_of(source):
+        piece = source[:, :context_span]
         piece = piece.reshape(req_count, context_count, context_rows, heads_kv * HD)
         return jnp.transpose(piece, (1, 0, 2, 3)).reshape(
             context_count, req_count * context_rows, heads_kv * HD
@@ -124,8 +121,8 @@
         piece = new_gathered[:, offset : offset + rows_here][:, decode_count:]
         return piece.reshape(req_count * prompt_count, heads_kv * HD)
 
-    key_block = context_of(0)
-    value_block = context_of(context_span)
+    key_block = context_of(context_gathered)
+    value_block = context_of(new_gathered)
     extent = key_block.shape[1]
     positions = jnp.arange(extent)
     key_split = key_block.reshape(context_count, extent, heads_kv, HD)
@@ -155,8 +152,8 @@
     )
     prompt_state = state_prompt
     own_positions = lax.axis_index("req") * prompt_count + jnp.arange(prompt_count, dtype=jnp.int32)
-    key_block = prompt_of(0)
-    value_block = prompt_of(rows_here)
+    key_block = prompt_of(context_span)
+    value_block = prompt_of(context_span + rows_here)
     extent = key_block.shape[0]
     positions = jnp.arange(extent, dtype=jnp.int32)
     block_scores = (

time: 364 us -> 366 us (level)
  waiting for transfers between devices: 173 us -> 177 us
    all_to_all x1, waiting for transfers between devices: 10.5 us -> 26 us  [per_device(): lax.all_to_all(new_copies.reshape(req_count * new_pack.shape[0], -1), 're...]
    all_gather x1, waiting for transfers between devices: 18.6 us -> 6.48 us  [per_device(): lax.all_gather(context_keys.reshape(context_span, heads_kv * HD), 'req',...]
  transfers between devices with their start and end apart: 6 -> 6, of which waited for: 6 -> 6; matrix products, arithmetic and copies ran while one was open for 8% -> 10% of each run, Pallas kernels for 0% -> 0%
where the time goes in v7:
time: 366 us; the launch traced here: 365 us
  waiting for transfers between devices  177 us (48%)
  blocking collectives  79.7 us (22%)
  matrix products  53.8 us (15%)
  local copies, waits for them, and re-layouts  18 us (5%)
  other arithmetic  14.3 us (4%)
  between operations  14.2 us (4%)
  starting transfers between devices  8.48 us (2%)
    all_gather x1, waiting for transfers between devices, per_device(): near_rows = lax.all_gather(normed, 'req', axis=0, tiled=True)  83.5 us
    all_gather x1, waiting for transfers between devices, per_device(): hidden_block = lax.all_gather(hidden, 'mlp', axis=1, tiled=True)  45.7 us
    all_to_all x1, blocking collectives, per_device(): lax.all_to_all(down_partial.astype(jnp.bfloat16), 'req', 0, 0, tiled=True)  43 us
    all_to_all x1, waiting for transfers between devices, per_device(): lax.all_to_all(new_copies.reshape(req_count * new_pack.shape[0], -1), 're...  26 us
    all_to_all x1, blocking collectives, per_device(): lax.all_to_all(head_partial.astype(jnp.bfloat16), 'mlp', 1, 0, tiled=True)  23.8 us
    dot_general x2, matrix products, project(): jnp.dot(far_rows, far_weight, preferred_element_type=jnp.float32)  16.8 us
    unnamed x1, blocking collectives  12.9 us
    dot_general x2, matrix products, project(): jnp.dot(near_rows, near_weight, preferred_element_type=jnp.float32)  11.7 us
  transfers between devices with their start and end apart: 6, of which 6 were waited for; matrix products, arithmetic and copies ran while one was open for 10% of the time, Pallas kernels for 0%

profile of v7, /device:TPU:0, one launch (start us, length us, event | category | flops | bytes accessed | tf_op | source)
XLA Modules:
  0.0 365.1 jit_solution(4457502554702608406)
XLA Ops:
  7.3 1.2 pad_maximum_fusion
  8.4 1.8 broadcast_in_dim.138
  10.2 8.3 %all-to-all-start = ((bf16[16,592,128]{2,1,0:T(8,128)(2,1)}), bf16[16,592,128]{2,1,0:T(8,128)(2,1)}, u32[]{:S(2)}, u32[]{:S(2)}) async-start(bf16[16,592,128]{2,1,0:T(8,128)(2,1)} %broadcast_in_dim.138), calls=%async_computation | async-start | bytes 4849664 | tf_op jit(solution)/shard_map/all_to_all | solution.py:109
  19.3 1.3 slice_convert_fusion
  26.1 2.2 fusion.96
  28.6 26.0 %all-to-all-done = bf16[16,592,128]{2,1,0:T(8,128)(2,1)} async-done(((bf16[16,592,128]{2,1,0:T(8,128)(2,1)}), bf16[16,592,128]{2,1,0:T(8,128)(2,1)}, u32[]{:S(2)}, u32[]{:S(2)}) %all-to-all-start) | async-done | bytes 2424864 | tf_op jit(solution)/shard_map/all_to_all | solution.py:109
  54.6 1.4 slice.52
  56.8 1.6 fusion.94
  61.2 4.8 %fusion.95 = (f32[133,5]{0,1:T(8,128)S(1)}, f32[133,1,5,2128]{3,0,2,1:T(8,128)}) fusion(bf16[2128,128,1]{1,0,2:T(8,128)(2,1)} %reshape.433, bf16[133,5,128]{2,1,0:T(8,128)(2,1)} %reshape.386, pred[133,2128]{1,0:T(8,128)(4,1)S(1)} %iota_compare_fusion), kind=kOutput, calls=%fused_computation.126 | convolution fusion | flops 366515392 | bytes 6661172 | tf_op jit(solution)/shard_map/jkgd,ckd->jkgc/dot_general | solution.py:160
  66.1 6.5 %all-gather.7.cloned.1.call-done = bf16[16,320,128]{2,1,0:T(8,128)(2,1)} async-done(((bf16[1,320,128]{2,1,0:T(8,128)(2,1)}), bf16[16,320,128]{2,1,0:T(8,128)(2,1)}) %all-gather.7.cloned.1.call-update) | async-done | bytes 1310736 | tf_op jit(solution)/shard_map/all_gather | solution.py:102
  72.6 1.4 copy.26
  74.0 1.7 slice.53
  75.7 1.7 gather_fusion.1
  77.4 1.6 fusion.97
  79.8 2.6 fusion.43
  83.4 1.4 fusion
  86.9 1.4 fusion.56
  89.1 1.3 convolution_convert_fusion
  90.5 23.8 %all_to_all.28 = bf16[136,8,640]{2,0,1:T(8,128)(2,1)S(1)} all-to-all(bf16[136,8,640]{2,0,1:T(8,128)(2,1)S(1)} %bitcast.171), channel_id=1, replica_groups=mesh['req'=16,'mlp'=8] {'mlp'}, dimensions={1} | all-to-all | bytes 2785280 | tf_op jit(solution)/shard_map/all_to_all | solution.py:185
  115.4 12.9 %all-gather.1 = f32[8,1,640]{2,1,0:T(1,128)S(1)} all-gather(f32[1,1,640]{2,1,0:T(1,128)S(1)} %reshape.427), channel_id=2, replica_groups=mesh['req'=16,'mlp'=8] {'mlp'}, dimensions={0}, use_global_device_ids=true | all-gather | bytes 23040 | tf_op args[13]
  128.4 8.6 %all-gather.9.cloned.1.call-done = bf16[136,5120]{1,0:T(8,128)(2,1)} async-done(((bf16[136,640]{1,0:T(8,128)(2,1)}), bf16[136,5120]{1,0:T(8,128)(2,1)}) %all-gather.9.cloned.1.call-update) | async-done | bytes 1392656 | tf_op jit(solution)/shard_map/all_gather | solution.py:193
  137.0 1.7 multiply_reduce_fusion
  138.7 1.6 convert_element_type.68
  141.4 83.5 %all-gather.11.cloned.1.call-done = bf16[2176,2560]{1,0:T(8,128)(2,1)} async-done(((bf16[136,2560]{1,0:T(8,128)(2,1)}), bf16[2176,2560]{1,0:T(8,128)(2,1)}) %all-gather.11.cloned.1.call-update) | async-done | bytes 11141136 | tf_op jit(solution)/shard_map/all_gather | solution.py:202
  224.9 8.1 %fusion.48 = f32[2176,216]{0,1:T(8,128)S(1)} fusion(bf16[2176,2560]{1,0:T(8,128)(2,1)} %all-gather.11.cloned.1.call-done, bf16[5120,216]{0,1:T(8,128)(2,1)} %param.31, s32[]{:T(128)S(6)} %select_n.78), kind=kOutput, calls=%fused_computation.57 | convolution fusion | flops 2406481920 | bytes 14127108 | tf_op jit(solution)/shard_map/dot_general | solution.py:209
  233.2 3.6 fusion.45
  236.8 5.5 %collective-permute-done = bf16[2176,2560]{1,0:T(8,128)(2,1)} collective-permute-done((bf16[2176,2560]{1,0:T(8,128)(2,1)}, bf16[2176,2560]{1,0:T(8,128)(2,1)}, u32[]{:S(2)}, u32[]{:S(2)}) %collective-permute-start) | collective-permute-done | bytes 11141152 | tf_op jit(solution)/shard_map/ppermute | solution.py:204
  242.3 7.7 %convolution_add_fusion.1 = f32[2176,216]{0,1:T(8,128)S(1)} fusion(f32[2176,216]{0,1:T(8,128)S(1)} %fusion.48, bf16[2176,2560]{1,0:T(8,128)(2,1)} %collective-permute-done, bf16[5120,216]{0,1:T(8,128)(2,1)S(1)} %copy-done.22, s32[]{:T(128)S(6)} %select_n.79), kind=kOutput, calls=%fused_computation.15 | convolution fusion | flops 2406951936 | bytes 16007172 | tf_op jit(solution)/shard_map/dot_general | solution.py:209
  250.1 9.0 %fusion.4 = bf16[2176,216]{0,1:T(8,128)(2,1)} fusion(f32[2176,216]{0,1:T(8,128)S(1)} %fusion.45, bf16[2176,2560]{1,0:T(8,128)(2,1)} %collective-permute-done, f32[2176,216]{0,1:T(8,128)S(1)} %convolution_add_fusion.1, bf16[5120,216]{0,1:T(8,128)(2,1)S(1)} %copy-done.23, s32[]{:T(128)S(6)} %select_n.79), kind=kOutput, calls=%fused_computation.14 | convolution fusion | flops 2409772032 | bytes 16947204 | tf_op jit(solution)/shard_map/dot_general | solution.py:209
  259.2 45.7 %all-gather.13.cloned.1.call-done = bf16[2176,1728]{0,1:T(8,128)(2,1)} async-done(((bf16[2176,216]{0,1:T(8,128)(2,1)}), bf16[2176,1728]{0,1:T(8,128)(2,1)}) %all-gather.13.cloned.1.call-update) | async-done | bytes 7520272 | tf_op jit(solution)/shard_map/all_gather | solution.py:216
  304.9 9.0 %convolution_convert_fusion.1 = bf16[2176,640]{1,0:T(8,128)(2,1)S(1)} fusion(bf16[2176,1728]{0,1:T(8,128)(2,1)} %all-gather.13.cloned.1.call-done, bf16[1728,640]{1,0:T(8,128)(2,1)S(1)} %copy-done.24), kind=kOutput, calls=%fused_computation.9 | convolution fusion | flops 4814356480 | bytes 12517376 | tf_op jit(solution)/shard_map/dot_general | solution.py:217
  313.9 43.0 %all_to_all.29 = bf16[16,136,640]{2,1,0:T(8,128)(2,1)S(1)} all-to-all(bf16[16,136,640]{2,1,0:T(8,128)(2,1)S(1)} %bitcast.175), channel_id=1, replica_groups=mesh['req'=16,'mlp'=8] {'req'}, dimensions={0} | all-to-all | bytes 5570560 | tf_op jit(solution)/shard_map/all_to_all | solution.py:218
  (108 shorter events, 18.8 us)
Async XLA Ops:
  6.5 19.5 %copy-start = (bf16[3,4096,128]{2,1,0:T(8,128)(2,1)S(1)}, bf16[3,4096,128]{2,1,0:T(8,128)(2,1)}, u32[]{:S(2)}) copy-start(bf16[3,4096,128]{2,1,0:T(8,128)(2,1)} %param.21) | copy-start | bytes 9437188
  6.5 66.0 %all-gather.7.cloned.1.call-start = ((), (), s32[]{:S(2)}) async-start(), calls=%async_computation.3 | async-start | bytes 1392640 | tf_op jit(solution)/shard_map/all_gather | solution.py:102
  10.2 10.4 %copy-start.25 = (s32[3]{0:T(128)S(1)}, s32[3]{0:T(128)}, u32[]{:S(2)}) copy-start(s32[3]{0:T(128)} %param.26) | copy-start | bytes 40
  10.2 11.0 %copy-start.2 = (s32[4]{0:T(128)S(1)}, s32[4]{0:T(128)}, u32[]{:S(2)}) copy-start(s32[4]{0:T(128)} %param.27) | copy-start | bytes 52
  10.2 12.8 %copy-start.9 = (bf16[136,640]{1,0:T(8,128)(2,1)S(1)}, bf16[136,640]{1,0:T(8,128)(2,1)}, u32[]{:S(2)}) copy-start(bf16[136,640]{1,0:T(8,128)(2,1)} %param.18) | copy-start | bytes 522244
  10.2 15.8 %copy-start.20 = (s32[3]{0:T(128)S(1)}, s32[3]{0:T(128)}, u32[]{:S(2)}) copy-start(s32[3]{0:T(128)} %param.25) | copy-start | bytes 40
  10.2 44.4 %all-to-all-start = ((bf16[16,592,128]{2,1,0:T(8,128)(2,1)}), bf16[16,592,128]{2,1,0:T(8,128)(2,1)}, u32[]{:S(2)}, u32[]{:S(2)}) async-start(bf16[16,592,128]{2,1,0:T(8,128)(2,1)} %broadcast_in_dim.138), calls=%async_computation | async-start | bytes 4849664 | tf_op jit(solution)/shard_map/all_to_all | solution.py:109
  18.6 118.4 %all-gather.9.cloned.1.call-start = ((), (), s32[]{:S(2)}) async-start(), calls=%async_computation.4 | async-start | bytes 1566720 | tf_op jit(solution)/shard_map/all_gather | solution.py:193
  23.1 2.9 copy-start.12
  24.0 4.3 %copy-start.19 = (s32[133]{0:T(256)S(1)}, s32[133]{0:T(256)}, u32[]{:S(2)}) copy-start(s32[133]{0:T(256)} %iota_add_fusion) | copy-start | bytes 1600
  66.1 11.3 %copy-start.11 = (pred[3,1024]{1,0:T(4,128)(4,1)S(1)}, pred[3,1024]{1,0:T(4,128)(4,1)}, u32[]{:S(2)}) copy-start(pred[3,1024]{1,0:T(4,128)(4,1)} %iota_compare_fusion.2) | copy-start | bytes 9220
  66.1 11.3 %copy-start.13 = (bf16[3,5,128]{2,1,0:T(8,128)(2,1)S(1)}, bf16[3,5,128]{2,1,0:T(8,128)(2,1)}, u32[]{:S(2)}) copy-start(bf16[3,5,128]{2,1,0:T(8,128)(2,1)} %copy-done.12) | copy-start | bytes 11524
  72.6 6.4 %copy-start.14 = (f32[3,5]{1,0:T(4,128)S(1)}, f32[3,5]{1,0:T(4,128)}, u32[]{:S(2)}) copy-start(f32[3,5]{1,0:T(4,128)} %get-tuple-element.24) | copy-start | bytes 184
  72.6 6.5 %copy-start.17 = (f32[3,1,5]{2,1,0:T(1,128)S(1)}, f32[3,1,5]{2,1,0:T(1,128)}, u32[]{:S(2)}) copy-start(f32[3,1,5]{2,1,0:T(1,128)} %fusion.79) | copy-start | bytes 184
  74.0 5.8 %copy-start.16 = (f32[3,128]{1,0:T(4,128)S(1)}, f32[3,128]{1,0:T(4,128)}, u32[]{:S(2)}) copy-start(f32[3,128]{1,0:T(4,128)} %slice_convert_fusion) | copy-start | bytes 4612
  77.4 5.0 %copy-start.4 = (bf16[133,5,128]{2,1,0:T(8,128)(2,1)S(1)}, bf16[133,5,128]{2,1,0:T(8,128)(2,1)}, u32[]{:S(2)}) copy-start(bf16[133,5,128]{2,1,0:T(8,128)(2,1)} %reshape.386) | copy-start | bytes 510724
  77.4 5.0 %copy-start.6 = (bf16[1,16,64,128]{3,2,0,1:T(8,128)(2,1)S(1)}, bf16[1,16,64,128]{3,2,0,1:T(8,128)(2,1)}, u32[]{:S(2)}) copy-start(bf16[1,16,64,128]{3,2,0,1:T(8,128)(2,1)} %slice.53) | copy-start | bytes 786436
  77.4 5.0 %copy-start.15 = (pred[1024]{0:T(1024)(128)(4,1)S(1)}, pred[1024]{0:T(1024)(128)(4,1)}, u32[]{:S(2)}) copy-start(pred[1024]{0:T(1024)(128)(4,1)} %iota_compare_fusion.3) | copy-start | bytes 3076
  79.8 3.6 copy-start.3
  85.8 1.0 copy-start.7
  85.8 2.6 slice-start
  86.9 2.3 slice-start.1
  90.5 24.1 %copy-start.10 = (bf16[136,640]{1,0:T(8,128)(2,1)S(1)}, bf16[136,640]{1,0:T(8,128)(2,1)}, u32[]{:S(2)}) copy-start(bf16[136,640]{1,0:T(8,128)(2,1)} %param.17) | copy-start | bytes 522244
  90.5 24.8 %copy-start.18 = (f32[640]{0:T(1024)S(1)}, f32[640]{0:T(1024)}, u32[]{:S(2)}) copy-start(f32[640]{0:T(1024)} %param.30) | copy-start | bytes 7684
  115.3 109.6 %all-gather.11.cloned.1.call-start = ((), (), s32[]{:S(2)}) async-start(), calls=%async_computation.5 | async-start | bytes 11837440 | tf_op jit(solution)/shard_map/all_gather | solution.py:202
  141.4 163.5 %all-gather.13.cloned.1.call-start = ((), (), s32[]{:S(2)}) async-start(), calls=%async_computation.6 | async-start | bytes 8460288 | tf_op jit(solution)/shard_map/all_gather | solution.py:216
  224.9 17.4 %collective-permute-start = (bf16[2176,2560]{1,0:T(8,128)(2,1)}, bf16[2176,2560]{1,0:T(8,128)(2,1)}, u32[]{:S(2)}, u32[]{:S(2)}) collective-permute-start(bf16[2176,2560]{1,0:T(8,128)(2,1)} %all-gather.11.cloned.1.call-done), channel_id=1, source_target_pairs={{0,1},{1,0},{2,3},{3,2},{4,5},{5,4},{6,7},{7,6},{8,9},{9,8},{10,11... | collective-permute-start | bytes 33423368 | tf_op jit(solution)/shard_map/ppermute | solution.py:204
  224.9 8.1 %copy-start.21 = (bf16[2176,2560]{1,0:T(8,128)(2,1)S(1)}, bf16[2176,2560]{1,0:T(8,128)(2,1)}, u32[]{:S(2)}) copy-start(bf16[2176,2560]{1,0:T(8,128)(2,1)} %all-gather.11.cloned.1.call-done) | copy-start | bytes 33423364
  224.9 8.3 %copy-start.23 = (bf16[5120,216]{0,1:T(8,128)(2,1)S(1)}, bf16[5120,216]{0,1:T(8,128)(2,1)}, u32[]{:S(2)}) copy-start(bf16[5120,216]{0,1:T(8,128)(2,1)} %param.32) | copy-start | bytes 6635524
  233.2 9.2 %copy-start.22 = (bf16[5120,216]{0,1:T(8,128)(2,1)S(1)}, bf16[5120,216]{0,1:T(8,128)(2,1)}, u32[]{:S(2)}) copy-start(bf16[5120,216]{0,1:T(8,128)(2,1)} %param.31) | copy-start | bytes 6635524
  250.1 54.8 %copy-start.24 = (bf16[1728,640]{1,0:T(8,128)(2,1)S(1)}, bf16[1728,640]{1,0:T(8,128)(2,1)}, u32[]{:S(2)}) copy-start(bf16[1728,640]{1,0:T(8,128)(2,1)} %param.33) | copy-start | bytes 6635524
  313.9 44.6 %copy-start.1 = (bf16[3,4096,128]{2,1,0:T(8,128)(2,1)S(1)}, bf16[3,4096,128]{2,1,0:T(8,128)(2,1)}, u32[]{:S(2)}) copy-start(bf16[3,4096,128]{2,1,0:T(8,128)(2,1)} %param.21) | copy-start | bytes 9437188
  (2 other events, 1.9 us)
Sparse Core Ops, SparseCore 0:
  9.5 63.0 all-gather.6
  115.4 21.4 all-gather.8
  141.5 83.3 all-gather.10
  259.3 45.5 all-gather.12

commit v8 on v6

--- a/solution.py
+++ b/solution.py
@@ -12,6 +12,7 @@
 
 
 NEGATIVE = -1e30
+REQ = ("ry", "rz")
 
 
 def absorb(carried, scores, allowed, values, pattern):
@@ -96,7 +97,7 @@
     prefix_here = prefix_lengths[group_ids]
     state_decode = decode_state
     state_prompt = fresh_state(prompt_count)
-    req_count = lax.axis_size("req")
+    req_count = lax.axis_size("ry") * lax.axis_size("rz")
     context_rows = context_keys.shape[1]
     context_pack = jnp.concatenate(
         [
@@ -105,11 +106,11 @@
         ],
         0,
     )
-    context_gathered = lax.all_gather(context_pack, "req", axis=0, tiled=False)
+    context_gathered = lax.all_gather(context_pack, REQ, axis=0, tiled=False)
     new_pack = jnp.concatenate([new_keys, new_values], 0)
     new_copies = jnp.broadcast_to(new_pack[None], (req_count,) + new_pack.shape)
     new_gathered = lax.all_to_all(
-        new_copies.reshape(req_count * new_pack.shape[0], -1), "req", 0, 0, tiled=True
+        new_copies.reshape(req_count * new_pack.shape[0], -1), REQ, 0, 0, tiled=True
     ).reshape(req_count, new_pack.shape[0], -1)
     context_span = context_count * context_rows
 
@@ -154,7 +155,7 @@
         state_prompt, block_scores, block_usable, value_split[context_count - 1], "jkgc,ckd->jkgd"
     )
     prompt_state = state_prompt
-    own_positions = lax.axis_index("req") * prompt_count + jnp.arange(prompt_count, dtype=jnp.int32)
+    own_positions = (lax.axis_index("ry") * lax.axis_size("rz") + lax.axis_index("rz")) * prompt_count + jnp.arange(prompt_count, dtype=jnp.int32)
     key_block = prompt_of(0)
     value_block = prompt_of(rows_here)
     extent = key_block.shape[0]
@@ -202,7 +203,7 @@
     normed = (
         own_half * lax.rsqrt(square_total / D + 1e-06)[:, None] * own_gain[None, :]
     ).astype(jnp.bfloat16)
-    near_rows = lax.all_gather(normed, "req", axis=0, tiled=True)
+    near_rows = lax.all_gather(normed, REQ, axis=0, tiled=True)
     pairs = [(i, i ^ 1) for i in range(mlp_count)]
     far_rows = lax.ppermute(near_rows, "mlp", pairs)
 
@@ -218,36 +219,44 @@
     hidden = (jax.nn.silu(gate_proj) * up_proj).astype(jnp.bfloat16)
     hidden_block = lax.all_gather(hidden, "mlp", axis=1, tiled=True)
     down_partial = jnp.dot(hidden_block, down_weight, preferred_element_type=jnp.float32)
-    req_pieces = lax.all_to_all(down_partial.astype(jnp.bfloat16), "req", 0, 0, tiled=True)
-    feed = jnp.sum(
-        req_pieces.reshape(req_count, rows_here, -1).astype(jnp.float32), axis=0
-    )
+    outer, inner = lax.axis_size("ry"), lax.axis_size("rz")
+    by_owner = down_partial.astype(jnp.bfloat16).reshape(outer, inner, rows_here, -1)
+    inner_pieces = lax.all_to_all(by_owner, "rz", 1, 1, tiled=True)
+    inner_sum = jnp.sum(
+        inner_pieces.reshape(outer, inner, rows_here, -1).astype(jnp.float32), axis=1
+    ).astype(jnp.bfloat16)
+    outer_pieces = lax.all_to_all(inner_sum, "ry", 0, 0, tiled=True)
+    feed = jnp.sum(outer_pieces.astype(jnp.float32), axis=0)
     return (mixed_wide + feed).astype(jnp.bfloat16)
 
 
 def solution(mesh):
+    req_size, mlp_size = mesh.devices.shape
+    split_mesh = jax.sharding.Mesh(
+        mesh.devices.reshape(4, req_size // 4, mlp_size), ("ry", "rz", "mlp")
+    )
     return jax.shard_map(
         per_device,
-        mesh=mesh,
+        mesh=split_mesh,
         in_specs=(
-            P("req", "mlp"),
-            P("req", "mlp"),
-            P("req", "mlp"),
-            P("req", "mlp"),
-            P("req", None, "mlp"),
-            P("req", None, "mlp"),
-            P(None, "req", "mlp"),
-            P(None, "req", "mlp"),
-            P("req"),
-            P("req"),
+            P(REQ, "mlp"),
+            P(REQ, "mlp"),
+            P(REQ, "mlp"),
+            P(REQ, "mlp"),
+            P(REQ, None, "mlp"),
+            P(REQ, None, "mlp"),
+            P(None, REQ, "mlp"),
+            P(None, REQ, "mlp"),
+            P(REQ),
+            P(REQ),
             P(),
             P(),
             P("mlp", None),
             P(),
-            P(None, ("req", "mlp")),
-            P(None, ("req", "mlp")),
-            P("req", "mlp"),
+            P(None, ("ry", "rz", "mlp")),
+            P(None, ("ry", "rz", "mlp")),
+            P(REQ, "mlp"),
         ),
-        out_specs=P("req", "mlp"),
+        out_specs=P(REQ, "mlp"),
         check_vma=False,
     )

time: 364 us -> 377 us (1.036)
  blocking collectives: 79.7 us -> 90.3 us
    all_to_all x1 -> x2, blocking collectives: 43 us -> 53.6 us  [the longest x1 38.7 us: per_device(): inner_pieces = lax.all_to_all(by_owner, 'rz', 1, 1, tiled=True)]
where the time goes in v8:
time: 377 us
  waiting for transfers between devices  173 us (46%)
  blocking collectives  90.3 us (24%)
  matrix products  52.2 us (14%)
  other arithmetic  19.6 us (5%)
  local copies, waits for them, and re-layouts  19.1 us (5%)
  between operations  14.3 us (4%)
  starting transfers between devices  8.37 us (2%)
    all_gather x1, waiting for transfers between devices, per_device(): near_rows = lax.all_gather(normed, REQ, axis=0, tiled=True)  83.5 us
    all_gather x1, waiting for transfers between devices, per_device(): hidden_block = lax.all_gather(hidden, 'mlp', axis=1, tiled=True)  45.7 us
    all_to_all x1, blocking collectives, per_device(): inner_pieces = lax.all_to_all(by_owner, 'rz', 1, 1, tiled=True)  38.7 us
    all_to_all x1, blocking collectives, per_device(): lax.all_to_all(head_partial.astype(jnp.bfloat16), 'mlp', 1, 0, tiled=True)  23.8 us
    all_gather x1, waiting for transfers between devices, per_device(): context_gathered = lax.all_gather(context_pack, REQ, axis=0, tiled=False)  18.6 us
    dot_general x2, matrix products, project(): jnp.dot(far_rows, far_weight, preferred_element_type=jnp.float32)  16.8 us
    all_to_all x1, blocking collectives, per_device(): outer_pieces = lax.all_to_all(inner_sum, 'ry', 0, 0, tiled=True)  14.9 us
    unnamed x1, blocking collectives  12.9 us
  transfers between devices with their start and end apart: 6, of which 6 were waited for; matrix products, arithmetic and copies ran while one was open for 8% of the time, Pallas kernels for 0%

profile of v8, /device:TPU:0, one launch (start us, length us, event | category | flops | bytes accessed | tf_op | source)
XLA Modules:
  0.0 376.5 jit_solution(8682409019946788826)
XLA Ops:
  6.6 1.8 pad_maximum_fusion
  10.3 8.2 %all-to-all-start = ((bf16[16,272,128]{2,1,0:T(8,128)(2,1)}), bf16[16,272,128]{2,1,0:T(8,128)(2,1)}, u32[]{:S(2)}, u32[]{:S(2)}) async-start(bf16[16,272,128]{2,1,0:T(8,128)(2,1)} %broadcast_in_dim.145), calls=%async_computation | async-start | bytes 2228224 | tf_op jit(solution)/shard_map/all_to_all | solution.py:112
  21.7 1.3 slice_convert_fusion
  25.9 2.3 fusion.97
  28.5 10.5 %all-to-all-done = bf16[16,272,128]{2,1,0:T(8,128)(2,1)} async-done(((bf16[16,272,128]{2,1,0:T(8,128)(2,1)}), bf16[16,272,128]{2,1,0:T(8,128)(2,1)}, u32[]{:S(2)}, u32[]{:S(2)}) %all-to-all-start) | async-done | bytes 1114144 | tf_op jit(solution)/shard_map/all_to_all | solution.py:112
  38.9 1.6 fusion.95
  41.7 3.7 fusion.96
  45.4 18.6 %all-gather.14.cloned.1.call-done = bf16[10240,128]{1,0:T(8,128)(2,1)} async-done(((bf16[640,128]{1,0:T(8,128)(2,1)}), bf16[10240,128]{1,0:T(8,128)(2,1)}) %all-gather.14.cloned.1.call-update) | async-done | bytes 2621456 | tf_op jit(solution)/shard_map/all_gather | solution.py:109
  64.0 1.9 fusion.94
  65.9 1.3 copy.33
  69.8 3.0 gather_fusion.1
  72.8 2.1 gather_fusion.2
  75.0 1.6 fusion.98
  78.3 2.5 fusion.43
  81.5 1.4 fusion
  87.2 1.3 convolution_convert_fusion
  88.7 23.8 %all_to_all.29 = bf16[136,8,640]{2,0,1:T(8,128)(2,1)S(1)} all-to-all(bf16[136,8,640]{2,0,1:T(8,128)(2,1)S(1)} %bitcast.176), channel_id=1, replica_groups=mesh['ry'=4,'rz'=4,'mlp'=8] {'mlp'}, dimensions={1} | all-to-all | bytes 2785280 | tf_op jit(solution)/shard_map/all_to_all | solution.py:189
  113.5 12.9 %all-gather.2 = f32[8,1,640]{2,1,0:T(1,128)S(1)} all-gather(f32[1,1,640]{2,1,0:T(1,128)S(1)} %reshape.432), channel_id=2, replica_groups=mesh['ry'=4,'rz'=4,'mlp'=8] {'mlp'}, dimensions={0}, use_global_device_ids=true | all-gather | bytes 23040 | tf_op args[13]
  126.5 8.4 %all-gather.8.cloned.1.call-done = bf16[136,5120]{1,0:T(8,128)(2,1)} async-done(((bf16[136,640]{1,0:T(8,128)(2,1)}), bf16[136,5120]{1,0:T(8,128)(2,1)}) %all-gather.8.cloned.1.call-update) | async-done | bytes 1392656 | tf_op jit(solution)/shard_map/all_gather | solution.py:197
  135.0 1.7 multiply_reduce_fusion
  136.7 1.8 convert_element_type.70
  139.6 83.5 %all-gather.10.cloned.1.call-done = bf16[2176,2560]{1,0:T(8,128)(2,1)} async-done(((bf16[136,2560]{1,0:T(8,128)(2,1)}), bf16[2176,2560]{1,0:T(8,128)(2,1)}) %all-gather.10.cloned.1.call-update) | async-done | bytes 11141136 | tf_op jit(solution)/shard_map/all_gather | solution.py:206
  223.1 7.8 %fusion.48 = f32[2176,216]{0,1:T(8,128)S(1)} fusion(bf16[2176,2560]{1,0:T(8,128)(2,1)} %all-gather.10.cloned.1.call-done, bf16[5120,216]{0,1:T(8,128)(2,1)S(1)} %copy-done.21, s32[]{:T(128)S(6)} %select_n.78), kind=kOutput, calls=%fused_computation.57 | convolution fusion | flops 2406481920 | bytes 14127108 | tf_op jit(solution)/shard_map/dot_general | solution.py:213
  231.0 3.6 fusion.45
  234.6 5.9 %collective-permute-done = bf16[2176,2560]{1,0:T(8,128)(2,1)} collective-permute-done((bf16[2176,2560]{1,0:T(8,128)(2,1)}, bf16[2176,2560]{1,0:T(8,128)(2,1)}, u32[]{:S(2)}, u32[]{:S(2)}) %collective-permute-start) | collective-permute-done | bytes 11141152 | tf_op jit(solution)/shard_map/ppermute | solution.py:208
  240.5 7.7 %convolution_add_fusion.1 = f32[2176,216]{0,1:T(8,128)S(1)} fusion(f32[2176,216]{0,1:T(8,128)S(1)} %fusion.48, bf16[2176,2560]{1,0:T(8,128)(2,1)} %collective-permute-done, bf16[5120,216]{0,1:T(8,128)(2,1)S(1)} %copy-done.21, s32[]{:T(128)S(6)} %select_n.79), kind=kOutput, calls=%fused_computation.14 | convolution fusion | flops 2406951936 | bytes 16007172 | tf_op jit(solution)/shard_map/dot_general | solution.py:213
  248.2 9.0 %fusion.4 = bf16[2176,216]{0,1:T(8,128)(2,1)} fusion(f32[2176,216]{0,1:T(8,128)S(1)} %fusion.45, bf16[2176,2560]{1,0:T(8,128)(2,1)} %collective-permute-done, f32[2176,216]{0,1:T(8,128)S(1)} %convolution_add_fusion.1, bf16[5120,216]{0,1:T(8,128)(2,1)S(1)} %copy-done.22, s32[]{:T(128)S(6)} %select_n.79), kind=kOutput, calls=%fused_computation.13 | convolution fusion | flops 2409772032 | bytes 16947204 | tf_op jit(solution)/shard_map/dot_general | solution.py:213
  257.3 45.7 %all-gather.12.cloned.1.call-done = bf16[2176,1728]{0,1:T(8,128)(2,1)} async-done(((bf16[2176,216]{0,1:T(8,128)(2,1)}), bf16[2176,1728]{0,1:T(8,128)(2,1)}) %all-gather.12.cloned.1.call-update) | async-done | bytes 7520272 | tf_op jit(solution)/shard_map/all_gather | solution.py:220
  303.0 9.0 %convolution_convert_fusion.1 = bf16[2176,640]{1,0:T(8,128)(2,1)S(1)} fusion(bf16[2176,1728]{0,1:T(8,128)(2,1)} %all-gather.12.cloned.1.call-done, bf16[1728,640]{1,0:T(8,128)(2,1)S(1)} %copy-done.23), kind=kOutput, calls=%fused_computation.8 | convolution fusion | flops 4814356480 | bytes 12517376 | tf_op jit(solution)/shard_map/dot_general | solution.py:221
  312.3 38.7 %all_to_all.30 = bf16[4,4,136,640]{3,2,0,1:T(8,128)(2,1)} all-to-all(bf16[4,4,136,640]{3,2,0,1:T(8,128)(2,1)S(1)} %copy.39), channel_id=1, replica_groups=mesh['ry'=4,'rz'=4,'mlp'=8] {'rz'}, dimensions={1} | all-to-all | bytes 5570560 | tf_op jit(solution)/shard_map/all_to_all | solution.py:224
  351.0 3.3 reduce_sum.85
  354.3 14.9 %all_to_all.31 = bf16[4,136,640]{2,1,0:T(8,128)(2,1)S(1)} all-to-all(bf16[4,136,640]{2,1,0:T(8,128)(2,1)} %reduce_sum.85), channel_id=1, replica_groups=mesh['ry'=4,'rz'=4,'mlp'=8] {'ry'}, dimensions={0} | all-to-all | bytes 1392640 | tf_op jit(solution)/shard_map/all_to_all | solution.py:228
  (115 shorter events, 21.4 us)
Async XLA Ops:
  6.5 19.4 %copy-start = (bf16[3,4096,128]{2,1,0:T(8,128)(2,1)S(1)}, bf16[3,4096,128]{2,1,0:T(8,128)(2,1)}, u32[]{:S(2)}) copy-start(bf16[3,4096,128]{2,1,0:T(8,128)(2,1)} %param.21) | copy-start | bytes 9437188
  6.5 12.0 %copy-start.9 = (bf16[136,640]{1,0:T(8,128)(2,1)S(1)}, bf16[136,640]{1,0:T(8,128)(2,1)}, u32[]{:S(2)}) copy-start(bf16[136,640]{1,0:T(8,128)(2,1)} %param.18) | copy-start | bytes 522244
  6.5 12.7 %copy-start.24 = (s32[3]{0:T(128)S(1)}, s32[3]{0:T(128)}, u32[]{:S(2)}) copy-start(s32[3]{0:T(128)} %param.26) | copy-start | bytes 40
  6.5 13.3 %copy-start.2 = (s32[4]{0:T(128)S(1)}, s32[4]{0:T(128)}, u32[]{:S(2)}) copy-start(s32[4]{0:T(128)} %param.27) | copy-start | bytes 52
  6.5 17.8 %copy-start.19 = (s32[3]{0:T(128)S(1)}, s32[3]{0:T(128)}, u32[]{:S(2)}) copy-start(s32[3]{0:T(128)} %param.25) | copy-start | bytes 40
  6.5 57.4 %all-gather.14.cloned.1.call-start = ((), (), s32[]{:S(2)}) async-start(), calls=%async_computation.7 | async-start | bytes 2785280 | tf_op jit(solution)/shard_map/all_gather | solution.py:109
  10.3 28.6 %all-to-all-start = ((bf16[16,272,128]{2,1,0:T(8,128)(2,1)}), bf16[16,272,128]{2,1,0:T(8,128)(2,1)}, u32[]{:S(2)}, u32[]{:S(2)}) async-start(bf16[16,272,128]{2,1,0:T(8,128)(2,1)} %broadcast_in_dim.145), calls=%async_computation | async-start | bytes 2228224 | tf_op jit(solution)/shard_map/all_to_all | solution.py:112
  18.5 116.5 %all-gather.8.cloned.1.call-start = ((), (), s32[]{:S(2)}) async-start(), calls=%async_computation.4 | async-start | bytes 1566720 | tf_op jit(solution)/shard_map/all_gather | solution.py:197
  18.6 5.8 %copy-start.12 = (bf16[3,5,128]{2,1,0:T(8,128)(2,1)}, bf16[3,5,128]{2,1,0:T(8,128)(2,1)S(1)}, u32[]{:S(2)}) copy-start(bf16[3,5,128]{2,1,0:T(8,128)(2,1)S(1)} %reshape.381) | copy-start | bytes 11524
  25.9 2.3 copy-start.18
  28.2 13.5 %copy-start.3 = (bf16[133,5,128]{2,1,0:T(8,128)(2,1)S(1)}, bf16[133,5,128]{2,1,0:T(8,128)(2,1)}, u32[]{:S(2)}) copy-start(bf16[133,5,128]{2,1,0:T(8,128)(2,1)} %reshape.389) | copy-start | bytes 510724
  67.9 7.1 %copy-start.11 = (pred[3,1024]{1,0:T(4,128)(4,1)S(1)}, pred[3,1024]{1,0:T(4,128)(4,1)}, u32[]{:S(2)}) copy-start(pred[3,1024]{1,0:T(4,128)(4,1)} %iota_compare_fusion.2) | copy-start | bytes 9220
  67.9 7.1 %copy-start.13 = (bf16[3,5,128]{2,1,0:T(8,128)(2,1)S(1)}, bf16[3,5,128]{2,1,0:T(8,128)(2,1)}, u32[]{:S(2)}) copy-start(bf16[3,5,128]{2,1,0:T(8,128)(2,1)} %copy-done.12) | copy-start | bytes 11524
  67.9 13.6 %slice-start = ((s8[5918720]{0:T(1024)(128)(4,1)}), s8[1724416]{0:T(1024)(128)(4,1)S(1)}, s32[]{:S(2)}) async-start(s8[5918720]{0:T(1024)(128)(4,1)} %bitcast.168), calls=%async_computation.8 | async-start | bytes 3448832
  69.1 7.5 %copy-start.14 = (f32[3,5]{1,0:T(4,128)S(1)}, f32[3,5]{1,0:T(4,128)}, u32[]{:S(2)}) copy-start(f32[3,5]{1,0:T(4,128)} %get-tuple-element.26) | copy-start | bytes 184
  69.1 7.5 %copy-start.16 = (f32[3,1,5]{2,1,0:T(1,128)S(1)}, f32[3,1,5]{2,1,0:T(1,128)}, u32[]{:S(2)}) copy-start(f32[3,1,5]{2,1,0:T(1,128)} %fusion.79) | copy-start | bytes 184
  75.0 5.7 %copy-start.4 = (bf16[133,5,128]{2,1,0:T(8,128)(2,1)S(1)}, bf16[133,5,128]{2,1,0:T(8,128)(2,1)}, u32[]{:S(2)}) copy-start(bf16[133,5,128]{2,1,0:T(8,128)(2,1)} %reshape.389) | copy-start | bytes 510724
  75.0 5.7 %copy-start.6 = (bf16[1,16,64,128]{3,2,0,1:T(8,128)(2,1)S(1)}, bf16[1,16,64,128]{3,2,0,1:T(8,128)(2,1)}, u32[]{:S(2)}) copy-start(bf16[1,16,64,128]{3,2,0,1:T(8,128)(2,1)} %slice.58) | copy-start | bytes 786436
  75.0 5.7 %copy-start.15 = (pred[1024]{0:T(1024)(128)(4,1)S(1)}, pred[1024]{0:T(1024)(128)(4,1)}, u32[]{:S(2)}) copy-start(pred[1024]{0:T(1024)(128)(4,1)} %iota_compare_fusion.3) | copy-start | bytes 3076
  76.8 4.7 %slice-start.1 = ((s8[5918720]{0:T(1024)(128)(4,1)}), s8[4194304]{0:T(1024)(128)(4,1)S(1)}, s32[]{:S(2)}) async-start(s8[5918720]{0:T(1024)(128)(4,1)} %bitcast.168), calls=%async_computation.9 | async-start | bytes 8388608
  83.9 2.5 slice-start.2
  88.6 24.1 %copy-start.10 = (bf16[136,640]{1,0:T(8,128)(2,1)S(1)}, bf16[136,640]{1,0:T(8,128)(2,1)}, u32[]{:S(2)}) copy-start(bf16[136,640]{1,0:T(8,128)(2,1)} %param.17) | copy-start | bytes 522244
  88.7 24.9 %copy-start.17 = (f32[640]{0:T(1024)S(1)}, f32[640]{0:T(1024)}, u32[]{:S(2)}) copy-start(f32[640]{0:T(1024)} %param.30) | copy-start | bytes 7684
  113.4 109.6 %all-gather.10.cloned.1.call-start = ((), (), s32[]{:S(2)}) async-start(), calls=%async_computation.5 | async-start | bytes 11837440 | tf_op jit(solution)/shard_map/all_gather | solution.py:206
  136.7 86.4 %copy-start.21 = (bf16[5120,216]{0,1:T(8,128)(2,1)S(1)}, bf16[5120,216]{0,1:T(8,128)(2,1)}, u32[]{:S(2)}) copy-start(bf16[5120,216]{0,1:T(8,128)(2,1)} %param.31) | copy-start | bytes 6635524
  139.5 163.5 %all-gather.12.cloned.1.call-start = ((), (), s32[]{:S(2)}) async-start(), calls=%async_computation.6 | async-start | bytes 8460288 | tf_op jit(solution)/shard_map/all_gather | solution.py:220
  223.0 17.4 %collective-permute-start = (bf16[2176,2560]{1,0:T(8,128)(2,1)}, bf16[2176,2560]{1,0:T(8,128)(2,1)}, u32[]{:S(2)}, u32[]{:S(2)}) collective-permute-start(bf16[2176,2560]{1,0:T(8,128)(2,1)} %all-gather.10.cloned.1.call-done), channel_id=1, source_target_pairs={{0,1},{1,0},{2,3},{3,2},{4,5},{5,4},{6,7},{7,6},{8,9},{9,8},{10,11... | collective-permute-start | bytes 33423368 | tf_op jit(solution)/shard_map/ppermute | solution.py:208
  223.1 7.9 %copy-start.20 = (bf16[2176,2560]{1,0:T(8,128)(2,1)S(1)}, bf16[2176,2560]{1,0:T(8,128)(2,1)}, u32[]{:S(2)}) copy-start(bf16[2176,2560]{1,0:T(8,128)(2,1)} %all-gather.10.cloned.1.call-done) | copy-start | bytes 33423364
  223.1 8.0 %copy-start.22 = (bf16[5120,216]{0,1:T(8,128)(2,1)S(1)}, bf16[5120,216]{0,1:T(8,128)(2,1)}, u32[]{:S(2)}) copy-start(bf16[5120,216]{0,1:T(8,128)(2,1)} %param.32) | copy-start | bytes 6635524
  248.2 54.8 %copy-start.23 = (bf16[1728,640]{1,0:T(8,128)(2,1)S(1)}, bf16[1728,640]{1,0:T(8,128)(2,1)}, u32[]{:S(2)}) copy-start(bf16[1728,640]{1,0:T(8,128)(2,1)} %param.33) | copy-start | bytes 6635524
  312.3 57.7 %copy-start.1 = (bf16[3,4096,128]{2,1,0:T(8,128)(2,1)S(1)}, bf16[3,4096,128]{2,1,0:T(8,128)(2,1)}, u32[]{:S(2)}) copy-start(bf16[3,4096,128]{2,1,0:T(8,128)(2,1)} %param.21) | copy-start | bytes 9437188
  351.0 18.3 %copy-start.5 = (bf16[136,640]{1,0:T(8,128)(2,1)S(1)}, bf16[136,640]{1,0:T(8,128)(2,1)}, u32[]{:S(2)}) copy-start(bf16[136,640]{1,0:T(8,128)(2,1)} %add_convert_fusion.1) | copy-start | bytes 522244
  (3 other events, 4.3 us)
Sparse Core Ops, SparseCore 0:
  9.5 54.4 all-gather.13
  113.6 21.3 all-gather.7
  139.6 83.3 all-gather.9
  257.4 45.5 all-gather.11

commit v9 on v6

--- a/solution.py
+++ b/solution.py
@@ -213,8 +213,10 @@
             far_rows, far_weight, preferred_element_type=jnp.float32
         )
 
-    gate_proj = project(gate_weight)
-    up_proj = project(up_weight)
+    width = gate_weight.shape[1]
+    both_proj = project(jnp.concatenate([gate_weight, up_weight], 1))
+    gate_proj = both_proj[:, :width]
+    up_proj = both_proj[:, width:]
     hidden = (jax.nn.silu(gate_proj) * up_proj).astype(jnp.bfloat16)
     hidden_block = lax.all_gather(hidden, "mlp", axis=1, tiled=True)
     down_partial = jnp.dot(hidden_block, down_weight, preferred_element_type=jnp.float32)

time: 364 us -> 357 us (0.981)
  matrix products: 52.2 us -> 40.9 us
    dot_general x2 -> x1, matrix products: 16.8 us -> 8.49 us  [project(): jnp.dot(far_rows, far_weight, preferred_element_type=jnp.float32)]
    dot_general x2 -> x1, matrix products: 11.5 us -> 8.42 us  [project(): jnp.dot(near_rows, near_weight, preferred_element_type=jnp.float32)]
  transfers between devices with their start and end apart: 6 -> 6, of which waited for: 6 -> 6; matrix products, arithmetic and copies ran while one was open for 8% -> 7% of each run, Pallas kernels for 0% -> 0%
where the time goes in v9:
time: 357 us
  waiting for transfers between devices  174 us (49%)
  blocking collectives  79.7 us (22%)
  matrix products  40.9 us (11%)
  local copies, waits for them, and re-layouts  21.1 us (6%)
  other arithmetic  18.2 us (5%)
  between operations  14.2 us (4%)
  starting transfers between devices  8.37 us (2%)
    all_gather x1, waiting for transfers between devices, per_device(): near_rows = lax.all_gather(normed, 'req', axis=0, tiled=True)  83.5 us
    all_gather x1, waiting for transfers between devices, per_device(): hidden_block = lax.all_gather(hidden, 'mlp', axis=1, tiled=True)  45.7 us
    all_to_all x1, blocking collectives, per_device(): lax.all_to_all(down_partial.astype(jnp.bfloat16), 'req', 0, 0, tiled=True)  43 us
    all_to_all x1, blocking collectives, per_device(): lax.all_to_all(head_partial.astype(jnp.bfloat16), 'mlp', 1, 0, tiled=True)  23.8 us
    all_gather x1, waiting for transfers between devices, per_device(): context_gathered = lax.all_gather(context_pack, 'req', axis=0, tiled=False)  18.5 us
    unnamed x1, blocking collectives  12.9 us
    all_to_all x1, waiting for transfers between devices, per_device(): lax.all_to_all(new_copies.reshape(req_count * new_pack.shape[0], -1), 're...  10.5 us
    dot_general x1, matrix products, per_device(): jnp.dot(hidden_block, down_weight, preferred_element_type=jnp.float32)  9.03 us
  transfers between devices with their start and end apart: 6, of which 6 were waited for; matrix products, arithmetic and copies ran while one was open for 7% of the time, Pallas kernels for 0%

profile of v9, /device:TPU:0, one launch (start us, length us, event | category | flops | bytes accessed | tf_op | source)
XLA Modules:
  0.0 356.5 jit_solution(12019672314609117947)
XLA Ops:
  6.6 1.8 pad_maximum_fusion
  10.3 8.2 %all-to-all-start = ((bf16[16,272,128]{2,1,0:T(8,128)(2,1)}), bf16[16,272,128]{2,1,0:T(8,128)(2,1)}, u32[]{:S(2)}, u32[]{:S(2)}) async-start(bf16[16,272,128]{2,1,0:T(8,128)(2,1)} %broadcast_in_dim.145), calls=%async_computation | async-start | bytes 2228224 | tf_op jit(solution)/shard_map/all_to_all | solution.py:111
  21.8 1.2 slice_convert_fusion
  25.9 2.2 fusion.91
  28.4 10.5 %all-to-all-done = bf16[16,272,128]{2,1,0:T(8,128)(2,1)} async-done(((bf16[16,272,128]{2,1,0:T(8,128)(2,1)}), bf16[16,272,128]{2,1,0:T(8,128)(2,1)}, u32[]{:S(2)}, u32[]{:S(2)}) %all-to-all-start) | async-done | bytes 1114144 | tf_op jit(solution)/shard_map/all_to_all | solution.py:111
  38.9 1.6 fusion.89
  41.7 3.7 %fusion.90 = (f32[133,5]{0,1:T(8,128)S(1)}, f32[133,1,5,2128]{3,0,2,1:T(8,128)}) fusion(bf16[2128,128,1]{1,0,2:T(8,128)(2,1)S(1)} %reshape.438, bf16[133,5,128]{2,1,0:T(8,128)(2,1)S(1)} %copy-done.5, pred[133,2128]{1,0:T(8,128)(4,1)S(1)} %iota_compare_fusion), kind=kOutput, calls=%fused_computation.124 | convolution fusion | flops 366515392 | bytes 6661172 | tf_op jit(solution)/shard_map/jkgd,ckd->jkgc/dot_general | solution.py:163
  45.4 18.5 %all-gather.14.cloned.1.call-done = bf16[10240,128]{1,0:T(8,128)(2,1)} async-done(((bf16[640,128]{1,0:T(8,128)(2,1)}), bf16[10240,128]{1,0:T(8,128)(2,1)}) %all-gather.14.cloned.1.call-update) | async-done | bytes 2621456 | tf_op jit(solution)/shard_map/all_gather | solution.py:108
  64.0 1.9 fusion.88
  66.6 1.3 copy.27
  68.6 1.2 copy.26
  69.8 2.1 gather_fusion.2
  71.9 3.0 gather_fusion.1
  75.0 1.6 fusion.92
  78.2 2.5 fusion.45
  81.5 1.4 fusion
  84.9 1.2 fusion.52
  87.1 1.3 convolution_convert_fusion
  88.6 23.8 %all_to_all.28 = bf16[136,8,640]{2,0,1:T(8,128)(2,1)S(1)} all-to-all(bf16[136,8,640]{2,0,1:T(8,128)(2,1)S(1)} %bitcast.174), channel_id=1, replica_groups=mesh['req'=16,'mlp'=8] {'mlp'}, dimensions={1} | all-to-all | bytes 2785280 | tf_op jit(solution)/shard_map/all_to_all | solution.py:188
  113.5 12.9 %all-gather.2 = f32[8,1,640]{2,1,0:T(1,128)S(1)} all-gather(f32[1,1,640]{2,1,0:T(1,128)S(1)} %reshape.432), channel_id=2, replica_groups=mesh['req'=16,'mlp'=8] {'mlp'}, dimensions={0}, use_global_device_ids=true | all-gather | bytes 23040 | tf_op args[13]
  126.5 8.4 %all-gather.8.cloned.1.call-done = bf16[136,5120]{1,0:T(8,128)(2,1)} async-done(((bf16[136,640]{1,0:T(8,128)(2,1)}), bf16[136,5120]{1,0:T(8,128)(2,1)}) %all-gather.8.cloned.1.call-update) | async-done | bytes 1392656 | tf_op jit(solution)/shard_map/all_gather | solution.py:196
  134.9 1.7 multiply_reduce_fusion
  136.6 1.8 convert_element_type.68
  139.6 83.5 %all-gather.10.cloned.1.call-done = bf16[2176,2560]{1,0:T(8,128)(2,1)} async-done(((bf16[136,2560]{1,0:T(8,128)(2,1)}), bf16[2176,2560]{1,0:T(8,128)(2,1)}) %all-gather.10.cloned.1.call-update) | async-done | bytes 11141136 | tf_op jit(solution)/shard_map/all_gather | solution.py:205
  223.2 1.5 copy-done.4
  224.8 8.4 %fusion.12 = f32[2176,432]{0,1:T(8,128)S(1)} fusion(bf16[2176,2560]{1,0:T(8,128)(2,1)} %all-gather.10.cloned.1.call-done, bf16[5120,432]{0,1:T(8,128)(2,1)S(1)} %constant_dynamic-update-slice_fusion, s32[]{:T(128)S(6)} %select_n.76), kind=kOutput, calls=%fused_computation.26 | convolution fusion | flops 4812963840 | bytes 17113092 | tf_op jit(solution)/shard_map/dot_general | solution.py:212
  233.2 7.2 %collective-permute-done = bf16[2176,2560]{1,0:T(8,128)(2,1)} collective-permute-done((bf16[2176,2560]{1,0:T(8,128)(2,1)}, bf16[2176,2560]{1,0:T(8,128)(2,1)}, u32[]{:S(2)}, u32[]{:S(2)}) %collective-permute-start) | collective-permute-done | bytes 11141152 | tf_op jit(solution)/shard_map/ppermute | solution.py:207
  240.5 8.5 %convolution_add_fusion = f32[2176,432]{0,1:T(8,128)S(1)} fusion(f32[2176,432]{0,1:T(8,128)S(1)} %fusion.12, bf16[2176,2560]{1,0:T(8,128)(2,1)} %collective-permute-done, bf16[5120,432]{0,1:T(8,128)(2,1)S(1)} %constant_dynamic-update-slice_fusion, s32[]{:T(128)S(6)} %select_n.77), kind=kOutput, calls=%fused_computation.10 | convolution fusion | flops 4813903872 | bytes 20873220 | tf_op jit(solution)/shard_map/dot_general | solution.py:212
  249.0 1.6 fusion.16
  250.6 45.7 %all-gather.12.cloned.1.call-done = bf16[2176,1728]{0,1:T(8,128)(2,1)} async-done(((bf16[2176,216]{0,1:T(8,128)(2,1)}), bf16[2176,1728]{0,1:T(8,128)(2,1)}) %all-gather.12.cloned.1.call-update) | async-done | bytes 7520272 | tf_op jit(solution)/shard_map/all_gather | solution.py:221
  296.3 9.0 %convolution_convert_fusion.1 = bf16[2176,640]{1,0:T(8,128)(2,1)S(1)} fusion(bf16[2176,1728]{0,1:T(8,128)(2,1)} %all-gather.12.cloned.1.call-done, bf16[1728,640]{1,0:T(8,128)(2,1)S(1)} %copy-done.23), kind=kOutput, calls=%fused_computation.9 | convolution fusion | flops 4814356480 | bytes 12517376 | tf_op jit(solution)/shard_map/dot_general | solution.py:222
  305.4 43.0 %all_to_all.29 = bf16[16,136,640]{2,1,0:T(8,128)(2,1)S(1)} all-to-all(bf16[16,136,640]{2,1,0:T(8,128)(2,1)S(1)} %bitcast.178), channel_id=1, replica_groups=mesh['req'=16,'mlp'=8] {'req'}, dimensions={0} | all-to-all | bytes 5570560 | tf_op jit(solution)/shard_map/all_to_all | solution.py:223
  (113 shorter events, 19.9 us)
Async XLA Ops:
  6.5 19.4 %copy-start = (bf16[3,4096,128]{2,1,0:T(8,128)(2,1)S(1)}, bf16[3,4096,128]{2,1,0:T(8,128)(2,1)}, u32[]{:S(2)}) copy-start(bf16[3,4096,128]{2,1,0:T(8,128)(2,1)} %param.21) | copy-start | bytes 9437188
  6.5 12.7 %copy-start.11 = (bf16[136,640]{1,0:T(8,128)(2,1)S(1)}, bf16[136,640]{1,0:T(8,128)(2,1)}, u32[]{:S(2)}) copy-start(bf16[136,640]{1,0:T(8,128)(2,1)} %param.18) | copy-start | bytes 522244
  6.5 12.7 %copy-start.24 = (s32[3]{0:T(128)S(1)}, s32[3]{0:T(128)}, u32[]{:S(2)}) copy-start(s32[3]{0:T(128)} %param.26) | copy-start | bytes 40
  6.5 13.3 %copy-start.2 = (s32[4]{0:T(128)S(1)}, s32[4]{0:T(128)}, u32[]{:S(2)}) copy-start(s32[4]{0:T(128)} %param.27) | copy-start | bytes 52
  6.5 17.8 %copy-start.22 = (s32[3]{0:T(128)S(1)}, s32[3]{0:T(128)}, u32[]{:S(2)}) copy-start(s32[3]{0:T(128)} %param.25) | copy-start | bytes 40
  6.5 57.4 %all-gather.14.cloned.1.call-start = ((), (), s32[]{:S(2)}) async-start(), calls=%async_computation.6 | async-start | bytes 2785280 | tf_op jit(solution)/shard_map/all_gather | solution.py:108
  10.3 28.6 %all-to-all-start = ((bf16[16,272,128]{2,1,0:T(8,128)(2,1)}), bf16[16,272,128]{2,1,0:T(8,128)(2,1)}, u32[]{:S(2)}, u32[]{:S(2)}) async-start(bf16[16,272,128]{2,1,0:T(8,128)(2,1)} %broadcast_in_dim.145), calls=%async_computation | async-start | bytes 2228224 | tf_op jit(solution)/shard_map/all_to_all | solution.py:111
  18.5 116.4 %all-gather.8.cloned.1.call-start = ((), (), s32[]{:S(2)}) async-start(), calls=%async_computation.3 | async-start | bytes 1566720 | tf_op jit(solution)/shard_map/all_gather | solution.py:196
  19.2 5.2 %copy-start.14 = (bf16[3,5,128]{2,1,0:T(8,128)(2,1)}, bf16[3,5,128]{2,1,0:T(8,128)(2,1)S(1)}, u32[]{:S(2)}) copy-start(bf16[3,5,128]{2,1,0:T(8,128)(2,1)S(1)} %reshape.382) | copy-start | bytes 11524
  25.9 2.2 copy-start.21
  28.2 13.6 %copy-start.5 = (bf16[133,5,128]{2,1,0:T(8,128)(2,1)S(1)}, bf16[133,5,128]{2,1,0:T(8,128)(2,1)}, u32[]{:S(2)}) copy-start(bf16[133,5,128]{2,1,0:T(8,128)(2,1)} %reshape.390) | copy-start | bytes 510724
  68.6 6.4 %copy-start.13 = (pred[3,1024]{1,0:T(4,128)(4,1)S(1)}, pred[3,1024]{1,0:T(4,128)(4,1)}, u32[]{:S(2)}) copy-start(pred[3,1024]{1,0:T(4,128)(4,1)} %iota_compare_fusion.2) | copy-start | bytes 9220
  68.6 6.4 %copy-start.15 = (bf16[3,5,128]{2,1,0:T(8,128)(2,1)S(1)}, bf16[3,5,128]{2,1,0:T(8,128)(2,1)}, u32[]{:S(2)}) copy-start(bf16[3,5,128]{2,1,0:T(8,128)(2,1)} %copy-done.14) | copy-start | bytes 11524
  68.6 8.0 %copy-start.16 = (f32[3,5]{1,0:T(4,128)S(1)}, f32[3,5]{1,0:T(4,128)}, u32[]{:S(2)}) copy-start(f32[3,5]{1,0:T(4,128)} %get-tuple-element.26) | copy-start | bytes 184
  68.6 8.0 %copy-start.19 = (f32[3,1,5]{2,1,0:T(1,128)S(1)}, f32[3,1,5]{2,1,0:T(1,128)}, u32[]{:S(2)}) copy-start(f32[3,1,5]{2,1,0:T(1,128)} %fusion.75) | copy-start | bytes 184
  68.6 12.8 %slice-start = ((s8[5918720]{0:T(1024)(128)(4,1)}), s8[1724416]{0:T(1024)(128)(4,1)S(1)}, s32[]{:S(2)}) async-start(s8[5918720]{0:T(1024)(128)(4,1)} %bitcast.166), calls=%async_computation.7 | async-start | bytes 3448832
  69.8 8.4 %copy-start.18 = (f32[3,128]{1,0:T(4,128)S(1)}, f32[3,128]{1,0:T(4,128)}, u32[]{:S(2)}) copy-start(f32[3,128]{1,0:T(4,128)} %slice_convert_fusion) | copy-start | bytes 4612
  75.0 5.7 %copy-start.6 = (bf16[133,5,128]{2,1,0:T(8,128)(2,1)S(1)}, bf16[133,5,128]{2,1,0:T(8,128)(2,1)}, u32[]{:S(2)}) copy-start(bf16[133,5,128]{2,1,0:T(8,128)(2,1)} %reshape.390) | copy-start | bytes 510724
  75.0 5.7 %copy-start.8 = (bf16[1,16,64,128]{3,2,0,1:T(8,128)(2,1)S(1)}, bf16[1,16,64,128]{3,2,0,1:T(8,128)(2,1)}, u32[]{:S(2)}) copy-start(bf16[1,16,64,128]{3,2,0,1:T(8,128)(2,1)} %slice.66) | copy-start | bytes 786436
  75.0 5.7 %copy-start.17 = (pred[1024]{0:T(1024)(128)(4,1)S(1)}, pred[1024]{0:T(1024)(128)(4,1)}, u32[]{:S(2)}) copy-start(pred[1024]{0:T(1024)(128)(4,1)} %iota_compare_fusion.3) | copy-start | bytes 3076
  76.8 4.7 %slice-start.1 = ((s8[5918720]{0:T(1024)(128)(4,1)}), s8[4194304]{0:T(1024)(128)(4,1)S(1)}, s32[]{:S(2)}) async-start(s8[5918720]{0:T(1024)(128)(4,1)} %bitcast.166), calls=%async_computation.8 | async-start | bytes 8388608
  83.8 2.5 slice-start.2
  84.9 2.3 slice-start.3
  88.6 24.1 %copy-start.12 = (bf16[136,640]{1,0:T(8,128)(2,1)S(1)}, bf16[136,640]{1,0:T(8,128)(2,1)}, u32[]{:S(2)}) copy-start(bf16[136,640]{1,0:T(8,128)(2,1)} %param.17) | copy-start | bytes 522244
  88.6 24.9 %copy-start.20 = (f32[640]{0:T(1024)S(1)}, f32[640]{0:T(1024)}, u32[]{:S(2)}) copy-start(f32[640]{0:T(1024)} %param.30) | copy-start | bytes 7684
  113.4 109.6 %all-gather.10.cloned.1.call-start = ((), (), s32[]{:S(2)}) async-start(), calls=%async_computation.4 | async-start | bytes 11837440 | tf_op jit(solution)/shard_map/all_gather | solution.py:205
  136.6 86.4 %copy-start.3 = (bf16[5120,216]{0,1:T(8,128)(2,1)S(1)}, bf16[5120,216]{0,1:T(8,128)(2,1)}, u32[]{:S(2)}) copy-start(bf16[5120,216]{0,1:T(8,128)(2,1)} %param.31) | copy-start | bytes 6635524
  139.5 156.8 %all-gather.12.cloned.1.call-start = ((), (), s32[]{:S(2)}) async-start(), calls=%async_computation.5 | async-start | bytes 8460288 | tf_op jit(solution)/shard_map/all_gather | solution.py:221
  223.0 17.4 %collective-permute-start = (bf16[2176,2560]{1,0:T(8,128)(2,1)}, bf16[2176,2560]{1,0:T(8,128)(2,1)}, u32[]{:S(2)}, u32[]{:S(2)}) collective-permute-start(bf16[2176,2560]{1,0:T(8,128)(2,1)} %all-gather.10.cloned.1.call-done), channel_id=1, source_target_pairs={{0,1},{1,0},{2,3},{3,2},{4,5},{5,4},{6,7},{7,6},{8,9},{9,8},{10,11... | collective-permute-start | bytes 33423368 | tf_op jit(solution)/shard_map/ppermute | solution.py:207
  223.0 1.6 copy-start.4
  249.0 47.3 %copy-start.23 = (bf16[1728,640]{1,0:T(8,128)(2,1)S(1)}, bf16[1728,640]{1,0:T(8,128)(2,1)}, u32[]{:S(2)}) copy-start(bf16[1728,640]{1,0:T(8,128)(2,1)} %param.33) | copy-start | bytes 6635524
  305.4 44.6 %copy-start.1 = (bf16[3,4096,128]{2,1,0:T(8,128)(2,1)S(1)}, bf16[3,4096,128]{2,1,0:T(8,128)(2,1)}, u32[]{:S(2)}) copy-start(bf16[3,4096,128]{2,1,0:T(8,128)(2,1)} %param.21) | copy-start | bytes 9437188
  (3 other events, 2.9 us)
Sparse Core Ops, SparseCore 0:
  9.5 54.4 all-gather.13
  113.5 21.3 all-gather.7
  139.6 83.3 all-gather.9
  250.7 45.5 all-gather.11

commit v10 on v9

--- a/solution.py
+++ b/solution.py
@@ -204,13 +204,21 @@
     ).astype(jnp.bfloat16)
     near_rows = lax.all_gather(normed, "req", axis=0, tiled=True)
     pairs = [(i, i ^ 1) for i in range(mlp_count)]
-    far_rows = lax.ppermute(near_rows, "mlp", pairs)
+    quarter = half // 2
+    far_parts = [
+        lax.ppermute(near_rows[:, :quarter], "mlp", pairs),
+        lax.ppermute(near_rows[:, quarter:], "mlp", pairs),
+    ]
 
     def project(weight):
         near_weight = lax.dynamic_slice_in_dim(weight, side * half, half, axis=0)
         far_weight = lax.dynamic_slice_in_dim(weight, (1 - side) * half, half, axis=0)
-        return jnp.dot(near_rows, near_weight, preferred_element_type=jnp.float32) + jnp.dot(
-            far_rows, far_weight, preferred_element_type=jnp.float32
+        total = jnp.dot(near_rows, near_weight, preferred_element_type=jnp.float32)
+        total = total + jnp.dot(
+            far_parts[0], far_weight[:quarter], preferred_element_type=jnp.float32
+        )
+        return total + jnp.dot(
+            far_parts[1], far_weight[quarter:], preferred_element_type=jnp.float32
         )
 
     width = gate_weight.shape[1]

time: 357 us -> 360 us (level)
  waiting for transfers between devices: 174 us -> 168 us
  matrix products: 40.9 us -> 46.1 us
  local copies, waits for them, and re-layouts: 21.1 us -> 25.4 us
    slice x0 -> x1, local copies, waits for them, and re-layouts: none -> 9.02 us  [per_device(): near_rows[:, quarter:]]
    ppermute x1 -> x2, waiting for transfers between devices: 7.23 us -> 1.42 us  [the longest x1 1.42 us: per_device(): lax.ppermute(near_rows[:, quarter:], 'mlp', pairs)]
    dot_general x2 -> x3, matrix products: 16.9 us -> 19.1 us  [the longest x1 8.35 us: project(): total = jnp.dot(near_rows, near_weight, preferred_element_type=jnp.float32)]
  transfers between devices with their start and end apart: 6 -> 7, of which waited for: 6 -> 6; matrix products, arithmetic and copies ran while one was open for 7% -> 9% of each run, Pallas kernels for 0% -> 0%
where the time goes in v10:
time: 360 us
  waiting for transfers between devices  168 us (47%)
  blocking collectives  79.7 us (22%)
  matrix products  46.1 us (13%)
  local copies, waits for them, and re-layouts  25.4 us (7%)
  other arithmetic  17.3 us (5%)
  between operations  14.3 us (4%)
  starting transfers between devices  8.88 us (2%)
    all_gather x1, waiting for transfers between devices, per_device(): near_rows = lax.all_gather(normed, 'req', axis=0, tiled=True)  83.5 us
    all_gather x1, waiting for transfers between devices, per_device(): hidden_block = lax.all_gather(hidden, 'mlp', axis=1, tiled=True)  45.7 us
    all_to_all x1, blocking collectives, per_device(): lax.all_to_all(down_partial.astype(jnp.bfloat16), 'req', 0, 0, tiled=True)  43 us
    all_to_all x1, blocking collectives, per_device(): lax.all_to_all(head_partial.astype(jnp.bfloat16), 'mlp', 1, 0, tiled=True)  23.8 us
    all_gather x1, waiting for transfers between devices, per_device(): context_gathered = lax.all_gather(context_pack, 'req', axis=0, tiled=False)  18.5 us
    unnamed x1, blocking collectives  12.9 us
    all_to_all x1, waiting for transfers between devices, per_device(): lax.all_to_all(new_copies.reshape(req_count * new_pack.shape[0], -1), 're...  10.4 us
    dot_general x1, matrix products, per_device(): jnp.dot(hidden_block, down_weight, preferred_element_type=jnp.float32)  9.03 us
  transfers between devices with their start and end apart: 7, of which 6 were waited for; matrix products, arithmetic and copies ran while one was open for 9% of the time, Pallas kernels for 0%

profile of v10, /device:TPU:0, one launch (start us, length us, event | category | flops | bytes accessed | tf_op | source)
XLA Modules:
  0.0 359.6 jit_solution(8417572861825804556)
XLA Ops:
  6.6 1.8 pad_maximum_fusion
  10.3 8.2 %all-to-all-start = ((bf16[16,272,128]{2,1,0:T(8,128)(2,1)}), bf16[16,272,128]{2,1,0:T(8,128)(2,1)}, u32[]{:S(2)}, u32[]{:S(2)}) async-start(bf16[16,272,128]{2,1,0:T(8,128)(2,1)} %broadcast_in_dim.145), calls=%async_computation | async-start | bytes 2228224 | tf_op jit(solution)/shard_map/all_to_all | solution.py:111
  21.8 1.2 slice_convert_fusion
  26.0 2.3 fusion.94
  28.6 10.4 %all-to-all-done = bf16[16,272,128]{2,1,0:T(8,128)(2,1)} async-done(((bf16[16,272,128]{2,1,0:T(8,128)(2,1)}), bf16[16,272,128]{2,1,0:T(8,128)(2,1)}, u32[]{:S(2)}, u32[]{:S(2)}) %all-to-all-start) | async-done | bytes 1114144 | tf_op jit(solution)/shard_map/all_to_all | solution.py:111
  38.9 1.6 fusion.92
  41.7 3.7 %fusion.93 = (f32[133,5]{0,1:T(8,128)S(1)}, f32[133,1,5,2128]{3,0,2,1:T(8,128)}) fusion(bf16[2128,128,1]{1,0,2:T(8,128)(2,1)S(1)} %reshape.438, bf16[133,5,128]{2,1,0:T(8,128)(2,1)S(1)} %copy-done.7, pred[133,2128]{1,0:T(8,128)(4,1)S(1)} %iota_compare_fusion), kind=kOutput, calls=%fused_computation.128 | convolution fusion | flops 366515392 | bytes 6661172 | tf_op jit(solution)/shard_map/jkgd,ckd->jkgc/dot_general | solution.py:163
  45.5 18.5 %all-gather.14.cloned.1.call-done = bf16[10240,128]{1,0:T(8,128)(2,1)} async-done(((bf16[640,128]{1,0:T(8,128)(2,1)}), bf16[10240,128]{1,0:T(8,128)(2,1)}) %all-gather.14.cloned.1.call-update) | async-done | bytes 2621456 | tf_op jit(solution)/shard_map/all_gather | solution.py:108
  64.0 2.0 fusion.91
  66.1 1.3 copy.27
  69.3 1.4 fusion
  72.7 1.4 fusion.53
  74.3 1.8 gather_fusion.2
  77.6 1.4 fusion.70
  79.2 2.5 fusion.44
  81.7 4.1 %convolution_convert_fusion = bf16[136,5120]{1,0:T(8,128)(2,1)S(1)} fusion(bf16[640,5120]{1,0:T(8,128)(2,1)} %param.29, bf16[133,640]{1,0:T(8,128)(2,1)S(1)} %bitcast.182, bf16[3,640]{1,0:T(4,128)(2,1)S(1)} %bitcast.187), kind=kOutput, calls=%fused_computation.3 | convolution fusion | flops 892334080 | bytes 8120320 | tf_op jit(solution)/shard_map/dot_general | solution.py:187
  86.0 23.8 %all_to_all.28 = bf16[136,8,640]{2,0,1:T(8,128)(2,1)S(1)} all-to-all(bf16[136,8,640]{2,0,1:T(8,128)(2,1)S(1)} %bitcast.173), channel_id=1, replica_groups=mesh['req'=16,'mlp'=8] {'mlp'}, dimensions={1} | all-to-all | bytes 2785280 | tf_op jit(solution)/shard_map/all_to_all | solution.py:188
  110.9 12.9 %all-gather.2 = f32[8,1,640]{2,1,0:T(1,128)S(1)} all-gather(f32[1,1,640]{2,1,0:T(1,128)S(1)} %reshape.432), channel_id=2, replica_groups=mesh['req'=16,'mlp'=8] {'mlp'}, dimensions={0}, use_global_device_ids=true | all-gather | bytes 23040 | tf_op args[13]
  123.9 8.4 %all-gather.8.cloned.1.call-done = bf16[136,5120]{1,0:T(8,128)(2,1)} async-done(((bf16[136,640]{1,0:T(8,128)(2,1)}), bf16[136,5120]{1,0:T(8,128)(2,1)}) %all-gather.8.cloned.1.call-update) | async-done | bytes 1392656 | tf_op jit(solution)/shard_map/all_gather | solution.py:196
  132.3 1.7 multiply_reduce_fusion
  134.0 1.6 convert_element_type.68
  136.8 83.5 %all-gather.10.cloned.1.call-done = bf16[2176,2560]{1,0:T(8,128)(2,1)} async-done(((bf16[136,2560]{1,0:T(8,128)(2,1)}), bf16[2176,2560]{1,0:T(8,128)(2,1)}) %all-gather.10.cloned.1.call-update) | async-done | bytes 11141136 | tf_op jit(solution)/shard_map/all_gather | solution.py:205
  220.2 9.0 %fusion.90 = (bf16[2176,1280]{1,0:T(8,128)(2,1)}, bf16[2176,1280]{1,0:T(8,128)(2,1)}) fusion(bf16[2176,2560]{1,0:T(8,128)(2,1)} %all-gather.10.cloned.1.call-done), kind=kLoop, calls=%fused_computation.125 | loop fusion | bytes 22282240 | tf_op jit(solution)/shard_map/slice | solution.py:210
  229.9 1.5 copy-done.6
  231.5 8.4 %fusion.11 = f32[2176,432]{0,1:T(8,128)S(1)} fusion(bf16[2176,2560]{1,0:T(8,128)(2,1)} %all-gather.10.cloned.1.call-done, bf16[5120,432]{0,1:T(8,128)(2,1)S(1)} %constant_dynamic-update-slice_fusion, s32[]{:T(128)S(6)} %select_n.76), kind=kOutput, calls=%fused_computation.26 | convolution fusion | flops 4812963840 | bytes 17113092 | tf_op jit(solution)/shard_map/dot_general | solution.py:216
  239.9 5.4 %convolution_add_fusion.1 = f32[2176,432]{0,1:T(8,128)S(1)} fusion(f32[2176,432]{0,1:T(8,128)S(1)} %fusion.11, bf16[2176,1280]{1,0:T(8,128)(2,1)} %collective-permute-done, bf16[5120,432]{0,1:T(8,128)(2,1)S(1)} %constant_dynamic-update-slice_fusion, s32[]{:T(128)S(6)} %select_n.77), kind=kOutput, calls=%fused_computation.11 | convolution fusion | flops 2407421952 | bytes 14196740 | tf_op jit(solution)/shard_map/dot_general | solution.py:217
  245.3 1.4 collective-permute-done.1
  246.7 5.4 %convolution_add_fusion = f32[2176,432]{0,1:T(8,128)S(1)} fusion(f32[2176,432]{0,1:T(8,128)S(1)} %convolution_add_fusion.1, bf16[2176,1280]{1,0:T(8,128)(2,1)} %collective-permute-done.1, bf16[5120,432]{0,1:T(8,128)(2,1)S(1)} %constant_dynamic-update-slice_fusion, s32[]{:T(128)S(6)} %add.138), kind=kOutput, calls=%fused_computation.10 | convolution fusion | flops 2407421952 | bytes 14196740 | tf_op jit(solution)/shard_map/dot_general | solution.py:220
  252.1 1.6 fusion.15
  253.7 45.7 %all-gather.12.cloned.1.call-done = bf16[2176,1728]{0,1:T(8,128)(2,1)} async-done(((bf16[2176,216]{0,1:T(8,128)(2,1)}), bf16[2176,1728]{0,1:T(8,128)(2,1)}) %all-gather.12.cloned.1.call-update) | async-done | bytes 7520272 | tf_op jit(solution)/shard_map/all_gather | solution.py:229
  299.4 9.0 %convolution_convert_fusion.1 = bf16[2176,640]{1,0:T(8,128)(2,1)S(1)} fusion(bf16[2176,1728]{0,1:T(8,128)(2,1)} %all-gather.12.cloned.1.call-done, bf16[1728,640]{1,0:T(8,128)(2,1)S(1)} %copy-done.23), kind=kOutput, calls=%fused_computation.9 | convolution fusion | flops 4814356480 | bytes 12517376 | tf_op jit(solution)/shard_map/dot_general | solution.py:230
  308.5 43.0 %all_to_all.29 = bf16[16,136,640]{2,1,0:T(8,128)(2,1)S(1)} all-to-all(bf16[16,136,640]{2,1,0:T(8,128)(2,1)S(1)} %bitcast.177), channel_id=1, replica_groups=mesh['req'=16,'mlp'=8] {'req'}, dimensions={0} | all-to-all | bytes 5570560 | tf_op jit(solution)/shard_map/all_to_all | solution.py:231
  (112 shorter events, 19.4 us)
Async XLA Ops:
  6.5 19.5 %copy-start = (bf16[3,4096,128]{2,1,0:T(8,128)(2,1)S(1)}, bf16[3,4096,128]{2,1,0:T(8,128)(2,1)}, u32[]{:S(2)}) copy-start(bf16[3,4096,128]{2,1,0:T(8,128)(2,1)} %param.21) | copy-start | bytes 9437188
  6.5 12.7 %copy-start.11 = (bf16[136,640]{1,0:T(8,128)(2,1)S(1)}, bf16[136,640]{1,0:T(8,128)(2,1)}, u32[]{:S(2)}) copy-start(bf16[136,640]{1,0:T(8,128)(2,1)} %param.18) | copy-start | bytes 522244
  6.5 12.7 %copy-start.24 = (s32[3]{0:T(128)S(1)}, s32[3]{0:T(128)}, u32[]{:S(2)}) copy-start(s32[3]{0:T(128)} %param.26) | copy-start | bytes 40
  6.5 13.3 %copy-start.2 = (s32[4]{0:T(128)S(1)}, s32[4]{0:T(128)}, u32[]{:S(2)}) copy-start(s32[4]{0:T(128)} %param.27) | copy-start | bytes 52
  6.5 17.9 %copy-start.22 = (s32[3]{0:T(128)S(1)}, s32[3]{0:T(128)}, u32[]{:S(2)}) copy-start(s32[3]{0:T(128)} %param.25) | copy-start | bytes 40
  6.5 57.4 %all-gather.14.cloned.1.call-start = ((), (), s32[]{:S(2)}) async-start(), calls=%async_computation.6 | async-start | bytes 2785280 | tf_op jit(solution)/shard_map/all_gather | solution.py:108
  10.3 28.6 %all-to-all-start = ((bf16[16,272,128]{2,1,0:T(8,128)(2,1)}), bf16[16,272,128]{2,1,0:T(8,128)(2,1)}, u32[]{:S(2)}, u32[]{:S(2)}) async-start(bf16[16,272,128]{2,1,0:T(8,128)(2,1)} %broadcast_in_dim.145), calls=%async_computation | async-start | bytes 2228224 | tf_op jit(solution)/shard_map/all_to_all | solution.py:111
  18.5 113.8 %all-gather.8.cloned.1.call-start = ((), (), s32[]{:S(2)}) async-start(), calls=%async_computation.3 | async-start | bytes 1566720 | tf_op jit(solution)/shard_map/all_gather | solution.py:196
  19.3 5.2 %copy-start.14 = (bf16[3,5,128]{2,1,0:T(8,128)(2,1)}, bf16[3,5,128]{2,1,0:T(8,128)(2,1)S(1)}, u32[]{:S(2)}) copy-start(bf16[3,5,128]{2,1,0:T(8,128)(2,1)S(1)} %reshape.382) | copy-start | bytes 11524
  26.0 2.3 copy-start.21
  28.3 13.4 %copy-start.7 = (bf16[133,5,128]{2,1,0:T(8,128)(2,1)S(1)}, bf16[133,5,128]{2,1,0:T(8,128)(2,1)}, u32[]{:S(2)}) copy-start(bf16[133,5,128]{2,1,0:T(8,128)(2,1)} %reshape.390) | copy-start | bytes 510724
  64.0 5.3 %slice-start = ((s8[5918720]{0:T(1024)(128)(4,1)}), s8[4194304]{0:T(1024)(128)(4,1)S(1)}, s32[]{:S(2)}) async-start(s8[5918720]{0:T(1024)(128)(4,1)} %bitcast.167), calls=%async_computation.7 | async-start | bytes 8388608
  66.1 2.5 copy-start.8
  66.1 2.5 copy-start.17
  66.1 3.2 slice-start.1
  72.7 1.6 copy-start.3
  74.1 2.0 copy-start.4
  74.1 2.9 copy-start.13
  74.1 2.9 copy-start.15
  74.1 3.3 copy-start.16
  74.1 3.2 copy-start.19
  74.3 5.0 %copy-start.18 = (f32[3,128]{1,0:T(4,128)S(1)}, f32[3,128]{1,0:T(4,128)}, u32[]{:S(2)}) copy-start(f32[3,128]{1,0:T(4,128)} %slice_convert_fusion) | copy-start | bytes 4612
  86.0 24.1 %copy-start.12 = (bf16[136,640]{1,0:T(8,128)(2,1)S(1)}, bf16[136,640]{1,0:T(8,128)(2,1)}, u32[]{:S(2)}) copy-start(bf16[136,640]{1,0:T(8,128)(2,1)} %param.17) | copy-start | bytes 522244
  86.0 24.9 %copy-start.20 = (f32[640]{0:T(1024)S(1)}, f32[640]{0:T(1024)}, u32[]{:S(2)}) copy-start(f32[640]{0:T(1024)} %param.30) | copy-start | bytes 7684
  110.8 109.4 %all-gather.10.cloned.1.call-start = ((), (), s32[]{:S(2)}) async-start(), calls=%async_computation.4 | async-start | bytes 11837440 | tf_op jit(solution)/shard_map/all_gather | solution.py:205
  136.7 93.1 %copy-start.5 = (bf16[5120,216]{0,1:T(8,128)(2,1)S(1)}, bf16[5120,216]{0,1:T(8,128)(2,1)}, u32[]{:S(2)}) copy-start(bf16[5120,216]{0,1:T(8,128)(2,1)} %param.31) | copy-start | bytes 6635524
  136.7 162.7 %all-gather.12.cloned.1.call-start = ((), (), s32[]{:S(2)}) async-start(), calls=%async_computation.5 | async-start | bytes 8460288 | tf_op jit(solution)/shard_map/all_gather | solution.py:229
  229.2 10.7 %collective-permute-start = (bf16[2176,1280]{1,0:T(8,128)(2,1)}, bf16[2176,1280]{1,0:T(8,128)(2,1)}, u32[]{:S(2)}, u32[]{:S(2)}) collective-permute-start(bf16[2176,1280]{1,0:T(8,128)(2,1)} %get-tuple-element.8), channel_id=1, source_target_pairs={{0,1},{1,0},{2,3},{3,2},{4,5},{5,4},{6,7},{7,6},{8,9},{9,8},{10,11... | collective-permute-start | bytes 16711688 | tf_op jit(solution)/shard_map/ppermute | solution.py:209
  229.3 17.4 %collective-permute-start.1 = (bf16[2176,1280]{1,0:T(8,128)(2,1)}, bf16[2176,1280]{1,0:T(8,128)(2,1)}, u32[]{:S(2)}, u32[]{:S(2)}) collective-permute-start(bf16[2176,1280]{1,0:T(8,128)(2,1)} %get-tuple-element.7), channel_id=1, source_target_pairs={{0,1},{1,0},{2,3},{3,2},{4,5},{5,4},{6,7},{7,6},{8,9},{9,8},{10,11... | collective-permute-start | bytes 16711688 | tf_op jit(solution)/shard_map/ppermute | solution.py:210
  229.8 1.6 copy-start.6
  252.1 47.3 %copy-start.23 = (bf16[1728,640]{1,0:T(8,128)(2,1)S(1)}, bf16[1728,640]{1,0:T(8,128)(2,1)}, u32[]{:S(2)}) copy-start(bf16[1728,640]{1,0:T(8,128)(2,1)} %param.33) | copy-start | bytes 6635524
  308.5 44.6 %copy-start.1 = (bf16[3,4096,128]{2,1,0:T(8,128)(2,1)S(1)}, bf16[3,4096,128]{2,1,0:T(8,128)(2,1)}, u32[]{:S(2)}) copy-start(bf16[3,4096,128]{2,1,0:T(8,128)(2,1)} %param.21) | copy-start | bytes 9437188
  (2 other events, 2.0 us)
Sparse Core Ops, SparseCore 0:
  9.5 54.4 all-gather.13
  110.9 21.3 all-gather.7
  136.8 83.3 all-gather.9
  253.9 45.5 all-gather.11
